TPU v7x, 32 devices: a whole 2x2x4 slice. The times are simulated.
32 devices in a mesh: ctx: 8 (over z, x), ch: 4 (over y, core).
Axes of the slice: x: 2, y: 2, z: 4, core: 2. Of those that a mesh axis runs over, the one named last changes fastest.
Arguments:
- arrivals: bfloat16 [3, 1024, 4096], P(None, 'ch', 'ctx'), may hold values from -12 to 12
- counts: int32 [8], P('ctx'), may hold values from 0 to 512, as said below
- short_taps: float32 [3, 3, 1024], P(None, None, 'ch'), may hold values from -3 to 3
- filter_taps: bfloat16 [1024, 2048], P('ch'), may hold values from -0.5 to 0.5
- skip_gain: float32 [1024], P('ch'), may hold values from 0.2 to 2
- out_weight: bfloat16 [8192, 1024], P('ch'), may hold values from -0.1875 to 0.1875
Outputs:
- mixed: bfloat16 [8192, 2048], P('ch', 'ctx')
Inputs may be any that keep to these rules, and one draw needn't show every extreme that they name: The counts sum to 2048. For every sampler i, offsets[i] differs from i * 256 by at most 128, and this bound is reached in both directions in every draw. counts[0] is 384.
All inputs are finite; a program needn't handle non-finite values.
Results may differ from a plain program's by a relative error of at most 0.0058.
Values may be sent and summed in bfloat16 or wider, within the bound.
No kernel may reach another device: no remote copies, remote signals or barrier semaphores. Data moves between devices by JAX's collectives and lax.ppermute only.
A program may use at most 64 MiB of HBM per device.

v0:
```python
import math

import jax
import jax.numpy as jnp
import ml_dtypes
import numpy as np
from jax import lax
from jax.sharding import PartitionSpec as P

T_DEV = 256
HALF = T_DEV // 2
PERIOD = 2 * T_DEV
GROUP = 8


def split_bf16(table):
    hi = table.astype(ml_dtypes.bfloat16)
    lo = (table - hi.astype(np.float64)).astype(ml_dtypes.bfloat16)
    return jnp.asarray(hi), jnp.asarray(lo)


def dft_tables():
    t = np.arange(T_DEV)[:, None]
    f = np.arange(T_DEV)[None, :]
    angle = 2.0 * np.pi * ((t * f) % PERIOD) / PERIOD
    forward = np.concatenate([np.cos(angle), -np.sin(angle)], axis=1)
    forward[:, T_DEV] = np.where(np.arange(T_DEV) % 2 == 0, 1.0, -1.0)
    fr = np.arange(T_DEV)[:, None]
    n = np.arange(T_DEV)[None, :]
    angle = 2.0 * np.pi * ((fr * n) % PERIOD) / PERIOD
    inv_re = 2.0 * np.cos(angle) / PERIOD
    inv_re[0, :] = 1.0 / PERIOD
    inv_im = -2.0 * np.sin(angle) / PERIOD
    inv_im[0, :] = np.where(np.arange(T_DEV) % 2 == 0, 1.0, -1.0) / PERIOD
    inverse = np.concatenate([inv_re, inv_im], axis=0).astype(np.float32)
    return split_bf16(forward), jnp.asarray(inverse)


def transform(blocks, forward):
    hi, lo = forward
    return jnp.einsum("kct,tf->kcf", blocks, hi, preferred_element_type=jnp.float32) + jnp.einsum(
        "kct,tf->kcf", blocks, lo, preferred_element_type=jnp.float32
    )


def kernel_spectra(tap_blocks, forward):
    spectra = transform(tap_blocks, forward)
    column = jnp.arange(PERIOD, dtype=jnp.int32) % T_DEV
    signs = jnp.where(column % 2 == 0, 1.0, -1.0).astype(jnp.float32)
    return spectra[1:] + signs * spectra[:-1]


def products(x_spec, g_spec):
    xr, xi = x_spec[..., :T_DEV], x_spec[..., T_DEV:]
    gr, gi = g_spec[..., :T_DEV], g_spec[..., T_DEV:]
    return (
        jnp.sum(xr * gr, axis=0),
        jnp.sum(xi * gi, axis=0),
        jnp.sum(xr * gi, axis=0),
        jnp.sum(xi * gr, axis=0),
    )


def on_device(arrivals, counts, short_taps, filter_taps, skip_gain, out_weight):
    n_ctx = lax.axis_size("ctx")
    device = lax.axis_index("ctx")
    channels = arrivals.shape[1]
    capacity = arrivals.shape[2]
    n_blocks = filter_taps.shape[1] // T_DEV
    forward, inverse = dft_tables()

    every_count = lax.all_gather(counts, "ctx", axis=0, tiled=True)
    earlier = jnp.arange(n_ctx, dtype=jnp.int32) < device
    offset = jnp.sum(jnp.where(earlier, every_count, 0))
    count = counts[0]

    frame = 2 * T_DEV
    row = jnp.arange(capacity, dtype=jnp.int32)[:, None]
    col = jnp.arange(frame, dtype=jnp.int32)[None, :]
    shift = offset - device * T_DEV + HALF
    select = ((row + shift == col) & (row < count)).astype(jnp.bfloat16)
    placed = jnp.einsum(
        "pcr,rj->pcj", arrivals, select, preferred_element_type=jnp.float32
    ).astype(jnp.bfloat16)
    to_prev = placed[:, :, :HALF]
    to_next = placed[:, :, frame - HALF - 2 :]
    from_next = lax.ppermute(to_prev, "ctx", [(i + 1, i) for i in range(n_ctx - 1)])
    from_prev = lax.ppermute(to_next, "ctx", [(i, i + 1) for i in range(n_ctx - 1)])
    window = placed[:, :, HALF - 2 : HALF + T_DEV]
    window = window + jnp.pad(from_prev, ((0, 0), (0, 0), (0, T_DEV - HALF)))
    window = window + jnp.pad(from_next, ((0, 0), (0, 0), (T_DEV + 2 - HALF, 0)))
    wide = window.astype(jnp.float32)
    shorted = short_taps[:, 0, :, None] * wide[:, :, 2:]
    shorted = shorted + short_taps[:, 1, :, None] * wide[:, :, 1:-1]
    shorted = shorted + short_taps[:, 2, :, None] * wide[:, :, :-2]
    mixed_input = (shorted[1] * shorted[2]).astype(jnp.bfloat16)

    tap_blocks = jnp.stack(
        [jnp.zeros((channels, T_DEV), filter_taps.dtype)]
        + [filter_taps[:, k * T_DEV : (k + 1) * T_DEV] for k in range(n_blocks)]
    )
    every_input = lax.all_gather(mixed_input, "ctx", axis=0)
    backwards = jnp.concatenate(
        [jnp.flip(every_input, 0), jnp.zeros_like(every_input)], axis=0
    )
    start = n_ctx - 1 - device
    if n_blocks <= GROUP:
        x_blocks = lax.dynamic_slice_in_dim(backwards, start, n_blocks, 0)
        sums = products(transform(x_blocks, forward), kernel_spectra(tap_blocks, forward))
    else:
        width = max(w for w in range(1, GROUP + 1) if n_blocks % w == 0)

        def group(g, acc):
            k0 = g * width
            x_blocks = lax.dynamic_slice_in_dim(backwards, start + k0, width, 0)
            taps = lax.dynamic_slice_in_dim(tap_blocks, k0, width + 1, 0)
            part = products(transform(x_blocks, forward), kernel_spectra(taps, forward))
            return tuple(a + b for a, b in zip(acc, part))

        zero = jnp.zeros((channels, T_DEV), jnp.float32)
        sums = lax.fori_loop(0, n_blocks // width, group, (zero, zero, zero, zero))
    rr, ii, ri, ir = sums
    first = jnp.arange(T_DEV, dtype=jnp.int32)[None, :] == 0
    spec_re = jnp.where(first, rr, rr - ii)
    spec_im = jnp.where(first, ii, ri + ir)
    spectrum = jnp.concatenate([spec_re, spec_im], axis=1)
    conv_core = jnp.dot(spectrum, inverse, precision=lax.Precision.HIGHEST)
    conv = conv_core + skip_gain[:, None] * mixed_input.astype(jnp.float32)
    gated = (shorted[0] * conv).astype(jnp.bfloat16)
    mixed = jnp.dot(
        out_weight,
        lax.all_gather(gated, "ch", axis=0, tiled=True),
        preferred_element_type=jnp.float32,
    )
    return mixed.astype(jnp.bfloat16)


def solution(mesh):
    return jax.shard_map(
        on_device,
        mesh=mesh,
        in_specs=(
            P(None, "ch", "ctx"),
            P("ctx"),
            P(None, None, "ch"),
            P("ch", None),
            P("ch"),
            P("ch", None),
        ),
        out_specs=P("ch", "ctx"),
        check_vma=False,
    )
```

profile of v0, /device:TPU:0, one launch (start us, length us, event | category | flops | bytes accessed | tf_op | source)
XLA Modules:
  0.0 100.2 jit_solution(9606081270032096954)
XLA Ops:
  6.5 0.0 copy-start
  6.5 0.0 copy-start.8
  6.5 0.0 copy-start.4
  6.5 0.0 all-gather.2.cloned.1.call-start
  7.3 1.3 %dynamic-slice = u32[1]{0:T(128)} dynamic-slice(u32[32]{0:T(128)} %constant.73, u32[]{:T(128)S(6)} %add.85), dynamic_slice_sizes={1} | dynamic-slice | bytes 12
  8.6 0.7 dynamic-update-slice
  9.3 13.1 %all-reduce.3 = s32[8]{0:T(128)S(1)} all-reduce(s32[8]{0:T(128)S(1)} %dynamic-update-slice), channel_id=1, replica_groups=mesh['ctx'=8,'ch'=4] {'ctx'}, use_global_device_ids=true, to_apply=%add.3 | all-reduce | flops 8 | bytes 64
  22.4 0.7 fusion.28
  23.7 0.0 copy-done
  23.7 0.6 fusion.2
  24.4 0.0 copy-start.5
  24.4 0.1 slice.107
  24.4 3.4 %collective-permute-start = (bf16[3,256,130]{1,2,0:T(8,128)(2,1)S(1)}, bf16[3,256,130]{1,2,0:T(8,128)(2,1)S(1)}, u32[]{:S(2)}, u32[]{:S(2)}) collective-permute-start(bf16[3,256,130]{1,2,0:T(8,128)(2,1)S(1)} %slice.107), channel_id=1, source_target_pairs={{0,4},{4,8},{8,12},{12,16},{16,20},{20,24},{24,28},{1,5},{5,9},{9,... | collective-permute-start | bytes 599048 | tf_op jit(solution)/shard_map/ppermute | solution.py:88
  27.9 0.7 slice.108
  28.5 0.0 copy-done.5
  28.6 1.3 %collective-permute-start.1 = (bf16[3,256,128]{1,2,0:T(8,128)(2,1)}, bf16[3,256,128]{1,2,0:T(8,128)(2,1)}, u32[]{:S(2)}, u32[]{:S(2)}) collective-permute-start(bf16[3,256,128]{1,2,0:T(8,128)(2,1)} %slice.108), channel_id=1, source_target_pairs={{4,0},{8,4},{12,8},{16,12},{20,16},{24,20},{28,24},{5,1},{9,5},{13... | collective-permute-start | bytes 589832 | tf_op jit(solution)/shard_map/ppermute | solution.py:87
  29.9 0.0 copy-done.8
  29.9 0.0 copy-done.4
  30.1 6.3 %collective-permute-done.1 = bf16[3,256,128]{1,2,0:T(8,128)(2,1)} collective-permute-done((bf16[3,256,128]{1,2,0:T(8,128)(2,1)}, bf16[3,256,128]{1,2,0:T(8,128)(2,1)}, u32[]{:S(2)}, u32[]{:S(2)}) %collective-permute-start.1) | collective-permute-done | bytes 196640 | tf_op jit(solution)/shard_map/ppermute | solution.py:87
  36.4 0.0 collective-permute-done
  36.4 1.2 %fusion.15 = f32[3,256,258]{1,2,0:T(8,128)S(1)} fusion(bf16[3,256,512]{1,2,0:T(8,128)(2,1)} %copy-done.5, bf16[3,256,128]{1,2,0:T(8,128)(2,1)} %collective-permute-done.1, bf16[3,256,130]{1,2,0:T(8,128)(2,1)S(1)} %collective-permute-done), kind=kLoop, calls=%fused_computation.30 | loop fusion | flops 1188864 | bytes 1585152 | tf_op jit(solution)/shard_map/convert_element_type | solution.py:92
  37.6 0.0 copy-start.3
  37.7 0.2 fusion.9
  37.9 0.8 copy.16
  38.7 0.0 all-gather.2.cloned.1.call-update
  38.7 0.9 bitcast_dynamic-update-slice_fusion.1
  39.7 0.9 bitcast_dynamic-update-slice_fusion
  40.6 0.0 copy-done.3
  40.6 0.0 copy-start.2
  40.6 0.8 fusion.34
  41.4 0.2 copy-done.2
  41.5 0.8 convolution_add_fusion
  42.3 2.5 %fusion = f32[8,256,512]{2,1,0:T(8,128)} fusion(f32[9,256,512]{2,1,0:T(8,128)S(1)} %convolution_add_fusion, f32[512]{0:T(512)S(1)} %fusion.27), kind=kLoop, calls=%fused_computation.1 | loop fusion | flops 2097152 | bytes 12584960 | tf_op jit(solution)/shard_map/add | solution.py:50
  44.9 32.3 %all-gather.2.cloned.1.call-done = bf16[8,256,256]{2,1,0:T(8,128)(2,1)} async-done(((bf16[1,256,256]{2,1,0:T(8,128)(2,1)}), bf16[8,256,256]{2,1,0:T(8,128)(2,1)}) %all-gather.2.cloned.1.call-update) | async-done | bytes 1048592 | tf_op jit(solution)/shard_map/all_gather | solution.py:102
  77.2 1.3 %rev.4 = bf16[8,256,256]{2,1,0:T(8,128)(2,1)S(1)} reverse(bf16[8,256,256]{2,1,0:T(8,128)(2,1)} %all-gather.2.cloned.1.call-done), dimensions={0} | reverse | bytes 2097152 | tf_op jit(solution)/shard_map/jit(_flip)/rev | solution.py:104
  78.5 0.7 fusion.11
  79.2 0.0 copy-start.1
  79.2 0.7 convolution_add_fusion.1
  79.9 1.5 %copy-done.1 = f32[8,256,512]{2,1,0:T(8,128)S(1)} copy-done((f32[8,256,512]{2,1,0:T(8,128)S(1)}, f32[8,256,512]{2,1,0:T(8,128)}, u32[]{:S(2)}) %copy-start.1) | copy-done | bytes 4194328
  81.4 0.0 copy-start.6
  81.4 0.0 copy-start.7
  81.4 0.0 copy-start.9
  81.4 0.0 copy-start.10
  81.4 0.6 multiply_reduce_fusion
  82.0 0.3 copy-done.6
  82.3 0.6 fusion.16
  82.9 0.0 copy-done.7
  82.9 0.0 copy-done.9
  82.9 0.6 fusion.5
  83.6 7.2 %all_gather.12 = bf16[1024,256]{0,1:T(8,128)(2,1)S(1)} all-gather(bf16[256,256]{0,1:T(8,128)(2,1)S(1)} %fusion.5), channel_id=1, replica_groups=mesh['ctx'=8,'ch'=4] {'ch'}, dimensions={0}, use_global_device_ids=true | all-gather | bytes 655360 | tf_op jit(solution)/shard_map/all_gather | solution.py:132
  90.7 0.0 copy-done.10
  90.7 1.3 %fusion.1 = bf16[2048,256]{0,1:T(8,128)(2,1)S(1)} fusion(bf16[1024,256]{0,1:T(8,128)(2,1)S(1)} %all_gather.12, bf16[2048,1024]{1,0:T(8,128)(2,1)S(1)} %copy-done.10), kind=kOutput, calls=%fused_computation.3 | convolution fusion | flops 1074266112 | bytes 5767168 | tf_op jit(solution)/shard_map/dot_general | solution.py:130
  92.1 1.3 %copy.19 = bf16[2048,256]{1,0:T(8,128)(2,1)} copy(bf16[2048,256]{0,1:T(8,128)(2,1)S(1)} %fusion.1) | data formatting | bytes 2097152 | tf_op jit(solution)/shard_map/convert_element_type | solution.py:135
  (16 shorter events, 0.2 us)
Async XLA Ops:
  6.5 17.2 %copy-start = (bf16[3,256,512]{2,1,0:T(8,128)(2,1)S(1)}, bf16[3,256,512]{2,1,0:T(8,128)(2,1)}, u32[]{:S(2)}) copy-start(bf16[3,256,512]{2,1,0:T(8,128)(2,1)} %param.9) | copy-start | bytes 2359300
  6.5 23.3 %copy-start.8 = (f32[3,3,256]{2,1,0:T(4,128)S(1)}, f32[3,3,256]{2,1,0:T(4,128)}, u32[]{:S(2)}) copy-start(f32[3,3,256]{2,1,0:T(4,128)} %param.11) | copy-start | bytes 27652
  6.5 23.4 %copy-start.4 = (bf16[256,2048]{1,0:T(8,128)(2,1)S(1)}, bf16[256,2048]{1,0:T(8,128)(2,1)}, u32[]{:S(2)}) copy-start(bf16[256,2048]{1,0:T(8,128)(2,1)} %param.12) | copy-start | bytes 3145732
  6.5 70.6 %all-gather.2.cloned.1.call-start = ((), (), s32[]{:S(2)}) async-start(), calls=%async_computation | async-start | bytes 1179648 | tf_op jit(solution)/shard_map/all_gather | solution.py:102
  24.4 4.2 %copy-start.5 = (bf16[3,256,512]{1,2,0:T(8,128)(2,1)}, bf16[3,256,512]{1,2,0:T(8,128)(2,1)S(1)}, u32[]{:S(2)}) copy-start(bf16[3,256,512]{1,2,0:T(8,128)(2,1)S(1)} %fusion.2) | copy-start | bytes 2359300
  24.4 12.0 %collective-permute-start = (bf16[3,256,130]{1,2,0:T(8,128)(2,1)S(1)}, bf16[3,256,130]{1,2,0:T(8,128)(2,1)S(1)}, u32[]{:S(2)}, u32[]{:S(2)}) collective-permute-start(bf16[3,256,130]{1,2,0:T(8,128)(2,1)S(1)} %slice.107), channel_id=1, source_target_pairs={{0,4},{4,8},{8,12},{12,16},{16,20},{20,24},{24,28},{1,5},{5,9},{9,... | collective-permute-start | bytes 599048 | tf_op jit(solution)/shard_map/ppermute | solution.py:88
  28.6 7.9 %collective-permute-start.1 = (bf16[3,256,128]{1,2,0:T(8,128)(2,1)}, bf16[3,256,128]{1,2,0:T(8,128)(2,1)}, u32[]{:S(2)}, u32[]{:S(2)}) collective-permute-start(bf16[3,256,128]{1,2,0:T(8,128)(2,1)} %slice.108), channel_id=1, source_target_pairs={{4,0},{8,4},{12,8},{16,12},{20,16},{24,20},{28,24},{5,1},{9,5},{13... | collective-permute-start | bytes 589832 | tf_op jit(solution)/shard_map/ppermute | solution.py:87
  37.6 2.9 %copy-start.3 = (bf16[256,512,1]{1,0,2:T(8,128)(2,1)S(1)}, bf16[256,512,1]{1,0,2:T(8,128)(2,1)}, u32[]{:S(2)}) copy-start(bf16[256,512,1]{1,0,2:T(8,128)(2,1)} %constant.77) | copy-start | bytes 786436
  40.6 1.0 copy-start.2
  79.2 2.2 %copy-start.1 = (f32[8,256,512]{2,1,0:T(8,128)S(1)}, f32[8,256,512]{2,1,0:T(8,128)}, u32[]{:S(2)}) copy-start(f32[8,256,512]{2,1,0:T(8,128)} %fusion) | copy-start | bytes 12582916
  81.4 0.9 copy-start.6
  81.4 1.6 %copy-start.7 = (f32[256,256]{1,0:T(8,128)S(1)}, f32[256,256]{1,0:T(8,128)}, u32[]{:S(2)}) copy-start(f32[256,256]{1,0:T(8,128)} %constant.70) | copy-start | bytes 786436
  81.4 1.6 %copy-start.9 = (f32[256]{0:T(256)S(1)}, f32[256]{0:T(256)}, u32[]{:S(2)}) copy-start(f32[256]{0:T(256)} %param.13) | copy-start | bytes 3076
  81.4 9.3 %copy-start.10 = (bf16[2048,1024]{1,0:T(8,128)(2,1)S(1)}, bf16[2048,1024]{1,0:T(8,128)(2,1)}, u32[]{:S(2)}) copy-start(bf16[2048,1024]{1,0:T(8,128)(2,1)} %param.14) | copy-start | bytes 12582916
Sparse Core Ops, SparseCore 0:
  38.8 38.2 all-gather.1
where the time goes:
time: 101 us; the launch traced here: 100 us
  waiting for transfers between devices  38.6 us (38%)
  blocking collectives  20.2 us (20%)
  between operations  15.1 us (15%)
  local copies, waits for them, and re-layouts  10.1 us (10%)
  matrix products  6.17 us (6%)
  other arithmetic  5.32 us (5%)
  starting transfers between devices  4.7 us (5%)
    all_gather x1, waiting for transfers between devices, on_device(): every_input = lax.all_gather(mixed_input, 'ctx', axis=0)  32.3 us
    unnamed x1, blocking collectives  13.1 us
    all_gather x1, blocking collectives, on_device(): lax.all_gather(gated, 'ch', axis=0, tiled=True)  7.15 us
    ppermute x1, waiting for transfers between devices, on_device(): lax.ppermute(to_prev, 'ctx', [(i + 1, i) for i in range(n_ctx - 1)])  6.33 us
    unnamed x35, local copies, waits for them, and re-layouts  5.04 us
    ppermute x1, starting transfers between devices, on_device(): lax.ppermute(to_next, 'ctx', [(i, i + 1) for i in range(n_ctx - 1)])  3.41 us
    add x1, other arithmetic, kernel_spectra(): return spectra[1:] + signs * spectra[:-1]  2.53 us
  transfers between devices with their start and end apart: 3, of which 2 were waited for; matrix products, arithmetic and copies ran while one was open for 7% of the time, Pallas kernels for 0%

commit v1 on v0

--- a/solution.py
+++ b/solution.py
@@ -11,6 +11,7 @@
 HALF = T_DEV // 2
 PERIOD = 2 * T_DEV
 GROUP = 8
+SENTINEL = 256.0
 
 
 def split_bf16(table):
@@ -36,10 +37,10 @@
     return split_bf16(forward), jnp.asarray(inverse)
 
 
-def transform(blocks, forward):
+def transform(blocks, forward, spec="kct,tf->kcf"):
     hi, lo = forward
-    return jnp.einsum("kct,tf->kcf", blocks, hi, preferred_element_type=jnp.float32) + jnp.einsum(
-        "kct,tf->kcf", blocks, lo, preferred_element_type=jnp.float32
+    return jnp.einsum(spec, blocks, hi, preferred_element_type=jnp.float32) + jnp.einsum(
+        spec, blocks, lo, preferred_element_type=jnp.float32
     )
 
 
@@ -61,7 +62,7 @@
     )
 
 
-def on_device(arrivals, counts, short_taps, filter_taps, skip_gain, out_weight):
+def by_gather(arrivals, counts, short_taps, filter_taps, skip_gain, out_weight):
     n_ctx = lax.axis_size("ctx")
     device = lax.axis_index("ctx")
     channels = arrivals.shape[1]
@@ -135,6 +136,90 @@
     return mixed.astype(jnp.bfloat16)
 
 
+def by_transpose(arrivals, counts, short_taps, filter_taps, skip_gain, out_weight):
+    n_ctx = lax.axis_size("ctx")
+    device = lax.axis_index("ctx")
+    channels = arrivals.shape[1]
+    capacity = arrivals.shape[2]
+    length = filter_taps.shape[1]
+    n_blocks = length // T_DEV
+    own = channels // n_ctx
+    forward, inverse = dft_tables()
+
+    live = jnp.arange(capacity, dtype=jnp.int32) < counts[0]
+    marked = jnp.where(live[None, None, :], arrivals, jnp.asarray(SENTINEL, arrivals.dtype))
+    marked = marked.reshape(3, n_ctx, own, capacity)
+    rows = lax.all_to_all(marked, "ctx", 1, 1, tiled=False)
+    every_count = jnp.sum((rows[0, :, 0, :] != SENTINEL).astype(jnp.int32), axis=1)
+    offsets = jnp.cumsum(every_count) - every_count
+
+    frame = 3 * T_DEV
+    row = jnp.arange(capacity, dtype=jnp.int32)[None, :, None]
+    col = jnp.arange(frame, dtype=jnp.int32)[None, None, :]
+    sampler = jnp.arange(n_ctx, dtype=jnp.int32)[:, None, None]
+    shift = offsets[:, None, None] - (sampler - 1) * T_DEV
+    select = ((row + shift == col) & (row < every_count[:, None, None])).astype(jnp.bfloat16)
+    placed = jnp.einsum("picr,irj->ipcj", rows, select, preferred_element_type=jnp.float32)
+    full = sum(
+        jnp.pad(placed[i], ((0, 0), (0, 0), (i * T_DEV, (n_ctx - 1 - i) * T_DEV)))
+        for i in range(n_ctx)
+    )
+    wide = full[:, :, T_DEV - 2 : T_DEV + length]
+    first = device * own
+    taps = lax.dynamic_slice_in_dim(short_taps, first, own, 2)
+    shorted = taps[:, 0, :, None] * wide[:, :, 2:]
+    shorted = shorted + taps[:, 1, :, None] * wide[:, :, 1:-1]
+    shorted = shorted + taps[:, 2, :, None] * wide[:, :, :-2]
+    mixed_input = (shorted[1] * shorted[2]).astype(jnp.bfloat16)
+
+    x_spec = transform(mixed_input.reshape(own, n_blocks, T_DEV), forward, "cnt,tf->cnf")
+    own_taps = lax.dynamic_slice_in_dim(filter_taps, first, own, 0)
+    tap_blocks = jnp.concatenate(
+        [jnp.zeros((own, T_DEV), own_taps.dtype), own_taps], axis=1
+    ).reshape(own, n_blocks + 1, T_DEV)
+    h_spec = transform(tap_blocks, forward, "cnt,tf->cnf")
+    column = jnp.arange(PERIOD, dtype=jnp.int32) % T_DEV
+    signs = jnp.where(column % 2 == 0, 1.0, -1.0).astype(jnp.float32)
+    g_spec = h_spec[:, 1:] + signs * h_spec[:, :-1]
+    xr, xi = x_spec[..., :T_DEV], x_spec[..., T_DEV:]
+    gr, gi = g_spec[..., :T_DEV], g_spec[..., T_DEV:]
+    sums = [jnp.zeros((own, n_blocks, T_DEV), jnp.float32) for _ in range(4)]
+    for k in range(n_blocks):
+        pad = ((0, 0), (k, 0), (0, 0))
+        terms = (
+            xr[:, : n_blocks - k] * gr[:, k : k + 1],
+            xi[:, : n_blocks - k] * gi[:, k : k + 1],
+            xr[:, : n_blocks - k] * gi[:, k : k + 1],
+            xi[:, : n_blocks - k] * gr[:, k : k + 1],
+        )
+        sums = [s + jnp.pad(t, pad) for s, t in zip(sums, terms)]
+    rr, ii, ri, ir = sums
+    at_zero = jnp.arange(T_DEV, dtype=jnp.int32)[None, None, :] == 0
+    spectrum = jnp.concatenate(
+        [jnp.where(at_zero, rr, rr - ii), jnp.where(at_zero, ii, ri + ir)], axis=2
+    )
+    conv_core = jnp.einsum("cnf,ft->cnt", spectrum, inverse, precision=lax.Precision.HIGHEST)
+    gains = lax.dynamic_slice_in_dim(skip_gain, first, own, 0)
+    conv = conv_core.reshape(own, length) + gains[:, None] * mixed_input.astype(jnp.float32)
+    gated = (shorted[0] * conv).astype(jnp.bfloat16)
+    back = lax.all_to_all(gated.reshape(own, n_ctx, T_DEV), "ctx", 1, 0, tiled=False)
+    gated_block = back.reshape(channels, T_DEV)
+    mixed = jnp.dot(
+        out_weight,
+        lax.all_gather(gated_block, "ch", axis=0, tiled=True),
+        preferred_element_type=jnp.float32,
+    )
+    return mixed.astype(jnp.bfloat16)
+
+
+def on_device(arrivals, counts, short_taps, filter_taps, skip_gain, out_weight):
+    n_ctx = lax.axis_size("ctx")
+    blocks = filter_taps.shape[1] // T_DEV
+    if arrivals.shape[1] % n_ctx == 0 and blocks == n_ctx:
+        return by_transpose(arrivals, counts, short_taps, filter_taps, skip_gain, out_weight)
+    return by_gather(arrivals, counts, short_taps, filter_taps, skip_gain, out_weight)
+
+
 def solution(mesh):
     return jax.shard_map(
         on_device,

time: 101 us -> 60.3 us (0.60)
  waiting for transfers between devices: 38.6 us -> 18.5 us
  between operations: 15.1 us -> 1.06 us
  local copies, waits for them, and re-layouts: 10.1 us -> 4.22 us
  starting transfers between devices: 4.7 us -> 7.25 us
  blocking collectives: 20.2 us -> 17.9 us
  other arithmetic: 5.32 us -> 3.44 us
  matrix products: 6.17 us -> 7.65 us
    all_gather x1 -> x0, waiting for transfers between devices: 32.3 us -> none  [on_device(): every_input = lax.all_gather(mixed_input, 'ctx', axis=0)]
    all_to_all x0 -> x1, waiting for transfers between devices: none -> 18.5 us  [by_transpose(): rows = lax.all_to_all(marked, 'ctx', 1, 1, tiled=False)]
    unnamed x1 -> x0, blocking collectives: 13.1 us -> none
    all_to_all x0 -> x1, blocking collectives: none -> 10.7 us  [by_transpose(): lax.all_to_all(gated.reshape(own, n_ctx, T_DEV), 'ctx', 1, 0, tiled=False)]
    all_to_all x0 -> x1, starting transfers between devices: none -> 7.25 us  [by_transpose(): rows = lax.all_to_all(marked, 'ctx', 1, 1, tiled=False)]
    ppermute x2 -> x0, waiting for transfers between devices: 6.33 us -> none  [the longest x1 6.33 us: on_device(): lax.ppermute(to_prev, 'ctx', [(i + 1, i) for i in range(n_ctx - 1)])]
    ppermute x2 -> x0, starting transfers between devices: 4.69 us -> none  [the longest x1 3.41 us: on_device(): lax.ppermute(to_next, 'ctx', [(i, i + 1) for i in range(n_ctx - 1)])]
    unnamed x35 -> x16, local copies, waits for them, and re-layouts: 5.04 us -> 0.7 us
  transfers between devices with their start and end apart: 3 -> 1, of which waited for: 2 -> 1; matrix products, arithmetic and copies ran while one was open for 7% -> 3% of each run, Pallas kernels for 0% -> 0%
where the time goes in v1:
time: 60.3 us; the launch traced here: 60 us
  waiting for transfers between devices  18.5 us (31%)
  blocking collectives  17.9 us (30%)
  matrix products  7.65 us (13%)
  starting transfers between devices  7.25 us (12%)
  local copies, waits for them, and re-layouts  4.22 us (7%)
  other arithmetic  3.44 us (6%)
  between operations  1.06 us (2%)
    all_to_all x1, waiting for transfers between devices, by_transpose(): rows = lax.all_to_all(marked, 'ctx', 1, 1, tiled=False)  18.5 us
    all_to_all x1, blocking collectives, by_transpose(): lax.all_to_all(gated.reshape(own, n_ctx, T_DEV), 'ctx', 1, 0, tiled=False)  10.7 us
    all_to_all x1, starting transfers between devices, by_transpose(): rows = lax.all_to_all(marked, 'ctx', 1, 1, tiled=False)  7.25 us
    all_gather x1, blocking collectives, by_transpose(): lax.all_gather(gated_block, 'ch', axis=0, tiled=True)  7.18 us
    dot_general x1, matrix products, by_transpose(): jnp.einsum('picr,irj->ipcj', rows, select, preferred_element_type=jnp.flo...  4.59 us
    convert_element_type x1, local copies, waits for them, and re-layouts, by_transpose(): return mixed.astype(jnp.bfloat16)  1.31 us
    dot_general x1, matrix products, by_transpose(): jnp.dot(out_weight, lax.all_gather(gated_block, 'ch', axis=0, tiled=True)...  1.31 us
    select_n x1, other arithmetic, by_transpose(): jnp.where(live[None, None, :], arrivals, jnp.asarray(SENTINEL, arrivals.d...  1.26 us
  transfers between devices with their start and end apart: 1, of which 1 were waited for; matrix products, arithmetic and copies ran while one was open for 3% of the time, Pallas kernels for 0%

profile of v1, /device:TPU:0, one launch (start us, length us, event | category | flops | bytes accessed | tf_op | source)
XLA Modules:
  0.0 60.0 jit_solution(2177436305627507959)
XLA Ops:
  0.0 0.0 copy-start
  0.0 0.0 copy-start.2
  0.0 0.0 copy-start.5
  0.8 0.0 copy-start.1
  0.8 1.3 %broadcast_select_fusion = bf16[3,256,512]{2,1,0:T(8,128)(2,1)S(1)} fusion(bf16[3,256,512]{2,1,0:T(8,128)(2,1)} %param.9, pred[512]{0:T(512)(128)(4,1)S(1)} %iota_compare_fusion.2), kind=kLoop, calls=%fused_computation.20 | loop fusion | flops 393216 | bytes 1573376 | tf_op jit(solution)/shard_map/jit(_where)/select_n | solution.py:150
  2.1 1.0 %copy.27 = bf16[3,8,32,512]{3,2,0,1:T(8,128)(2,1)} copy(bf16[3,8,32,512]{3,2,1,0:T(8,128)(2,1)S(1)} %bitcast.96) | data formatting | bytes 1572864 | tf_op jit(solution)/shard_map/reshape | solution.py:151
  3.0 7.3 %all-to-all-start = ((bf16[3,8,32,512]{3,2,0,1:T(8,128)(2,1)}), bf16[3,8,32,512]{3,2,0,1:T(8,128)(2,1)S(1)}, u32[]{:S(2)}, u32[]{:S(2)}) async-start(bf16[3,8,32,512]{3,2,0,1:T(8,128)(2,1)} %copy.27), calls=%async_computation | async-start | bytes 1572864 | tf_op jit(solution)/shard_map/all_to_all | solution.py:152
  10.3 0.0 copy-done
  10.3 0.9 %constant_dynamic-slice_fusion.1 = (f32[3,1,32]{2,1,0:T(1,128)S(1)}, f32[3,1,32]{2,1,0:T(1,128)S(1)}, f32[3,1,32]{2,1,0:T(1,128)S(1)}) fusion(f32[3,3,256]{2,1,0:T(4,128)} %param.11, s32[]{:T(128)S(6)} %select_n.43, s32[]{:T(128)S(6)} %add.300, s32[]{:T(128)S(6)} %add.301), kind=kLoop, calls=%fused_computation.109 | loop fusion | bytes 2316 | tf_op jit(solution)/shard_map/slice | solution.py:170
  11.2 0.0 copy-done.5
  11.2 0.1 dynamic_slice.11
  11.3 0.0 copy-done.2
  11.3 0.2 fusion.16
  11.6 0.0 copy-done.1
  11.6 0.2 convolution_add_fusion
  11.8 0.1 fusion.12
  11.9 18.5 %all-to-all-done = bf16[3,8,32,512]{3,2,0,1:T(8,128)(2,1)S(1)} async-done(((bf16[3,8,32,512]{3,2,0,1:T(8,128)(2,1)}), bf16[3,8,32,512]{3,2,0,1:T(8,128)(2,1)S(1)}, u32[]{:S(2)}, u32[]{:S(2)}) %all-to-all-start) | async-done | bytes 786464 | tf_op jit(solution)/shard_map/all_to_all | solution.py:152
  30.5 0.2 fusion.23
  30.7 0.1 iota_compare_fusion.1
  30.8 0.2 reduce-window.8
  31.0 0.1 iota_add_fusion
  31.0 4.6 %fusion.2 = f32[8,3,32,768]{3,2,1,0:T(8,128)S(1)} fusion(bf16[3,8,32,512]{3,2,0,1:T(8,128)(2,1)S(1)} %all-to-all-done, s32[8,512]{1,0:T(8,128)S(1)} %iota_add_fusion, pred[8,512]{1,0:T(8,128)(4,1)S(1)} %iota_compare_fusion.1), kind=kOutput, calls=%fused_computation.3 | convolution fusion | flops 610271232 | bytes 3166208 | tf_op jit(solution)/shard_map/picr,irj->ipcj/dot_general | solution.py:162
  35.6 0.2 slice_bitcast_fusion.7
  35.9 0.1 pad_add_fusion
  36.0 0.5 fusion.10
  36.6 0.1 copy.43
  36.7 0.2 fusion.21
  36.9 0.2 convolution_add_fusion.1
  37.3 0.1 slice_multiply_fusion.15
  37.4 0.1 slice_multiply_fusion.11
  37.5 0.1 slice_multiply_fusion.7
  37.6 0.0 copy-start.3
  37.6 0.2 subtract_select_fusion
  37.8 0.0 copy-start.4
  37.8 0.2 add_select_fusion
  38.0 0.1 pad_maximum_fusion
  38.1 0.6 copy-done.3
  38.6 0.9 %fusion.9 = bf16[1,32,8,256]{3,2,1,0:T(8,128)(2,1)S(1)} fusion(f32[32,8,256]{2,1,0:T(8,128)S(1)} %bitcast.102, f32[512,256,1]{1,0,2:T(8,128)S(1)} %copy-done.3, f32[32,8,512]{2,0,1:T(8,128)S(1)} %pad_maximum_fusion, bf16[32,8,256]{2,1,0:T(8,128)(2,1)S(1)} %bitcast.99, f32[32]{0:T(128)S(1)} %dynamic_slice.11), kind=kOutput, calls=%fused_computation.13 | convolution fusion | flops 402980864 | bytes 1572992 | tf_op jit(solution)/shard_map/cnf,ft->cnt/dot_general | solution.py:201
  39.5 10.7 %all_to_all.20 = bf16[1,32,8,256]{3,1,0,2:T(8,128)(2,1)S(1)} all-to-all(bf16[1,32,8,256]{3,1,0,2:T(8,128)(2,1)S(1)} %copy.33), channel_id=1, replica_groups=mesh['ctx'=8,'ch'=4] {'ctx'}, dimensions={2} | all-to-all | bytes 262144 | tf_op jit(solution)/shard_map/all_to_all | solution.py:205
  50.2 7.2 %all_gather.3 = bf16[1024,256]{1,0:T(8,128)(2,1)S(1)} all-gather(bf16[256,256]{1,0:T(8,128)(2,1)S(1)} %bitcast.105), channel_id=1, replica_groups=mesh['ctx'=8,'ch'=4] {'ch'}, dimensions={0}, use_global_device_ids=true | all-gather | bytes 655360 | tf_op jit(solution)/shard_map/all_gather | solution.py:209
  57.4 0.0 copy-done.4
  57.4 1.3 %fusion.6 = bf16[2048,256]{0,1:T(8,128)(2,1)S(1)} fusion(bf16[1024,256]{1,0:T(8,128)(2,1)S(1)} %all_gather.3, bf16[2048,1024]{1,0:T(8,128)(2,1)S(1)} %copy-done.4), kind=kOutput, calls=%fused_computation.7 | convolution fusion | flops 1074266112 | bytes 5767168 | tf_op jit(solution)/shard_map/dot_general | solution.py:207
  58.7 1.3 %copy.34 = bf16[2048,256]{1,0:T(8,128)(2,1)} copy(bf16[2048,256]{0,1:T(8,128)(2,1)S(1)} %fusion.6) | data formatting | bytes 2097152 | tf_op jit(solution)/shard_map/convert_element_type | solution.py:212
  (16 shorter events, 0.3 us)
Async XLA Ops:
  0.0 10.3 %copy-start = (bf16[256,2048]{1,0:T(8,128)(2,1)S(1)}, bf16[256,2048]{1,0:T(8,128)(2,1)}, u32[]{:S(2)}) copy-start(bf16[256,2048]{1,0:T(8,128)(2,1)} %param.12) | copy-start | bytes 3145732
  0.0 11.3 %copy-start.2 = (bf16[256,512,1]{1,0,2:T(8,128)(2,1)S(1)}, bf16[256,512,1]{1,0,2:T(8,128)(2,1)}, u32[]{:S(2)}) copy-start(bf16[256,512,1]{1,0,2:T(8,128)(2,1)} %constant.140) | copy-start | bytes 786436
  0.0 11.2 %copy-start.5 = (f32[256]{0:T(256)S(1)}, f32[256]{0:T(256)}, u32[]{:S(2)}) copy-start(f32[256]{0:T(256)} %param.13) | copy-start | bytes 3076
  0.8 10.8 %copy-start.1 = (bf16[256,512,1]{1,0,2:T(8,128)(2,1)S(1)}, bf16[256,512,1]{1,0,2:T(8,128)(2,1)}, u32[]{:S(2)}) copy-start(bf16[256,512,1]{1,0,2:T(8,128)(2,1)} %constant.141) | copy-start | bytes 786436
  3.0 27.4 %all-to-all-start = ((bf16[3,8,32,512]{3,2,0,1:T(8,128)(2,1)}), bf16[3,8,32,512]{3,2,0,1:T(8,128)(2,1)S(1)}, u32[]{:S(2)}, u32[]{:S(2)}) async-start(bf16[3,8,32,512]{3,2,0,1:T(8,128)(2,1)} %copy.27), calls=%async_computation | async-start | bytes 1572864 | tf_op jit(solution)/shard_map/all_to_all | solution.py:152
  37.6 1.0 %copy-start.3 = (f32[512,256,1]{1,0,2:T(8,128)S(1)}, f32[512,256,1]{1,0,2:T(8,128)}, u32[]{:S(2)}) copy-start(f32[512,256,1]{1,0,2:T(8,128)} %constant.142) | copy-start | bytes 1572868
  37.8 19.6 %copy-start.4 = (bf16[2048,1024]{1,0:T(8,128)(2,1)S(1)}, bf16[2048,1024]{1,0:T(8,128)(2,1)}, u32[]{:S(2)}) copy-start(bf16[2048,1024]{1,0:T(8,128)(2,1)} %param.14) | copy-start | bytes 12582916

commit v2 on v1

--- a/solution.py
+++ b/solution.py
@@ -147,24 +147,17 @@
     forward, inverse = dft_tables()
 
     live = jnp.arange(capacity, dtype=jnp.int32) < counts[0]
-    marked = jnp.where(live[None, None, :], arrivals, jnp.asarray(SENTINEL, arrivals.dtype))
-    marked = marked.reshape(3, n_ctx, own, capacity)
-    rows = lax.all_to_all(marked, "ctx", 1, 1, tiled=False)
+    by_owner = jnp.transpose(arrivals.reshape(3, n_ctx, own, capacity), (1, 0, 2, 3))
+    marked = jnp.where(live, by_owner, jnp.asarray(SENTINEL, arrivals.dtype))
+    rows = jnp.transpose(lax.all_to_all(marked, "ctx", 0, 0, tiled=False), (1, 0, 2, 3))
     every_count = jnp.sum((rows[0, :, 0, :] != SENTINEL).astype(jnp.int32), axis=1)
     offsets = jnp.cumsum(every_count) - every_count
 
-    frame = 3 * T_DEV
-    row = jnp.arange(capacity, dtype=jnp.int32)[None, :, None]
-    col = jnp.arange(frame, dtype=jnp.int32)[None, None, :]
-    sampler = jnp.arange(n_ctx, dtype=jnp.int32)[:, None, None]
-    shift = offsets[:, None, None] - (sampler - 1) * T_DEV
-    select = ((row + shift == col) & (row < every_count[:, None, None])).astype(jnp.bfloat16)
-    placed = jnp.einsum("picr,irj->ipcj", rows, select, preferred_element_type=jnp.float32)
-    full = sum(
-        jnp.pad(placed[i], ((0, 0), (0, 0), (i * T_DEV, (n_ctx - 1 - i) * T_DEV)))
-        for i in range(n_ctx)
-    )
-    wide = full[:, :, T_DEV - 2 : T_DEV + length]
+    full = jnp.zeros((3, own, length + capacity), arrivals.dtype)
+    for i in range(n_ctx):
+        full = lax.dynamic_update_slice(full, rows[:, i], (0, 0, offsets[i]))
+    full = jnp.pad(full[:, :, :length], ((0, 0), (0, 0), (2, 0))).astype(jnp.float32)
+    wide = full
     first = device * own
     taps = lax.dynamic_slice_in_dim(short_taps, first, own, 2)
     shorted = taps[:, 0, :, None] * wide[:, :, 2:]

time: 60.3 us -> 76 us (1.26)
  between operations: 1.06 us -> 16 us
  local copies, waits for them, and re-layouts: 4.22 us -> 10.4 us
  matrix products: 7.65 us -> 4.01 us
  waiting for transfers between devices: 18.5 us -> 15.7 us
    dynamic_update_slice x0 -> x8, local copies, waits for them, and re-layouts: none -> 4.76 us  [by_transpose(): full = lax.dynamic_update_slice(full, rows[:, i], (0, 0, offsets[i]))]
    dot_general x1 -> x0, matrix products: 4.59 us -> none  [by_transpose(): jnp.einsum('picr,irj->ipcj', rows, select, preferred_element_type=jnp.flo...]
    all_to_all x1, waiting for transfers between devices: 18.5 us -> 15.7 us  [by_transpose(): lax.all_to_all(marked, 'ctx', 0, 0, tiled=False)]
    dynamic_slice x1, local copies, waits for them, and re-layouts: 0.08 us -> 1.34 us  [by_transpose(): gains = lax.dynamic_slice_in_dim(skip_gain, first, own, 0)]
    reshape x1 -> x0, local copies, waits for them, and re-layouts: 0.96 us -> none  [by_transpose(): marked = marked.reshape(3, n_ctx, own, capacity)]
    dot_general x2, matrix products: 0.45 us -> 1.4 us  [transform(): jnp.einsum(spec, blocks, hi, preferred_element_type=jnp.float32)]
    select_n x1, other arithmetic: 1.26 us -> 2.09 us  [by_transpose(): marked = jnp.where(live, by_owner, jnp.asarray(SENTINEL, arrivals.dtype))]
  transfers between devices with their start and end apart: 1 -> 1, of which waited for: 1 -> 1; matrix products, arithmetic and copies ran while one was open for 3% -> 6% of each run, Pallas kernels for 0% -> 0%
where the time goes in v2:
time: 76 us; the launch traced here: 75.5 us
  blocking collectives  17.9 us (24%)
  between operations  16 us (21%)
  waiting for transfers between devices  15.7 us (21%)
  local copies, waits for them, and re-layouts  10.4 us (14%)
  starting transfers between devices  7.25 us (10%)
  other arithmetic  4.17 us (5%)
  matrix products  4.01 us (5%)
    all_to_all x1, waiting for transfers between devices, by_transpose(): lax.all_to_all(marked, 'ctx', 0, 0, tiled=False)  15.7 us
    all_to_all x1, blocking collectives, by_transpose(): lax.all_to_all(gated.reshape(own, n_ctx, T_DEV), 'ctx', 1, 0, tiled=False)  10.7 us
    all_to_all x1, starting transfers between devices, by_transpose(): lax.all_to_all(marked, 'ctx', 0, 0, tiled=False)  7.25 us
    all_gather x1, blocking collectives, by_transpose(): lax.all_gather(gated_block, 'ch', axis=0, tiled=True)  7.18 us
    dynamic_update_slice x8, local copies, waits for them, and re-layouts, by_transpose(): full = lax.dynamic_update_slice(full, rows[:, i], (0, 0, offsets[i]))  4.76 us
    select_n x1, other arithmetic, by_transpose(): marked = jnp.where(live, by_owner, jnp.asarray(SENTINEL, arrivals.dtype))  2.09 us
  transfers between devices with their start and end apart: 1, of which 1 were waited for; matrix products, arithmetic and copies ran while one was open for 6% of the time, Pallas kernels for 0%

profile of v2, /device:TPU:0, one launch (start us, length us, event | category | flops | bytes accessed | tf_op | source)
XLA Modules:
  0.0 75.5 jit_solution(16267654687887007281)
XLA Ops:
  0.0 0.0 copy-start
  0.0 0.0 copy-start.1
  0.8 2.1 %fusion.6 = bf16[8,3,32,512]{3,2,1,0:T(8,128)(2,1)} fusion(bf16[3,8,32,512]{3,2,1,0:T(8,128)(2,1)} %bitcast.108, pred[512]{0:T(512)(128)(4,1)S(1)} %iota_compare_fusion), kind=kLoop, calls=%fused_computation.14 | loop fusion | flops 393216 | bytes 1573376 | tf_op jit(solution)/shard_map/jit(_where)/select_n | solution.py:151
  2.9 7.3 %all-to-all-start = ((bf16[8,3,32,512]{3,2,1,0:T(8,128)(2,1)}), bf16[8,3,32,512]{3,2,1,0:T(8,128)(2,1)S(1)}, u32[]{:S(2)}, u32[]{:S(2)}) async-start(bf16[8,3,32,512]{3,2,1,0:T(8,128)(2,1)} %fusion.6), calls=%async_computation | async-start | bytes 1572864 | tf_op jit(solution)/shard_map/all_to_all | solution.py:152
  10.1 0.0 copy-done
  10.1 0.9 %constant_dynamic-slice_fusion.1 = (f32[3,1,32]{2,1,0:T(1,128)S(1)}, f32[3,1,32]{2,1,0:T(1,128)S(1)}, f32[3,1,32]{2,1,0:T(1,128)S(1)}) fusion(f32[3,3,256]{2,1,0:T(4,128)} %param.11, s32[]{:T(128)S(6)} %select_n.70, s32[]{:T(128)S(6)} %add.260, s32[]{:T(128)S(6)} %add.261), kind=kLoop, calls=%fused_computation.102 | loop fusion | bytes 2316 | tf_op jit(solution)/shard_map/slice | solution.py:163
  11.0 1.3 %dynamic_slice.11 = f32[32]{0:T(128)} dynamic-slice(f32[256]{0:T(256)} %param.13, s32[]{:T(128)S(6)} %select_n.70), dynamic_slice_sizes={32} | dynamic-slice | bytes 260 | tf_op jit(solution)/shard_map/dynamic_slice | solution.py:195
  12.4 1.2 %fusion.11 = f32[32,9,512]{2,0,1:T(8,128)S(1)} fusion(bf16[256,512,1]{1,0,2:T(8,128)(2,1)} %constant.126, bf16[4,9,8,256]{3,2,1,0:T(8,128)(2,1)S(1)} %bitcast.104), kind=kOutput, calls=%fused_computation.38 | convolution fusion | flops 75497472 | bytes 999424 | tf_op jit(solution)/shard_map/cnt,tf->cnf/dot_general | solution.py:42
  13.6 0.0 copy-done.1
  13.6 0.2 convolution_add_fusion
  13.9 0.1 fusion.7
  13.9 0.6 slice_bitcast_fusion.21
  14.5 15.7 %all-to-all-done = bf16[8,3,32,512]{3,2,1,0:T(8,128)(2,1)S(1)} async-done(((bf16[8,3,32,512]{3,2,1,0:T(8,128)(2,1)}), bf16[8,3,32,512]{3,2,1,0:T(8,128)(2,1)S(1)}, u32[]{:S(2)}, u32[]{:S(2)}) %all-to-all-start) | async-done | bytes 786464 | tf_op jit(solution)/shard_map/all_to_all | solution.py:152
  30.3 0.2 fusion.18
  30.5 0.1 slice_bitcast_fusion
  30.6 0.2 reduce-window.9
  30.8 0.7 fusion.25
  46.4 0.5 dynamic_update_slice.24
  47.0 0.5 dynamic_update_slice.25
  47.5 0.0 copy-start.2
  47.6 0.5 dynamic_update_slice.26
  48.1 1.1 %dynamic_update_slice.27 = bf16[3,32,2560]{2,1,0:T(8,128)(2,1)S(1)} dynamic-update-slice(bf16[3,32,2560]{2,1,0:T(8,128)(2,1)S(1)} %dynamic_update_slice.26, bf16[3,32,512]{2,1,0:T(8,128)(2,1)S(1)} %get-tuple-element.17, s32[]{:T(128)} %constant.48.clone.1, s32[]{:T(128)} %constant.48.clone.1, s32[]{:T(128)S(6)} %select_n.76) | dynamic-update-slice | bytes 196612 | tf_op jit(solution)/shard_map/dynamic_update_slice | solution.py:158
  49.2 0.5 dynamic_update_slice.28
  49.7 0.5 dynamic_update_slice.29
  50.3 0.5 dynamic_update_slice.30
  50.8 0.5 dynamic_update_slice.31
  51.3 0.2 pad_convert_fusion
  51.5 0.5 fusion.4
  52.0 0.0 copy-start.4
  52.1 0.1 copy.43
  52.2 0.0 copy-done.2
  52.2 0.2 fusion.16
  52.4 0.2 convolution_add_fusion.1
  52.8 0.1 slice_multiply_fusion.15
  52.9 0.0 copy-done.4
  52.9 0.1 slice_multiply_fusion.11
  53.0 0.0 copy-start.3
  53.0 0.0 copy-start.5
  53.0 0.1 slice_multiply_fusion.7
  53.1 0.0 copy-start.6
  53.2 0.2 subtract_select_fusion
  53.3 0.2 add_select_fusion
  53.6 0.1 pad_maximum_fusion
  53.6 0.4 copy-done.3
  54.1 0.0 copy-done.5
  54.1 0.9 %fusion.3 = bf16[1,32,8,256]{3,2,1,0:T(8,128)(2,1)S(1)} fusion(f32[32,8,256]{2,1,0:T(8,128)S(1)} %bitcast.106, f32[512,256,1]{1,0,2:T(8,128)S(1)} %copy-done.3, f32[32,8,512]{2,0,1:T(8,128)S(1)} %pad_maximum_fusion, bf16[32,8,256]{2,1,0:T(8,128)(2,1)S(1)} %bitcast.103, f32[32]{0:T(128)S(1)} %copy-done.5), kind=kOutput, calls=%fused_computation.7 | convolution fusion | flops 402980864 | bytes 1572992 | tf_op jit(solution)/shard_map/cnf,ft->cnt/dot_general | solution.py:194
  55.0 10.7 %all_to_all.20 = bf16[1,32,8,256]{3,1,0,2:T(8,128)(2,1)S(1)} all-to-all(bf16[1,32,8,256]{3,1,0,2:T(8,128)(2,1)S(1)} %copy.34), channel_id=1, replica_groups=mesh['ctx'=8,'ch'=4] {'ctx'}, dimensions={2} | all-to-all | bytes 262144 | tf_op jit(solution)/shard_map/all_to_all | solution.py:198
  65.7 7.2 %all_gather.3 = bf16[1024,256]{1,0:T(8,128)(2,1)S(1)} all-gather(bf16[256,256]{1,0:T(8,128)(2,1)S(1)} %bitcast.110), channel_id=1, replica_groups=mesh['ctx'=8,'ch'=4] {'ch'}, dimensions={0}, use_global_device_ids=true | all-gather | bytes 655360 | tf_op jit(solution)/shard_map/all_gather | solution.py:202
  72.8 0.0 copy-done.6
  72.8 1.3 %fusion = bf16[2048,256]{0,1:T(8,128)(2,1)S(1)} fusion(bf16[1024,256]{1,0:T(8,128)(2,1)S(1)} %all_gather.3, bf16[2048,1024]{1,0:T(8,128)(2,1)S(1)} %copy-done.6), kind=kOutput, calls=%fused_computation.1 | convolution fusion | flops 1074266112 | bytes 5767168 | tf_op jit(solution)/shard_map/dot_general | solution.py:200
  74.2 1.3 %copy.35 = bf16[2048,256]{1,0:T(8,128)(2,1)} copy(bf16[2048,256]{0,1:T(8,128)(2,1)S(1)} %fusion) | data formatting | bytes 2097152 | tf_op jit(solution)/shard_map/convert_element_type | solution.py:205
  (17 shorter events, 0.4 us)
Async XLA Ops:
  0.0 10.1 %copy-start = (bf16[256,2048]{1,0:T(8,128)(2,1)S(1)}, bf16[256,2048]{1,0:T(8,128)(2,1)}, u32[]{:S(2)}) copy-start(bf16[256,2048]{1,0:T(8,128)(2,1)} %param.12) | copy-start | bytes 3145732
  0.0 13.6 %copy-start.1 = (bf16[256,512,1]{1,0,2:T(8,128)(2,1)S(1)}, bf16[256,512,1]{1,0,2:T(8,128)(2,1)}, u32[]{:S(2)}) copy-start(bf16[256,512,1]{1,0,2:T(8,128)(2,1)} %constant.127) | copy-start | bytes 786436
  2.9 27.4 %all-to-all-start = ((bf16[8,3,32,512]{3,2,1,0:T(8,128)(2,1)}), bf16[8,3,32,512]{3,2,1,0:T(8,128)(2,1)S(1)}, u32[]{:S(2)}, u32[]{:S(2)}) async-start(bf16[8,3,32,512]{3,2,1,0:T(8,128)(2,1)} %fusion.6), calls=%async_computation | async-start | bytes 1572864 | tf_op jit(solution)/shard_map/all_to_all | solution.py:152
  47.5 4.7 %copy-start.2 = (bf16[256,512,1]{1,0,2:T(8,128)(2,1)S(1)}, bf16[256,512,1]{1,0,2:T(8,128)(2,1)}, u32[]{:S(2)}) copy-start(bf16[256,512,1]{1,0,2:T(8,128)(2,1)} %constant.126) | copy-start | bytes 786436
  52.0 0.9 %copy-start.4 = (f32[32,256]{1,0:T(8,128)S(1)}, f32[32,256]{1,0:T(8,128)}, u32[]{:S(2)}) copy-start(f32[32,256]{1,0:T(8,128)} %get-tuple-element.69) | copy-start | bytes 98308
  53.0 1.0 %copy-start.3 = (f32[512,256,1]{1,0,2:T(8,128)S(1)}, f32[512,256,1]{1,0,2:T(8,128)}, u32[]{:S(2)}) copy-start(f32[512,256,1]{1,0,2:T(8,128)} %constant.128) | copy-start | bytes 1572868
  53.0 1.0 %copy-start.5 = (f32[32]{0:T(128)S(1)}, f32[32]{0:T(128)}, u32[]{:S(2)}) copy-start(f32[32]{0:T(128)} %dynamic_slice.11) | copy-start | bytes 388
  53.1 19.7 %copy-start.6 = (bf16[2048,1024]{1,0:T(8,128)(2,1)S(1)}, bf16[2048,1024]{1,0:T(8,128)(2,1)}, u32[]{:S(2)}) copy-start(bf16[2048,1024]{1,0:T(8,128)(2,1)} %param.14) | copy-start | bytes 12582916

commit v3 on v2

--- a/solution.py
+++ b/solution.py
@@ -148,16 +148,30 @@
 
     live = jnp.arange(capacity, dtype=jnp.int32) < counts[0]
     by_owner = jnp.transpose(arrivals.reshape(3, n_ctx, own, capacity), (1, 0, 2, 3))
-    marked = jnp.where(live, by_owner, jnp.asarray(SENTINEL, arrivals.dtype))
-    rows = jnp.transpose(lax.all_to_all(marked, "ctx", 0, 0, tiled=False), (1, 0, 2, 3))
-    every_count = jnp.sum((rows[0, :, 0, :] != SENTINEL).astype(jnp.int32), axis=1)
+    marker = jnp.where(live, by_owner[:, 0, 0, :], jnp.asarray(SENTINEL, arrivals.dtype))
+    marked = by_owner.at[:, 0, 0, :].set(marker)
+    rows = lax.all_to_all(marked, "ctx", 0, 0, tiled=False)
+    every_count = jnp.sum((rows[:, 0, 0, :] != SENTINEL).astype(jnp.int32), axis=1)
     offsets = jnp.cumsum(every_count) - every_count
 
-    full = jnp.zeros((3, own, length + capacity), arrivals.dtype)
-    for i in range(n_ctx):
-        full = lax.dynamic_update_slice(full, rows[:, i], (0, 0, offsets[i]))
-    full = jnp.pad(full[:, :, :length], ((0, 0), (0, 0), (2, 0))).astype(jnp.float32)
-    wide = full
+    local = jnp.arange(T_DEV, dtype=jnp.int32)[None, :, None]
+    col = jnp.arange(PERIOD, dtype=jnp.int32)[None, None, :]
+    sampler = jnp.arange(n_ctx, dtype=jnp.int32)[:, None, None]
+    shift = offsets[:, None, None] - (sampler - 1) * T_DEV - HALF
+    total = (n_ctx + 3) * T_DEV
+    full = 0.0
+    for q in range(capacity // T_DEV):
+        select = (local + shift == col) & (local + q * T_DEV < every_count[:, None, None])
+        placed = jnp.einsum(
+            "ipcr,irj->ipcj",
+            rows[..., q * T_DEV : (q + 1) * T_DEV],
+            select.astype(jnp.bfloat16),
+            preferred_element_type=jnp.float32,
+        )
+        for i in range(n_ctx):
+            left = i * T_DEV + q * T_DEV + HALF
+            full = full + jnp.pad(placed[i], ((0, 0), (0, 0), (left, total - left - PERIOD)))
+    wide = full[:, :, T_DEV - 2 : T_DEV + length]
     first = device * own
     taps = lax.dynamic_slice_in_dim(short_taps, first, own, 2)
     shorted = taps[:, 0, :, None] * wide[:, :, 2:]

time: 76 us -> 64.3 us (0.85)
  between operations: 16 us -> 0.98 us
  matrix products: 4.01 us -> 8.18 us
  waiting for transfers between devices: 15.7 us -> 18.5 us
  local copies, waits for them, and re-layouts: 10.4 us -> 7.9 us
  other arithmetic: 4.17 us -> 3.09 us
    dot_general x0 -> x2, matrix products: none -> 5.13 us  [by_transpose(): jnp.einsum('ipcr,irj->ipcj', rows[..., q * T_DEV:(q + 1) * T_DEV], select...]
    dynamic_update_slice x8 -> x0, local copies, waits for them, and re-layouts: 4.76 us -> none  [by_transpose(): full = lax.dynamic_update_slice(full, rows[:, i], (0, 0, offsets[i]))]
    all_to_all x1, waiting for transfers between devices: 15.7 us -> 18.5 us  [by_transpose(): rows = lax.all_to_all(marked, 'ctx', 0, 0, tiled=False)]
    reshape x0 -> x1, local copies, waits for them, and re-layouts: none -> 2.18 us  [by_transpose(): arrivals.reshape(3, n_ctx, own, capacity)]
    scatter x0 -> x1, local copies, waits for them, and re-layouts: none -> 1.53 us  [by_transpose(): marked = by_owner.at[:, 0, 0, :].set(marker)]
    dynamic_slice x1, local copies, waits for them, and re-layouts: 1.34 us -> 0.08 us  [by_transpose(): gains = lax.dynamic_slice_in_dim(skip_gain, first, own, 0)]
    select_n x1, other arithmetic: 2.09 us -> 0.86 us  [by_transpose(): jnp.where(live, by_owner[:, 0, 0, :], jnp.asarray(SENTINEL, arrivals.dtype))]
    dot_general x2, matrix products: 1.4 us -> 0.45 us  [transform(): jnp.einsum(spec, blocks, hi, preferred_element_type=jnp.float32)]
  transfers between devices with their start and end apart: 1 -> 1, of which waited for: 1 -> 1; matrix products, arithmetic and copies ran while one was open for 6% -> 2% of each run, Pallas kernels for 0% -> 0%
where the time goes in v3:
time: 64.3 us; the launch traced here: 63.9 us
  waiting for transfers between devices  18.5 us (29%)
  blocking collectives  17.9 us (28%)
  matrix products  8.18 us (13%)
  local copies, waits for them, and re-layouts  7.9 us (12%)
  starting transfers between devices  7.38 us (11%)
  other arithmetic  3.09 us (5%)
  between operations  0.98 us (2%)
    all_to_all x1, waiting for transfers between devices, by_transpose(): rows = lax.all_to_all(marked, 'ctx', 0, 0, tiled=False)  18.5 us
    all_to_all x1, blocking collectives, by_transpose(): lax.all_to_all(gated.reshape(own, n_ctx, T_DEV), 'ctx', 1, 0, tiled=False)  10.7 us
    all_to_all x1, starting transfers between devices, by_transpose(): rows = lax.all_to_all(marked, 'ctx', 0, 0, tiled=False)  7.38 us
    all_gather x1, blocking collectives, by_transpose(): lax.all_gather(gated_block, 'ch', axis=0, tiled=True)  7.18 us
    dot_general x2, matrix products, by_transpose(): jnp.einsum('ipcr,irj->ipcj', rows[..., q * T_DEV:(q + 1) * T_DEV], select...  5.13 us
    reshape x1, local copies, waits for them, and re-layouts, by_transpose(): arrivals.reshape(3, n_ctx, own, capacity)  2.18 us
    scatter x1, local copies, waits for them, and re-layouts, by_transpose(): marked = by_owner.at[:, 0, 0, :].set(marker)  1.53 us
    unnamed x16, local copies, waits for them, and re-layouts  1.32 us
  transfers between devices with their start and end apart: 1, of which 1 were waited for; matrix products, arithmetic and copies ran while one was open for 2% of the time, Pallas kernels for 0%

profile of v3, /device:TPU:0, one launch (start us, length us, event | category | flops | bytes accessed | tf_op | source)
XLA Modules:
  0.0 63.9 jit_solution(651567504899618776)
XLA Ops:
  0.0 0.0 copy-start
  0.0 2.2 %copy.64 = bf16[3,8,32,512]{3,2,0,1:T(8,128)(2,1)} copy(bf16[3,8,32,512]{3,2,1,0:T(8,128)(2,1)} %bitcast.128) | data formatting | bytes 1572864 | tf_op jit(solution)/shard_map/reshape | solution.py:150
  2.2 0.0 copy-start.5
  2.9 0.9 %broadcast_select_fusion = bf16[8,1,1,512]{3,2,1,0:T(2,128)(2,1)S(1)} fusion(pred[512]{0:T(512)(128)(4,1)S(1)} %iota_compare_fusion.2, bf16[8,3,32,512]{3,2,1,0:T(8,128)(2,1)} %bitcast.118), kind=kLoop, calls=%fused_computation.100 | loop fusion | flops 4096 | bytes 16896 | tf_op jit(solution)/shard_map/jit(_where)/select_n | solution.py:151
  3.7 1.5 %scatter.4 = bf16[8,3,32,512]{3,2,1,0:T(8,128)(2,1)} dynamic-update-slice(bf16[8,3,32,512]{3,2,1,0:T(8,128)(2,1)} %bitcast.118, bf16[8,1,1,512]{3,2,1,0:T(2,128)(2,1)S(1)} %broadcast_select_fusion, s32[]{:T(128)} %constant.80.clone.1, s32[]{:T(128)} %constant.80.clone.1, s32[]{:T(128)} %constant.80.clone.1, s32[]{:T(128)} %constant.80.clone.1) | dynamic-update-slice | bytes 16388 | tf_op jit(solution)/shard_map/scatter | solution.py:152
  5.3 0.0 copy-start.2
  5.3 7.4 %all-to-all-start = ((bf16[8,3,32,512]{3,2,1,0:T(8,128)(2,1)}), bf16[8,3,32,512]{3,2,1,0:T(8,128)(2,1)S(1)}, u32[]{:S(2)}, u32[]{:S(2)}) async-start(bf16[8,3,32,512]{3,2,1,0:T(8,128)(2,1)} %scatter.4), calls=%async_computation | async-start | bytes 1572864 | tf_op jit(solution)/shard_map/all_to_all | solution.py:153
  12.6 0.0 copy-start.1
  12.7 0.0 copy-done
  12.7 0.9 %constant_dynamic-slice_fusion.1 = (f32[3,1,32]{2,1,0:T(1,128)S(1)}, f32[3,1,32]{2,1,0:T(1,128)S(1)}, f32[3,1,32]{2,1,0:T(1,128)S(1)}) fusion(f32[3,3,256]{2,1,0:T(4,128)} %param.13, s32[]{:T(128)S(6)} %select_n.44, s32[]{:T(128)S(6)} %add.376, s32[]{:T(128)S(6)} %add.377), kind=kLoop, calls=%fused_computation.127 | loop fusion | bytes 2316 | tf_op jit(solution)/shard_map/slice | solution.py:177
  13.6 0.0 copy-done.5
  13.6 0.1 dynamic_slice.11
  13.7 0.0 copy-done.2
  13.7 0.2 fusion.24
  14.0 0.0 copy-done.1
  14.0 0.2 convolution_add_fusion
  14.2 0.1 fusion.18
  14.3 18.5 %all-to-all-done = bf16[8,3,32,512]{3,2,1,0:T(8,128)(2,1)S(1)} async-done(((bf16[8,3,32,512]{3,2,1,0:T(8,128)(2,1)}), bf16[8,3,32,512]{3,2,1,0:T(8,128)(2,1)S(1)}, u32[]{:S(2)}, u32[]{:S(2)}) %all-to-all-start) | async-done | bytes 786464 | tf_op jit(solution)/shard_map/all_to_all | solution.py:153
  32.8 0.2 fusion.31
  33.1 0.2 reduce-window.8
  33.3 0.1 iota_add_fusion
  33.3 0.1 iota_compare_fusion.1
  33.4 2.6 %fusion.3 = f32[8,3,32,512]{3,2,1,0:T(8,128)S(1)} fusion(s32[8,256]{1,0:T(8,128)S(1)} %iota_add_fusion, pred[8,256]{1,0:T(8,128)(4,1)S(1)} %get-tuple-element.94, bf16[8,3,32,512]{3,2,1,0:T(8,128)(2,1)S(1)} %all-to-all-done), kind=kOutput, calls=%fused_computation.4 | convolution fusion | flops 203423744 | bytes 1976320 | tf_op jit(solution)/shard_map/ipcr,irj->ipcj/dot_general | solution.py:165
  36.0 2.6 %fusion.6 = f32[8,3,32,512]{3,2,1,0:T(8,128)S(1)} fusion(s32[8,256]{1,0:T(8,128)S(1)} %iota_add_fusion, pred[8,256]{1,0:T(8,128)(4,1)S(1)} %get-tuple-element.95, bf16[8,3,32,512]{3,2,1,0:T(8,128)(2,1)S(1)} %all-to-all-done), kind=kOutput, calls=%fused_computation.6 | convolution fusion | flops 203423744 | bytes 1976320 | tf_op jit(solution)/shard_map/ipcr,irj->ipcj/dot_general | solution.py:165
  38.6 0.5 slice_bitcast_fusion.7
  39.1 0.2 pad_add_fusion
  39.3 0.5 fusion.16
  39.9 0.2 fusion.29
  40.1 0.2 convolution_add_fusion.1
  40.4 0.1 copy.44
  40.5 0.1 slice_multiply_fusion.7
  40.6 0.1 slice_multiply_fusion.11
  40.7 0.1 slice_multiply_fusion.15
  40.9 0.0 copy-start.4
  40.9 0.2 subtract_select_fusion
  41.1 0.2 add_select_fusion
  41.3 0.0 copy-start.3
  41.3 0.1 pad_maximum_fusion
  41.4 1.2 %copy-done.3 = f32[512,256,1]{1,0,2:T(8,128)S(1)} copy-done((f32[512,256,1]{1,0,2:T(8,128)S(1)}, f32[512,256,1]{1,0,2:T(8,128)}, u32[]{:S(2)}) %copy-start.3) | copy-done | bytes 524312
  42.5 0.8 %fusion.15 = bf16[1,32,8,256]{3,2,1,0:T(8,128)(2,1)S(1)} fusion(f32[32,8,256]{2,1,0:T(8,128)S(1)} %bitcast.126, f32[512,256,1]{1,0,2:T(8,128)S(1)} %copy-done.3, f32[32,8,512]{2,0,1:T(8,128)S(1)} %pad_maximum_fusion, bf16[32,8,256]{2,1,0:T(8,128)(2,1)S(1)} %bitcast.123, f32[32]{0:T(128)S(1)} %dynamic_slice.11), kind=kOutput, calls=%fused_computation.18 | convolution fusion | flops 402980864 | bytes 1572992 | tf_op jit(solution)/shard_map/cnf,ft->cnt/dot_general | solution.py:208
  43.4 10.7 %all_to_all.20 = bf16[1,32,8,256]{3,1,0,2:T(8,128)(2,1)S(1)} all-to-all(bf16[1,32,8,256]{3,1,0,2:T(8,128)(2,1)S(1)} %copy.33), channel_id=1, replica_groups=mesh['ctx'=8,'ch'=4] {'ctx'}, dimensions={2} | all-to-all | bytes 262144 | tf_op jit(solution)/shard_map/all_to_all | solution.py:212
  54.1 7.2 %all_gather.3 = bf16[1024,256]{1,0:T(8,128)(2,1)S(1)} all-gather(bf16[256,256]{1,0:T(8,128)(2,1)S(1)} %bitcast.130), channel_id=1, replica_groups=mesh['ctx'=8,'ch'=4] {'ch'}, dimensions={0}, use_global_device_ids=true | all-gather | bytes 655360 | tf_op jit(solution)/shard_map/all_gather | solution.py:216
  61.3 0.0 copy-done.4
  61.3 1.3 %fusion.8 = bf16[2048,256]{0,1:T(8,128)(2,1)S(1)} fusion(bf16[1024,256]{1,0:T(8,128)(2,1)S(1)} %all_gather.3, bf16[2048,1024]{1,0:T(8,128)(2,1)S(1)} %copy-done.4), kind=kOutput, calls=%fused_computation.8 | convolution fusion | flops 1074266112 | bytes 5767168 | tf_op jit(solution)/shard_map/dot_general | solution.py:214
  62.6 1.3 %copy.34 = bf16[2048,256]{1,0:T(8,128)(2,1)} copy(bf16[2048,256]{0,1:T(8,128)(2,1)S(1)} %fusion.8) | data formatting | bytes 2097152 | tf_op jit(solution)/shard_map/convert_element_type | solution.py:219
  (17 shorter events, 0.3 us)
Async XLA Ops:
  0.0 12.7 %copy-start = (bf16[256,2048]{1,0:T(8,128)(2,1)S(1)}, bf16[256,2048]{1,0:T(8,128)(2,1)}, u32[]{:S(2)}) copy-start(bf16[256,2048]{1,0:T(8,128)(2,1)} %param.14) | copy-start | bytes 3145732
  2.2 11.4 %copy-start.5 = (f32[256]{0:T(256)S(1)}, f32[256]{0:T(256)}, u32[]{:S(2)}) copy-start(f32[256]{0:T(256)} %param.15) | copy-start | bytes 3076
  5.3 8.5 %copy-start.2 = (bf16[256,512,1]{1,0,2:T(8,128)(2,1)S(1)}, bf16[256,512,1]{1,0,2:T(8,128)(2,1)}, u32[]{:S(2)}) copy-start(bf16[256,512,1]{1,0,2:T(8,128)(2,1)} %constant.189) | copy-start | bytes 786436
  5.3 27.6 %all-to-all-start = ((bf16[8,3,32,512]{3,2,1,0:T(8,128)(2,1)}), bf16[8,3,32,512]{3,2,1,0:T(8,128)(2,1)S(1)}, u32[]{:S(2)}, u32[]{:S(2)}) async-start(bf16[8,3,32,512]{3,2,1,0:T(8,128)(2,1)} %scatter.4), calls=%async_computation | async-start | bytes 1572864 | tf_op jit(solution)/shard_map/all_to_all | solution.py:153
  12.6 1.3 %copy-start.1 = (bf16[256,512,1]{1,0,2:T(8,128)(2,1)S(1)}, bf16[256,512,1]{1,0,2:T(8,128)(2,1)}, u32[]{:S(2)}) copy-start(bf16[256,512,1]{1,0,2:T(8,128)(2,1)} %constant.190) | copy-start | bytes 786436
  40.9 20.4 %copy-start.4 = (bf16[2048,1024]{1,0:T(8,128)(2,1)S(1)}, bf16[2048,1024]{1,0:T(8,128)(2,1)}, u32[]{:S(2)}) copy-start(bf16[2048,1024]{1,0:T(8,128)(2,1)} %param.16) | copy-start | bytes 12582916
  41.3 1.2 %copy-start.3 = (f32[512,256,1]{1,0,2:T(8,128)S(1)}, f32[512,256,1]{1,0,2:T(8,128)}, u32[]{:S(2)}) copy-start(f32[512,256,1]{1,0,2:T(8,128)} %constant.191) | copy-start | bytes 1572868

commit v4 on v1

--- a/solution.py
+++ b/solution.py
@@ -5,6 +5,7 @@
 import ml_dtypes
 import numpy as np
 from jax import lax
+from jax.experimental import pallas as pl
 from jax.sharding import PartitionSpec as P
 
 T_DEV = 256
@@ -159,7 +160,7 @@
     sampler = jnp.arange(n_ctx, dtype=jnp.int32)[:, None, None]
     shift = offsets[:, None, None] - (sampler - 1) * T_DEV
     select = ((row + shift == col) & (row < every_count[:, None, None])).astype(jnp.bfloat16)
-    placed = jnp.einsum("picr,irj->ipcj", rows, select, preferred_element_type=jnp.float32)
+    placed = jnp.einsum("picr,irj->ipcj", rows, select, preferred_element_type=jnp.bfloat16)
     full = sum(
         jnp.pad(placed[i], ((0, 0), (0, 0), (i * T_DEV, (n_ctx - 1 - i) * T_DEV)))
         for i in range(n_ctx)
@@ -204,12 +205,28 @@
     gated = (shorted[0] * conv).astype(jnp.bfloat16)
     back = lax.all_to_all(gated.reshape(own, n_ctx, T_DEV), "ctx", 1, 0, tiled=False)
     gated_block = back.reshape(channels, T_DEV)
-    mixed = jnp.dot(
-        out_weight,
-        lax.all_gather(gated_block, "ch", axis=0, tiled=True),
-        preferred_element_type=jnp.float32,
-    )
-    return mixed.astype(jnp.bfloat16)
+    return project(out_weight, lax.all_gather(gated_block, "ch", axis=0, tiled=True))
+
+
+def project_kernel(w_ref, g_ref, o_ref):
+    o_ref[...] = jnp.dot(
+        w_ref[...], g_ref[...], preferred_element_type=jnp.float32
+    ).astype(o_ref.dtype)
+
+
+def project(weight, gated, rows=512):
+    features, width = weight.shape
+    tokens = gated.shape[1]
+    return pl.pallas_call(
+        project_kernel,
+        grid=(features // rows,),
+        in_specs=[
+            pl.BlockSpec((rows, width), lambda i: (i, 0)),
+            pl.BlockSpec((width, tokens), lambda i: (0, 0)),
+        ],
+        out_specs=pl.BlockSpec((rows, tokens), lambda i: (i, 0)),
+        out_shape=jax.ShapeDtypeStruct((features, tokens), jnp.bfloat16),
+    )(weight, gated)
 
 
 def on_device(arrivals, counts, short_taps, filter_taps, skip_gain, out_weight):

time: 60.3 us -> 62.1 us (1.030)
  Pallas kernels: 0 us -> 4.94 us
  matrix products: 7.65 us -> 5.39 us
  local copies, waits for them, and re-layouts: 4.22 us -> 2.77 us
    pallas_call x0 -> x1, Pallas kernels: none -> 4.94 us  [project(): pl.pallas_call(project_kernel, grid=(features // rows,), in_specs=[pl.Blo...]
    dot_general x2 -> x1, matrix products: 5.9 us -> 3.63 us  [by_transpose(): jnp.einsum('picr,irj->ipcj', rows, select, preferred_element_type=jnp.bfl...]
    convert_element_type x1 -> x0, local copies, waits for them, and re-layouts: 1.31 us -> none  [by_transpose(): return mixed.astype(jnp.bfloat16)]
where the time goes in v4:
time: 62.1 us; the launch traced here: 61.7 us
  waiting for transfers between devices  18.5 us (30%)
  blocking collectives  18.3 us (29%)
  starting transfers between devices  7.25 us (12%)
  matrix products  5.39 us (9%)
  Pallas kernels  4.94 us (8%)
  other arithmetic  3.39 us (5%)
  local copies, waits for them, and re-layouts  2.77 us (4%)
  between operations  1.04 us (2%)
    all_to_all x1, waiting for transfers between devices, by_transpose(): rows = lax.all_to_all(marked, 'ctx', 1, 1, tiled=False)  18.5 us
    all_to_all x1, blocking collectives, by_transpose(): lax.all_to_all(gated.reshape(own, n_ctx, T_DEV), 'ctx', 1, 0, tiled=False)  10.7 us
    all_gather x1, blocking collectives, by_transpose(): lax.all_gather(gated_block, 'ch', axis=0, tiled=True)  7.63 us
    all_to_all x1, starting transfers between devices, by_transpose(): rows = lax.all_to_all(marked, 'ctx', 1, 1, tiled=False)  7.25 us
    pallas_call x1, Pallas kernels, project(): pl.pallas_call(project_kernel, grid=(features // rows,), in_specs=[pl.Blo...  4.94 us
    dot_general x1, matrix products, by_transpose(): jnp.einsum('picr,irj->ipcj', rows, select, preferred_element_type=jnp.bfl...  3.63 us
    select_n x1, other arithmetic, by_transpose(): jnp.where(live[None, None, :], arrivals, jnp.asarray(SENTINEL, arrivals.d...  1.26 us
  transfers between devices with their start and end apart: 1, of which 1 were waited for; matrix products, arithmetic and copies ran while one was open for 3% of the time, Pallas kernels for 0%

profile of v4, /device:TPU:0, one launch (start us, length us, event | category | flops | bytes accessed | tf_op | source)
XLA Modules:
  0.0 61.7 jit_solution(2191313053810980656)
XLA Ops:
  0.0 0.0 copy-start
  0.0 0.0 copy-start.2
  0.0 0.0 copy-start.4
  0.8 0.0 copy-start.1
  0.8 1.3 %broadcast_select_fusion = bf16[3,256,512]{2,1,0:T(8,128)(2,1)S(1)} fusion(bf16[3,256,512]{2,1,0:T(8,128)(2,1)} %param.9, pred[512]{0:T(512)(128)(4,1)S(1)} %iota_compare_fusion.2), kind=kLoop, calls=%fused_computation.13 | loop fusion | flops 393216 | bytes 1573376 | tf_op jit(solution)/shard_map/jit(_where)/select_n | solution.py:151
  2.1 1.0 %copy.25 = bf16[3,8,32,512]{3,2,0,1:T(8,128)(2,1)} copy(bf16[3,8,32,512]{3,2,1,0:T(8,128)(2,1)S(1)} %bitcast.92) | data formatting | bytes 1572864 | tf_op jit(solution)/shard_map/reshape | solution.py:152
  3.0 7.3 %all-to-all-start = ((bf16[3,8,32,512]{3,2,0,1:T(8,128)(2,1)}), bf16[3,8,32,512]{3,2,0,1:T(8,128)(2,1)S(1)}, u32[]{:S(2)}, u32[]{:S(2)}) async-start(bf16[3,8,32,512]{3,2,0,1:T(8,128)(2,1)} %copy.25), calls=%async_computation | async-start | bytes 1572864 | tf_op jit(solution)/shard_map/all_to_all | solution.py:153
  10.3 0.0 copy-done
  10.3 0.9 %constant_dynamic-slice_fusion.1 = (f32[3,1,32]{2,1,0:T(1,128)S(1)}, f32[3,1,32]{2,1,0:T(1,128)S(1)}, f32[3,1,32]{2,1,0:T(1,128)S(1)}) fusion(f32[3,3,256]{2,1,0:T(4,128)} %param.11, s32[]{:T(128)S(6)} %select_n.43, s32[]{:T(128)S(6)} %add.300, s32[]{:T(128)S(6)} %add.301), kind=kLoop, calls=%fused_computation.103 | loop fusion | bytes 2316 | tf_op jit(solution)/shard_map/slice | solution.py:171
  11.2 0.0 copy-done.4
  11.2 0.1 dynamic_slice.11
  11.3 0.0 copy-done.2
  11.3 0.2 fusion.13
  11.6 0.0 copy-done.1
  11.6 0.2 convolution_add_fusion
  11.8 0.1 fusion.9
  11.9 18.5 %all-to-all-done = bf16[3,8,32,512]{3,2,0,1:T(8,128)(2,1)S(1)} async-done(((bf16[3,8,32,512]{3,2,0,1:T(8,128)(2,1)}), bf16[3,8,32,512]{3,2,0,1:T(8,128)(2,1)S(1)}, u32[]{:S(2)}, u32[]{:S(2)}) %all-to-all-start) | async-done | bytes 786464 | tf_op jit(solution)/shard_map/all_to_all | solution.py:153
  30.5 0.2 fusion.20
  30.7 0.1 iota_compare_fusion.1
  30.8 0.2 reduce-window.8
  31.0 0.1 iota_add_fusion
  31.0 3.6 %fusion.2 = bf16[8,3,32,768]{3,2,1,0:T(8,128)(2,1)S(1)} fusion(bf16[3,8,32,512]{3,2,0,1:T(8,128)(2,1)S(1)} %all-to-all-done, s32[8,512]{1,0:T(8,128)S(1)} %iota_add_fusion, pred[8,512]{1,0:T(8,128)(4,1)S(1)} %iota_compare_fusion.1), kind=kOutput, calls=%fused_computation.3 | convolution fusion | flops 610271232 | bytes 1986560 | tf_op jit(solution)/shard_map/picr,irj->ipcj/dot_general | solution.py:163
  34.7 0.1 slice_bitcast_fusion.7
  34.8 0.1 pad_add_fusion
  34.9 0.5 multiply_add_fusion
  35.5 0.1 copy.40
  35.5 0.2 fusion.18
  35.8 0.2 convolution_add_fusion.1
  36.2 0.1 slice_multiply_fusion.12
  36.3 0.1 slice_multiply_fusion.8
  36.3 0.1 slice_multiply_fusion.4
  36.5 0.0 copy-start.3
  36.5 0.2 subtract_select_fusion
  36.7 0.2 add_select_fusion
  36.9 0.1 pad_maximum_fusion
  36.9 0.6 copy-done.3
  37.5 0.9 %fusion.8 = bf16[1,32,8,256]{3,2,1,0:T(8,128)(2,1)S(1)} fusion(f32[32,8,256]{2,1,0:T(8,128)S(1)} %bitcast.98, f32[512,256,1]{1,0,2:T(8,128)S(1)} %copy-done.3, f32[32,8,512]{2,0,1:T(8,128)S(1)} %pad_maximum_fusion, bf16[32,8,256]{2,1,0:T(8,128)(2,1)S(1)} %bitcast.95, f32[32]{0:T(128)S(1)} %dynamic_slice.11), kind=kOutput, calls=%fused_computation.11 | convolution fusion | flops 402980864 | bytes 1572992 | tf_op jit(solution)/shard_map/cnf,ft->cnt/dot_general | solution.py:202
  38.4 10.7 %all_to_all.20 = bf16[1,32,8,256]{3,1,0,2:T(8,128)(2,1)S(1)} all-to-all(bf16[1,32,8,256]{3,1,0,2:T(8,128)(2,1)S(1)} %copy.31), channel_id=1, replica_groups=mesh['ctx'=8,'ch'=4] {'ctx'}, dimensions={2} | all-to-all | bytes 262144 | tf_op jit(solution)/shard_map/all_to_all | solution.py:206
  49.1 7.6 %all_gather.3.g_ref = bf16[1024,256]{1,0:T(8,128)(2,1)} all-gather(bf16[256,256]{1,0:T(8,128)(2,1)S(1)} %bitcast.101), channel_id=1, replica_groups=mesh['ctx'=8,'ch'=4] {'ch'}, dimensions={0}, use_global_device_ids=true | all-gather | bytes 655360 | tf_op jit(solution)/shard_map/all_gather | solution.py:208
  56.7 4.9 %shard_map.91 = bf16[2048,256]{1,0:T(8,128)(2,1)} custom-call(bf16[2048,1024]{1,0:T(8,128)(2,1)} %w_ref.1, bf16[1024,256]{1,0:T(8,128)(2,1)} %all_gather.3.g_ref), custom_call_target="tpu_custom_call" | custom-call | tf_op jit(solution)/shard_map/pallas_call | solution.py:220
  (16 shorter events, 0.3 us)
Async XLA Ops:
  0.0 10.3 %copy-start = (bf16[256,2048]{1,0:T(8,128)(2,1)S(1)}, bf16[256,2048]{1,0:T(8,128)(2,1)}, u32[]{:S(2)}) copy-start(bf16[256,2048]{1,0:T(8,128)(2,1)} %param.12) | copy-start | bytes 3145732
  0.0 11.3 %copy-start.2 = (bf16[256,512,1]{1,0,2:T(8,128)(2,1)S(1)}, bf16[256,512,1]{1,0,2:T(8,128)(2,1)}, u32[]{:S(2)}) copy-start(bf16[256,512,1]{1,0,2:T(8,128)(2,1)} %constant.141) | copy-start | bytes 786436
  0.0 11.2 %copy-start.4 = (f32[256]{0:T(256)S(1)}, f32[256]{0:T(256)}, u32[]{:S(2)}) copy-start(f32[256]{0:T(256)} %param.13) | copy-start | bytes 3076
  0.8 10.8 %copy-start.1 = (bf16[256,512,1]{1,0,2:T(8,128)(2,1)S(1)}, bf16[256,512,1]{1,0,2:T(8,128)(2,1)}, u32[]{:S(2)}) copy-start(bf16[256,512,1]{1,0,2:T(8,128)(2,1)} %constant.142) | copy-start | bytes 786436
  3.0 27.4 %all-to-all-start = ((bf16[3,8,32,512]{3,2,0,1:T(8,128)(2,1)}), bf16[3,8,32,512]{3,2,0,1:T(8,128)(2,1)S(1)}, u32[]{:S(2)}, u32[]{:S(2)}) async-start(bf16[3,8,32,512]{3,2,0,1:T(8,128)(2,1)} %copy.25), calls=%async_computation | async-start | bytes 1572864 | tf_op jit(solution)/shard_map/all_to_all | solution.py:153
  36.5 1.0 %copy-start.3 = (f32[512,256,1]{1,0,2:T(8,128)S(1)}, f32[512,256,1]{1,0,2:T(8,128)}, u32[]{:S(2)}) copy-start(f32[512,256,1]{1,0,2:T(8,128)} %constant.143) | copy-start | bytes 1572868

commit v5 on v1

--- a/solution.py
+++ b/solution.py
@@ -159,7 +159,7 @@
     sampler = jnp.arange(n_ctx, dtype=jnp.int32)[:, None, None]
     shift = offsets[:, None, None] - (sampler - 1) * T_DEV
     select = ((row + shift == col) & (row < every_count[:, None, None])).astype(jnp.bfloat16)
-    placed = jnp.einsum("picr,irj->ipcj", rows, select, preferred_element_type=jnp.float32)
+    placed = jnp.einsum("picr,irj->ipcj", rows, select, preferred_element_type=jnp.bfloat16)
     full = sum(
         jnp.pad(placed[i], ((0, 0), (0, 0), (i * T_DEV, (n_ctx - 1 - i) * T_DEV)))
         for i in range(n_ctx)

time: 60.3 us -> 59.2 us (0.982)
  matrix products: 7.65 us -> 6.7 us
    dot_general x1, matrix products: 4.59 us -> 3.63 us  [by_transpose(): jnp.einsum('picr,irj->ipcj', rows, select, preferred_element_type=jnp.bfl...]
where the time goes in v5:
time: 59.2 us; the launch traced here: 58.9 us
  waiting for transfers between devices  18.5 us (31%)
  blocking collectives  17.9 us (30%)
  starting transfers between devices  7.25 us (12%)
  matrix products  6.7 us (11%)
  local copies, waits for them, and re-layouts  4.08 us (7%)
  other arithmetic  3.39 us (6%)
  between operations  1.06 us (2%)
    all_to_all x1, waiting for transfers between devices, by_transpose(): rows = lax.all_to_all(marked, 'ctx', 1, 1, tiled=False)  18.5 us
    all_to_all x1, blocking collectives, by_transpose(): lax.all_to_all(gated.reshape(own, n_ctx, T_DEV), 'ctx', 1, 0, tiled=False)  10.7 us
    all_to_all x1, starting transfers between devices, by_transpose(): rows = lax.all_to_all(marked, 'ctx', 1, 1, tiled=False)  7.25 us
    all_gather x1, blocking collectives, by_transpose(): lax.all_gather(gated_block, 'ch', axis=0, tiled=True)  7.18 us
    dot_general x1, matrix products, by_transpose(): jnp.einsum('picr,irj->ipcj', rows, select, preferred_element_type=jnp.bfl...  3.63 us
    convert_element_type x1, local copies, waits for them, and re-layouts, by_transpose(): return mixed.astype(jnp.bfloat16)  1.31 us
    dot_general x1, matrix products, by_transpose(): jnp.dot(out_weight, lax.all_gather(gated_block, 'ch', axis=0, tiled=True)...  1.31 us
    select_n x1, other arithmetic, by_transpose(): jnp.where(live[None, None, :], arrivals, jnp.asarray(SENTINEL, arrivals.d...  1.26 us
  transfers between devices with their start and end apart: 1, of which 1 were waited for; matrix products, arithmetic and copies ran while one was open for 3% of the time, Pallas kernels for 0%

profile of v5, /device:TPU:0, one launch (start us, length us, event | category | flops | bytes accessed | tf_op | source)
XLA Modules:
  0.0 58.9 jit_solution(6305264324180627496)
XLA Ops:
  0.0 0.0 copy-start
  0.0 0.0 copy-start.2
  0.0 0.0 copy-start.5
  0.8 0.0 copy-start.1
  0.8 1.3 %broadcast_select_fusion = bf16[3,256,512]{2,1,0:T(8,128)(2,1)S(1)} fusion(bf16[3,256,512]{2,1,0:T(8,128)(2,1)} %param.9, pred[512]{0:T(512)(128)(4,1)S(1)} %iota_compare_fusion.2), kind=kLoop, calls=%fused_computation.15 | loop fusion | flops 393216 | bytes 1573376 | tf_op jit(solution)/shard_map/jit(_where)/select_n | solution.py:150
  2.1 1.0 %copy.27 = bf16[3,8,32,512]{3,2,0,1:T(8,128)(2,1)} copy(bf16[3,8,32,512]{3,2,1,0:T(8,128)(2,1)S(1)} %bitcast.96) | data formatting | bytes 1572864 | tf_op jit(solution)/shard_map/reshape | solution.py:151
  3.0 7.3 %all-to-all-start = ((bf16[3,8,32,512]{3,2,0,1:T(8,128)(2,1)}), bf16[3,8,32,512]{3,2,0,1:T(8,128)(2,1)S(1)}, u32[]{:S(2)}, u32[]{:S(2)}) async-start(bf16[3,8,32,512]{3,2,0,1:T(8,128)(2,1)} %copy.27), calls=%async_computation | async-start | bytes 1572864 | tf_op jit(solution)/shard_map/all_to_all | solution.py:152
  10.3 0.0 copy-done
  10.3 0.9 %constant_dynamic-slice_fusion.1 = (f32[3,1,32]{2,1,0:T(1,128)S(1)}, f32[3,1,32]{2,1,0:T(1,128)S(1)}, f32[3,1,32]{2,1,0:T(1,128)S(1)}) fusion(f32[3,3,256]{2,1,0:T(4,128)} %param.11, s32[]{:T(128)S(6)} %select_n.43, s32[]{:T(128)S(6)} %add.300, s32[]{:T(128)S(6)} %add.301), kind=kLoop, calls=%fused_computation.105 | loop fusion | bytes 2316 | tf_op jit(solution)/shard_map/slice | solution.py:170
  11.2 0.0 copy-done.5
  11.2 0.1 dynamic_slice.11
  11.3 0.0 copy-done.2
  11.3 0.2 fusion.14
  11.6 0.0 copy-done.1
  11.6 0.2 convolution_add_fusion
  11.8 0.1 fusion.10
  11.9 18.5 %all-to-all-done = bf16[3,8,32,512]{3,2,0,1:T(8,128)(2,1)S(1)} async-done(((bf16[3,8,32,512]{3,2,0,1:T(8,128)(2,1)}), bf16[3,8,32,512]{3,2,0,1:T(8,128)(2,1)S(1)}, u32[]{:S(2)}, u32[]{:S(2)}) %all-to-all-start) | async-done | bytes 786464 | tf_op jit(solution)/shard_map/all_to_all | solution.py:152
  30.5 0.2 fusion.21
  30.7 0.1 iota_compare_fusion.1
  30.8 0.2 reduce-window.8
  31.0 0.1 iota_add_fusion
  31.0 3.6 %fusion.2 = bf16[8,3,32,768]{3,2,1,0:T(8,128)(2,1)S(1)} fusion(bf16[3,8,32,512]{3,2,0,1:T(8,128)(2,1)S(1)} %all-to-all-done, s32[8,512]{1,0:T(8,128)S(1)} %iota_add_fusion, pred[8,512]{1,0:T(8,128)(4,1)S(1)} %iota_compare_fusion.1), kind=kOutput, calls=%fused_computation.3 | convolution fusion | flops 610271232 | bytes 1986560 | tf_op jit(solution)/shard_map/picr,irj->ipcj/dot_general | solution.py:162
  34.7 0.1 slice_bitcast_fusion.7
  34.8 0.1 pad_add_fusion
  34.9 0.5 multiply_add_fusion
  35.5 0.1 copy.43
  35.5 0.2 fusion.19
  35.8 0.2 convolution_add_fusion.1
  36.2 0.1 slice_multiply_fusion.12
  36.3 0.1 slice_multiply_fusion.8
  36.3 0.1 slice_multiply_fusion.4
  36.5 0.0 copy-start.3
  36.5 0.2 subtract_select_fusion
  36.7 0.0 copy-start.4
  36.7 0.2 add_select_fusion
  36.9 0.1 pad_maximum_fusion
  36.9 0.6 copy-done.3
  37.5 0.9 %fusion.9 = bf16[1,32,8,256]{3,2,1,0:T(8,128)(2,1)S(1)} fusion(f32[32,8,256]{2,1,0:T(8,128)S(1)} %bitcast.102, f32[512,256,1]{1,0,2:T(8,128)S(1)} %copy-done.3, f32[32,8,512]{2,0,1:T(8,128)S(1)} %pad_maximum_fusion, bf16[32,8,256]{2,1,0:T(8,128)(2,1)S(1)} %bitcast.99, f32[32]{0:T(128)S(1)} %dynamic_slice.11), kind=kOutput, calls=%fused_computation.13 | convolution fusion | flops 402980864 | bytes 1572992 | tf_op jit(solution)/shard_map/cnf,ft->cnt/dot_general | solution.py:201
  38.4 10.7 %all_to_all.20 = bf16[1,32,8,256]{3,1,0,2:T(8,128)(2,1)S(1)} all-to-all(bf16[1,32,8,256]{3,1,0,2:T(8,128)(2,1)S(1)} %copy.33), channel_id=1, replica_groups=mesh['ctx'=8,'ch'=4] {'ctx'}, dimensions={2} | all-to-all | bytes 262144 | tf_op jit(solution)/shard_map/all_to_all | solution.py:205
  49.1 7.2 %all_gather.3 = bf16[1024,256]{1,0:T(8,128)(2,1)S(1)} all-gather(bf16[256,256]{1,0:T(8,128)(2,1)S(1)} %bitcast.105), channel_id=1, replica_groups=mesh['ctx'=8,'ch'=4] {'ch'}, dimensions={0}, use_global_device_ids=true | all-gather | bytes 655360 | tf_op jit(solution)/shard_map/all_gather | solution.py:209
  56.3 0.0 copy-done.4
  56.3 1.3 %fusion.6 = bf16[2048,256]{0,1:T(8,128)(2,1)S(1)} fusion(bf16[1024,256]{1,0:T(8,128)(2,1)S(1)} %all_gather.3, bf16[2048,1024]{1,0:T(8,128)(2,1)S(1)} %copy-done.4), kind=kOutput, calls=%fused_computation.7 | convolution fusion | flops 1074266112 | bytes 5767168 | tf_op jit(solution)/shard_map/dot_general | solution.py:207
  57.6 1.3 %copy.34 = bf16[2048,256]{1,0:T(8,128)(2,1)} copy(bf16[2048,256]{0,1:T(8,128)(2,1)S(1)} %fusion.6) | data formatting | bytes 2097152 | tf_op jit(solution)/shard_map/convert_element_type | solution.py:212
  (16 shorter events, 0.3 us)
Async XLA Ops:
  0.0 10.3 %copy-start = (bf16[256,2048]{1,0:T(8,128)(2,1)S(1)}, bf16[256,2048]{1,0:T(8,128)(2,1)}, u32[]{:S(2)}) copy-start(bf16[256,2048]{1,0:T(8,128)(2,1)} %param.12) | copy-start | bytes 3145732
  0.0 11.3 %copy-start.2 = (bf16[256,512,1]{1,0,2:T(8,128)(2,1)S(1)}, bf16[256,512,1]{1,0,2:T(8,128)(2,1)}, u32[]{:S(2)}) copy-start(bf16[256,512,1]{1,0,2:T(8,128)(2,1)} %constant.141) | copy-start | bytes 786436
  0.0 11.2 %copy-start.5 = (f32[256]{0:T(256)S(1)}, f32[256]{0:T(256)}, u32[]{:S(2)}) copy-start(f32[256]{0:T(256)} %param.13) | copy-start | bytes 3076
  0.8 10.8 %copy-start.1 = (bf16[256,512,1]{1,0,2:T(8,128)(2,1)S(1)}, bf16[256,512,1]{1,0,2:T(8,128)(2,1)}, u32[]{:S(2)}) copy-start(bf16[256,512,1]{1,0,2:T(8,128)(2,1)} %constant.142) | copy-start | bytes 786436
  3.0 27.4 %all-to-all-start = ((bf16[3,8,32,512]{3,2,0,1:T(8,128)(2,1)}), bf16[3,8,32,512]{3,2,0,1:T(8,128)(2,1)S(1)}, u32[]{:S(2)}, u32[]{:S(2)}) async-start(bf16[3,8,32,512]{3,2,0,1:T(8,128)(2,1)} %copy.27), calls=%async_computation | async-start | bytes 1572864 | tf_op jit(solution)/shard_map/all_to_all | solution.py:152
  36.5 1.0 %copy-start.3 = (f32[512,256,1]{1,0,2:T(8,128)S(1)}, f32[512,256,1]{1,0,2:T(8,128)}, u32[]{:S(2)}) copy-start(f32[512,256,1]{1,0,2:T(8,128)} %constant.143) | copy-start | bytes 1572868
  36.7 19.6 %copy-start.4 = (bf16[2048,1024]{1,0:T(8,128)(2,1)S(1)}, bf16[2048,1024]{1,0:T(8,128)(2,1)}, u32[]{:S(2)}) copy-start(bf16[2048,1024]{1,0:T(8,128)(2,1)} %param.14) | copy-start | bytes 12582916

commit v6 on v5

--- a/solution.py
+++ b/solution.py
@@ -11,7 +11,6 @@
 HALF = T_DEV // 2
 PERIOD = 2 * T_DEV
 GROUP = 8
-SENTINEL = 256.0
 
 
 def split_bf16(table):
@@ -146,11 +145,8 @@
     own = channels // n_ctx
     forward, inverse = dft_tables()
 
-    live = jnp.arange(capacity, dtype=jnp.int32) < counts[0]
-    marked = jnp.where(live[None, None, :], arrivals, jnp.asarray(SENTINEL, arrivals.dtype))
-    marked = marked.reshape(3, n_ctx, own, capacity)
-    rows = lax.all_to_all(marked, "ctx", 1, 1, tiled=False)
-    every_count = jnp.sum((rows[0, :, 0, :] != SENTINEL).astype(jnp.int32), axis=1)
+    rows = lax.all_to_all(arrivals.reshape(3, n_ctx, own, capacity), "ctx", 1, 1, tiled=False)
+    every_count = lax.all_gather(counts, "ctx", axis=0, tiled=True)
     offsets = jnp.cumsum(every_count) - every_count
 
     frame = 3 * T_DEV

time: 59.2 us -> 59.9 us (1.012)
  waiting for transfers between devices: 18.5 us -> 0.01 us
  blocking collectives: 17.9 us -> 36.2 us
  local copies, waits for them, and re-layouts: 4.08 us -> 6.68 us
  other arithmetic: 3.39 us -> 1.89 us
    all_to_all x1, waiting for transfers between devices: 18.5 us -> 0.01 us  [by_transpose(): lax.all_to_all(arrivals.reshape(3, n_ctx, own, capacity), 'ctx', 1, 1, ti...]
    unnamed x0 -> x1, blocking collectives: none -> 18.3 us
    unnamed x16 -> x21, local copies, waits for them, and re-layouts: 0.7 us -> 2.06 us
    select_n x1 -> x0, other arithmetic: 1.26 us -> none  [by_transpose(): jnp.where(live[None, None, :], arrivals, jnp.asarray(SENTINEL, arrivals.d...]
    reshape x1, local copies, waits for them, and re-layouts: 0.96 us -> 2.2 us  [by_transpose(): arrivals.reshape(3, n_ctx, own, capacity)]
  transfers between devices with their start and end apart: 1 -> 1, of which waited for: 1 -> 0; matrix products, arithmetic and copies ran while one was open for 3% -> 5% of each run, Pallas kernels for 0% -> 0%
where the time goes in v6:
time: 59.9 us; the launch traced here: 59.6 us
  blocking collectives  36.2 us (60%)
  starting transfers between devices  7.26 us (12%)
  local copies, waits for them, and re-layouts  6.68 us (11%)
  matrix products  6.59 us (11%)
  other arithmetic  1.89 us (3%)
  between operations  0.93 us (2%)
    unnamed x1, blocking collectives  18.3 us
    all_to_all x1, blocking collectives, by_transpose(): lax.all_to_all(gated.reshape(own, n_ctx, T_DEV), 'ctx', 1, 0, tiled=False)  10.7 us
    all_to_all x1, starting transfers between devices, by_transpose(): lax.all_to_all(arrivals.reshape(3, n_ctx, own, capacity), 'ctx', 1, 1, ti...  7.26 us
    all_gather x1, blocking collectives, by_transpose(): lax.all_gather(gated_block, 'ch', axis=0, tiled=True)  7.18 us
    dot_general x1, matrix products, by_transpose(): jnp.einsum('picr,irj->ipcj', rows, select, preferred_element_type=jnp.bfl...  3.53 us
    reshape x1, local copies, waits for them, and re-layouts, by_transpose(): arrivals.reshape(3, n_ctx, own, capacity)  2.2 us
    unnamed x21, local copies, waits for them, and re-layouts  2.06 us
    convert_element_type x1, local copies, waits for them, and re-layouts, by_transpose(): return mixed.astype(jnp.bfloat16)  1.31 us
  transfers between devices with their start and end apart: 1, of which 0 were waited for; matrix products, arithmetic and copies ran while one was open for 5% of the time, Pallas kernels for 0%

profile of v6, /device:TPU:0, one launch (start us, length us, event | category | flops | bytes accessed | tf_op | source)
XLA Modules:
  0.0 59.6 jit_solution(1919022495270531363)
XLA Ops:
  0.0 0.0 copy-start
  0.0 0.0 copy-start.6
  0.0 0.0 copy-start.2
  0.0 0.0 copy-start.1
  0.0 0.0 copy-start.5
  0.0 2.2 %copy.27 = bf16[3,8,32,512]{3,2,0,1:T(8,128)(2,1)} copy(bf16[3,8,32,512]{3,2,1,0:T(8,128)(2,1)} %bitcast.106) | data formatting | bytes 1572864 | tf_op jit(solution)/shard_map/reshape | solution.py:148
  2.2 7.3 %all-to-all-start = ((bf16[3,8,32,512]{3,2,0,1:T(8,128)(2,1)}), bf16[3,8,32,512]{3,2,0,1:T(8,128)(2,1)S(1)}, u32[]{:S(2)}, u32[]{:S(2)}) async-start(bf16[3,8,32,512]{3,2,0,1:T(8,128)(2,1)} %copy.27), calls=%async_computation | async-start | bytes 1572864 | tf_op jit(solution)/shard_map/all_to_all | solution.py:148
  10.1 0.0 copy-done.6
  10.2 0.6 %dynamic-slice = u32[1]{0:T(128)} dynamic-slice(u32[32]{0:T(128)S(1)} %copy-done.6, u32[]{:T(128)S(6)} %add.296), dynamic_slice_sizes={1} | dynamic-slice | bytes 12
  10.8 0.7 %dynamic-update-slice = s32[8]{0:T(128)S(1)} dynamic-update-slice(s32[8]{0:T(128)S(1)} %broadcast.186, s32[1]{0:T(128)S(6)} %copy.64, u32[]{:T(128)} %bitcast) | dynamic-update-slice | bytes 12
  11.5 18.3 %all-reduce.37 = s32[8]{0:T(128)S(1)} all-reduce(s32[8]{0:T(128)S(1)} %dynamic-update-slice), channel_id=1, replica_groups=mesh['ctx'=8,'ch'=4] {'ctx'}, use_global_device_ids=true, to_apply=%add.37 | all-reduce | flops 8 | bytes 64
  29.9 0.1 iota_compare_fusion.1
  29.9 0.2 reduce-window.9
  30.1 0.0 copy-done
  30.1 0.9 %constant_dynamic-slice_fusion.1 = (f32[3,1,32]{2,1,0:T(1,128)S(1)}, f32[3,1,32]{2,1,0:T(1,128)S(1)}, f32[3,1,32]{2,1,0:T(1,128)S(1)}) fusion(f32[3,3,256]{2,1,0:T(4,128)} %param.11, s32[]{:T(128)S(6)} %select_n.39, s32[]{:T(128)S(6)} %add.298, s32[]{:T(128)S(6)} %add.299), kind=kLoop, calls=%fused_computation.102 | loop fusion | bytes 2316 | tf_op jit(solution)/shard_map/slice | solution.py:166
  31.0 0.0 copy-done.5
  31.1 0.1 dynamic_slice.11
  31.2 0.1 iota_add_fusion
  31.2 0.0 copy-done.2
  31.2 0.2 fusion.17
  31.5 0.0 copy-done.1
  31.5 0.2 convolution_add_fusion
  31.7 0.1 fusion.13
  31.8 0.0 all-to-all-done
  31.8 3.5 %fusion.7 = bf16[8,3,32,768]{3,2,1,0:T(8,128)(2,1)S(1)} fusion(bf16[3,8,32,512]{3,2,0,1:T(8,128)(2,1)S(1)} %all-to-all-done, s32[8,512]{1,0:T(8,128)S(1)} %iota_add_fusion, pred[8,512]{1,0:T(8,128)(4,1)S(1)} %iota_compare_fusion.1), kind=kOutput, calls=%fused_computation.8 | convolution fusion | flops 610271232 | bytes 1986560 | tf_op jit(solution)/shard_map/picr,irj->ipcj/dot_general | solution.py:158
  35.4 0.1 slice_bitcast_fusion.7
  35.4 0.1 pad_add_fusion
  35.6 0.5 multiply_add_fusion
  36.1 0.1 copy.43
  36.2 0.2 fusion.22
  36.5 0.2 convolution_add_fusion.1
  36.9 0.1 slice_multiply_fusion.12
  36.9 0.1 slice_multiply_fusion.8
  37.0 0.1 slice_multiply_fusion.4
  37.1 0.0 copy-start.3
  37.1 0.2 subtract_select_fusion
  37.3 0.0 copy-start.4
  37.4 0.2 add_select_fusion
  37.6 0.1 pad_maximum_fusion
  37.6 0.6 copy-done.3
  38.2 0.9 %fusion.12 = bf16[1,32,8,256]{3,2,1,0:T(8,128)(2,1)S(1)} fusion(f32[32,8,256]{2,1,0:T(8,128)S(1)} %bitcast.104, f32[512,256,1]{1,0,2:T(8,128)S(1)} %copy-done.3, f32[32,8,512]{2,0,1:T(8,128)S(1)} %pad_maximum_fusion, bf16[32,8,256]{2,1,0:T(8,128)(2,1)S(1)} %bitcast.101, f32[32]{0:T(128)S(1)} %dynamic_slice.11), kind=kOutput, calls=%fused_computation.14 | convolution fusion | flops 402980864 | bytes 1572992 | tf_op jit(solution)/shard_map/cnf,ft->cnt/dot_general | solution.py:197
  39.1 10.7 %all_to_all.20 = bf16[1,32,8,256]{3,1,0,2:T(8,128)(2,1)S(1)} all-to-all(bf16[1,32,8,256]{3,1,0,2:T(8,128)(2,1)S(1)} %copy.33), channel_id=1, replica_groups=mesh['ctx'=8,'ch'=4] {'ctx'}, dimensions={2} | all-to-all | bytes 262144 | tf_op jit(solution)/shard_map/all_to_all | solution.py:201
  49.8 7.2 %all_gather.7 = bf16[1024,256]{1,0:T(8,128)(2,1)S(1)} all-gather(bf16[256,256]{1,0:T(8,128)(2,1)S(1)} %bitcast.108), channel_id=1, replica_groups=mesh['ctx'=8,'ch'=4] {'ch'}, dimensions={0}, use_global_device_ids=true | all-gather | bytes 655360 | tf_op jit(solution)/shard_map/all_gather | solution.py:205
  57.0 0.0 copy-done.4
  57.0 1.3 %fusion.6 = bf16[2048,256]{0,1:T(8,128)(2,1)S(1)} fusion(bf16[1024,256]{1,0:T(8,128)(2,1)S(1)} %all_gather.7, bf16[2048,1024]{1,0:T(8,128)(2,1)S(1)} %copy-done.4), kind=kOutput, calls=%fused_computation.7 | convolution fusion | flops 1074266112 | bytes 5767168 | tf_op jit(solution)/shard_map/dot_general | solution.py:203
  58.3 1.3 %copy.34 = bf16[2048,256]{1,0:T(8,128)(2,1)} copy(bf16[2048,256]{0,1:T(8,128)(2,1)S(1)} %fusion.6) | data formatting | bytes 2097152 | tf_op jit(solution)/shard_map/convert_element_type | solution.py:208
  (16 shorter events, 0.3 us)
Async XLA Ops:
  0.0 30.1 %copy-start = (bf16[256,2048]{1,0:T(8,128)(2,1)S(1)}, bf16[256,2048]{1,0:T(8,128)(2,1)}, u32[]{:S(2)}) copy-start(bf16[256,2048]{1,0:T(8,128)(2,1)} %param.12) | copy-start | bytes 3145732
  0.0 10.1 %copy-start.6 = (u32[32]{0:T(128)S(1)}, u32[32]{0:T(128)}, u32[]{:S(2)}) copy-start(u32[32]{0:T(128)} %constant.140) | copy-start | bytes 388
  0.0 31.2 %copy-start.2 = (bf16[256,512,1]{1,0,2:T(8,128)(2,1)S(1)}, bf16[256,512,1]{1,0,2:T(8,128)(2,1)}, u32[]{:S(2)}) copy-start(bf16[256,512,1]{1,0,2:T(8,128)(2,1)} %constant.144) | copy-start | bytes 786436
  0.0 31.5 %copy-start.1 = (bf16[256,512,1]{1,0,2:T(8,128)(2,1)S(1)}, bf16[256,512,1]{1,0,2:T(8,128)(2,1)}, u32[]{:S(2)}) copy-start(bf16[256,512,1]{1,0,2:T(8,128)(2,1)} %constant.145) | copy-start | bytes 786436
  0.0 31.0 %copy-start.5 = (f32[256]{0:T(256)S(1)}, f32[256]{0:T(256)}, u32[]{:S(2)}) copy-start(f32[256]{0:T(256)} %param.13) | copy-start | bytes 3076
  2.2 29.6 %all-to-all-start = ((bf16[3,8,32,512]{3,2,0,1:T(8,128)(2,1)}), bf16[3,8,32,512]{3,2,0,1:T(8,128)(2,1)S(1)}, u32[]{:S(2)}, u32[]{:S(2)}) async-start(bf16[3,8,32,512]{3,2,0,1:T(8,128)(2,1)} %copy.27), calls=%async_computation | async-start | bytes 1572864 | tf_op jit(solution)/shard_map/all_to_all | solution.py:148
  37.1 1.0 %copy-start.3 = (f32[512,256,1]{1,0,2:T(8,128)S(1)}, f32[512,256,1]{1,0,2:T(8,128)}, u32[]{:S(2)}) copy-start(f32[512,256,1]{1,0,2:T(8,128)} %constant.146) | copy-start | bytes 1572868
  37.3 19.6 %copy-start.4 = (bf16[2048,1024]{1,0:T(8,128)(2,1)S(1)}, bf16[2048,1024]{1,0:T(8,128)(2,1)}, u32[]{:S(2)}) copy-start(bf16[2048,1024]{1,0:T(8,128)(2,1)} %param.14) | copy-start | bytes 12582916

commit v7 on v6

--- a/solution.py
+++ b/solution.py
@@ -145,8 +145,43 @@
     own = channels // n_ctx
     forward, inverse = dft_tables()
 
-    rows = lax.all_to_all(arrivals.reshape(3, n_ctx, own, capacity), "ctx", 1, 1, tiled=False)
-    every_count = lax.all_gather(counts, "ctx", axis=0, tiled=True)
+    count = counts[0]
+    pair = arrivals[1:].astype(jnp.float32)
+    ahead = jnp.pad(pair, ((0, 0), (0, 0), (2, 0)))
+    near = short_taps[1:, 0, :, None] * ahead[:, :, 2:]
+    near = near + short_taps[1:, 1, :, None] * ahead[:, :, 1:-1]
+    near = near + short_taps[1:, 2, :, None] * ahead[:, :, :-2]
+    own_mixed = (near[0] * near[1]).astype(jnp.bfloat16)
+    row = jnp.arange(capacity, dtype=jnp.int32)
+    last = jnp.stack(
+        [jnp.sum(jnp.where(row == count - 2 + k, pair, 0.0), axis=2) for k in range(2)], axis=2
+    )
+    edge = jnp.concatenate(
+        [pair[0, :, :2], pair[1, :, :2], last[0], last[1]], axis=1
+    ).astype(jnp.bfloat16)
+    code = jnp.stack([count // 16, count % 16]).astype(jnp.bfloat16)
+    edge_row = jnp.concatenate(
+        [
+            edge.reshape(n_ctx, own * 8),
+            jnp.broadcast_to(code, (n_ctx, 2)),
+            jnp.zeros((n_ctx, capacity - own * 8 - 2), jnp.bfloat16),
+        ],
+        axis=1,
+    )
+    payload = jnp.concatenate(
+        [
+            arrivals[0].reshape(n_ctx, own, capacity),
+            own_mixed.reshape(n_ctx, own, capacity),
+            edge_row[:, None, :],
+        ],
+        axis=1,
+    )
+    got = lax.all_to_all(payload, "ctx", 0, 0, tiled=False)
+    rows = got[:, : 2 * own]
+    edge_in = got[:, 2 * own]
+    every_count = (
+        edge_in[:, own * 8].astype(jnp.int32) * 16 + edge_in[:, own * 8 + 1].astype(jnp.int32)
+    )
     offsets = jnp.cumsum(every_count) - every_count
 
     frame = 3 * T_DEV
@@ -155,18 +190,41 @@
     sampler = jnp.arange(n_ctx, dtype=jnp.int32)[:, None, None]
     shift = offsets[:, None, None] - (sampler - 1) * T_DEV
     select = ((row + shift == col) & (row < every_count[:, None, None])).astype(jnp.bfloat16)
-    placed = jnp.einsum("picr,irj->ipcj", rows, select, preferred_element_type=jnp.bfloat16)
+    placed = jnp.einsum("icr,irj->icj", rows, select, preferred_element_type=jnp.bfloat16)
     full = sum(
-        jnp.pad(placed[i], ((0, 0), (0, 0), (i * T_DEV, (n_ctx - 1 - i) * T_DEV)))
-        for i in range(n_ctx)
-    )
-    wide = full[:, :, T_DEV - 2 : T_DEV + length]
+        jnp.pad(placed[i], ((0, 0), (i * T_DEV, (n_ctx - 1 - i) * T_DEV))) for i in range(n_ctx)
+    )
     first = device * own
     taps = lax.dynamic_slice_in_dim(short_taps, first, own, 2)
-    shorted = taps[:, 0, :, None] * wide[:, :, 2:]
-    shorted = shorted + taps[:, 1, :, None] * wide[:, :, 1:-1]
-    shorted = shorted + taps[:, 2, :, None] * wide[:, :, :-2]
-    mixed_input = (shorted[1] * shorted[2]).astype(jnp.bfloat16)
+    gate = full[:own, T_DEV - 2 : T_DEV + length].astype(jnp.float32)
+    shorted_gate = taps[0, 0, :, None] * gate[:, 2:]
+    shorted_gate = shorted_gate + taps[0, 1, :, None] * gate[:, 1:-1]
+    shorted_gate = shorted_gate + taps[0, 2, :, None] * gate[:, :-2]
+    from_senders = full[own:, T_DEV : T_DEV + length]
+
+    values = edge_in[:, : own * 8].reshape(n_ctx, own, 8)
+    count_col = every_count[:, None]
+    at_row = jnp.concatenate(
+        [jnp.zeros_like(count_col), jnp.ones_like(count_col), count_col - 2, count_col - 1], axis=1
+    )
+    valid = jnp.concatenate([at_row[:, :2] < count_col, at_row[:, 2:] >= 2], axis=1)
+    spot = offsets[:, None] + at_row
+    slot = jnp.arange(length + 2, dtype=jnp.int32)[None, None, :]
+    marks = ((slot - 2 == spot[:, :, None]) & valid[:, :, None]).astype(jnp.bfloat16)
+    near_in = []
+    for part in range(2):
+        pick = values[:, :, jnp.array([2 * part, 2 * part + 1, 4 + 2 * part, 5 + 2 * part])]
+        around = jnp.einsum(
+            "ics,isj->cj", pick, marks, preferred_element_type=jnp.float32
+        )
+        s = taps[1 + part, 0, :, None] * around[:, 2:]
+        s = s + taps[1 + part, 1, :, None] * around[:, 1:-1]
+        s = s + taps[1 + part, 2, :, None] * around[:, :-2]
+        near_in.append(s)
+    at_start = jnp.sum(marks[:, :2, 2:].astype(jnp.float32), axis=(0, 1)) > 0
+    mixed_input = jnp.where(
+        at_start[None, :], (near_in[0] * near_in[1]).astype(jnp.bfloat16), from_senders
+    )
 
     x_spec = transform(mixed_input.reshape(own, n_blocks, T_DEV), forward, "cnt,tf->cnf")
     own_taps = lax.dynamic_slice_in_dim(filter_taps, first, own, 0)
@@ -197,7 +255,7 @@
     conv_core = jnp.einsum("cnf,ft->cnt", spectrum, inverse, precision=lax.Precision.HIGHEST)
     gains = lax.dynamic_slice_in_dim(skip_gain, first, own, 0)
     conv = conv_core.reshape(own, length) + gains[:, None] * mixed_input.astype(jnp.float32)
-    gated = (shorted[0] * conv).astype(jnp.bfloat16)
+    gated = (shorted_gate * conv).astype(jnp.bfloat16)
     back = lax.all_to_all(gated.reshape(own, n_ctx, T_DEV), "ctx", 1, 0, tiled=False)
     gated_block = back.reshape(channels, T_DEV)
     mixed = jnp.dot(

time: 59.9 us -> 64.2 us (1.072)
  blocking collectives: 36.2 us -> 18 us
  waiting for transfers between devices: 0.01 us -> 11.8 us
  other arithmetic: 1.89 us -> 8.31 us
  local copies, waits for them, and re-layouts: 6.68 us -> 8.99 us
  matrix products: 6.59 us -> 7.89 us
    unnamed x1 -> x0, blocking collectives: 18.3 us -> none
    all_to_all x1, waiting for transfers between devices: 0.01 us -> 11.8 us  [by_transpose(): got = lax.all_to_all(payload, 'ctx', 0, 0, tiled=False)]
    reshape x1 -> x2, local copies, waits for them, and re-layouts: 2.2 us -> 0.22 us  [by_transpose(): values = edge_in[:, :own * 8].reshape(n_ctx, own, 8)]
    convert_element_type x1 -> x4, other arithmetic: 0.05 us -> 1.63 us  [the longest x1 1.2 us: by_transpose(): pair = arrivals[1:].astype(jnp.float32)]
    mul x0 -> x1, local copies, waits for them, and re-layouts: none -> 1.52 us  [by_transpose(): shorted_gate = taps[0, 0, :, None] * gate[:, 2:]]
    reduce_sum x0 -> x2, other arithmetic: none -> 1.48 us  [the longest x1 1.37 us: by_transpose(): jnp.sum(jnp.where(row == count - 2 + k, pair, 0.0), axis=2)]
    dot_general x1 -> x3, matrix products: 3.53 us -> 4.82 us  [the longest x1 4.31 us: by_transpose(): jnp.einsum('icr,irj->icj', rows, select, preferred_element_type=jnp.bfloa...]
    gather x0 -> x2, local copies, waits for them, and re-layouts: none -> 1.13 us  [by_transpose(): values[:, :, jnp.array([2 * part, 2 * part + 1, 4 + 2 * part, 5 + 2 * par...]
  transfers between devices with their start and end apart: 1 -> 1, of which waited for: 0 -> 1; matrix products, arithmetic and copies ran while one was open for 5% -> 6% of each run, Pallas kernels for 0% -> 0%
where the time goes in v7:
time: 64.2 us; the launch traced here: 63.7 us
  blocking collectives  18 us (28%)
  waiting for transfers between devices  11.8 us (18%)
  local copies, waits for them, and re-layouts  8.99 us (14%)
  other arithmetic  8.31 us (13%)
  matrix products  7.89 us (12%)
  starting transfers between devices  7.25 us (11%)
  between operations  1.46 us (2%)
    all_to_all x1, waiting for transfers between devices, by_transpose(): got = lax.all_to_all(payload, 'ctx', 0, 0, tiled=False)  11.8 us
    all_to_all x1, blocking collectives, by_transpose(): lax.all_to_all(gated.reshape(own, n_ctx, T_DEV), 'ctx', 1, 0, tiled=False)  10.8 us
    all_to_all x1, starting transfers between devices, by_transpose(): got = lax.all_to_all(payload, 'ctx', 0, 0, tiled=False)  7.25 us
    all_gather x1, blocking collectives, by_transpose(): lax.all_gather(gated_block, 'ch', axis=0, tiled=True)  7.18 us
    dot_general x1, matrix products, by_transpose(): jnp.einsum('icr,irj->icj', rows, select, preferred_element_type=jnp.bfloa...  4.31 us
    mul x1, local copies, waits for them, and re-layouts, by_transpose(): shorted_gate = taps[0, 0, :, None] * gate[:, 2:]  1.52 us
    reduce_sum x1, other arithmetic, by_transpose(): jnp.sum(jnp.where(row == count - 2 + k, pair, 0.0), axis=2)  1.37 us
    convert_element_type x1, local copies, waits for them, and re-layouts, by_transpose(): return mixed.astype(jnp.bfloat16)  1.31 us
  transfers between devices with their start and end apart: 1, of which 1 were waited for; matrix products, arithmetic and copies ran while one was open for 6% of the time, Pallas kernels for 0%

profile of v7, /device:TPU:0, one launch (start us, length us, event | category | flops | bytes accessed | tf_op | source)
XLA Modules:
  0.0 63.7 jit_solution(4575788041601861336)
XLA Ops:
  0.8 0.9 %fusion.49 = (bf16[1,256,2]{2,1,0:T(8,128)(2,1)S(1)}, bf16[1,256,2]{2,1,0:T(8,128)(2,1)S(1)}) fusion(bf16[3,256,512]{2,1,0:T(8,128)(2,1)} %param.11), kind=kLoop, calls=%fused_computation.177 | loop fusion | bytes 4096 | tf_op jit(solution)/shard_map/slice | solution.py:160
  1.7 0.0 slice-start
  1.7 1.2 %slice_convert_fusion = f32[2,256,512]{2,1,0:T(8,128)S(1)} fusion(bf16[3,256,512]{2,1,0:T(8,128)(2,1)} %param.11), kind=kLoop, calls=%fused_computation.30 | loop fusion | flops 262144 | bytes 1572864 | tf_op jit(solution)/shard_map/convert_element_type | solution.py:149
  2.9 1.4 %select_reduce_fusion.1 = (bf16[2,256]{1,0:T(2,128)(2,1)S(1)}, bf16[2,256]{1,0:T(2,128)(2,1)S(1)}) fusion(pred[512]{0:T(512)(128)(4,1)S(1)} %get-tuple-element.93, bf16[3,256,512]{2,1,0:T(8,128)(2,1)} %param.11, pred[512]{0:T(512)(128)(4,1)S(1)} %get-tuple-element.92), kind=kLoop, calls=%fused_computation.20 | loop fusion | flops 1309696 | bytes 527360 | tf_op jit(solution)/shard_map/reduce_sum | solution.py:157
  4.4 0.8 %fusion.50 = (f32[2,1,256]{2,1,0:T(1,128)S(1)}, f32[2,1,256]{2,1,0:T(1,128)S(1)}, f32[2,1,256]{2,1,0:T(1,128)S(1)}) fusion(f32[3,3,256]{2,1,0:T(4,128)} %param.13), kind=kLoop, calls=%fused_computation.178 | loop fusion | bytes 12288 | tf_op jit(solution)/shard_map/slice | solution.py:151
  5.2 0.1 copy.100
  5.3 0.1 copy.101
  5.4 0.1 copy.77
  5.6 0.1 convert_element_type.127
  5.7 0.1 pad_maximum_fusion.3
  5.8 0.1 pad.181.clone
  5.9 0.9 %fusion.8 = f32[2,256,512]{2,1,0:T(8,128)S(1)} fusion(f32[2,256,512]{2,1,0:T(8,128)S(1)} %slice_convert_fusion, f32[2,256]{1,0:T(2,128)S(1)} %get-tuple-element.94, f32[2,256]{1,0:T(2,128)S(1)} %get-tuple-element.95, f32[2,256]{1,0:T(2,128)S(1)} %bitcast.155), kind=kLoop, calls=%fused_computation.17 | loop fusion | flops 1310720 | bytes 2103296 | tf_op jit(solution)/shard_map/add | solution.py:153
  6.8 0.1 fusion.12
  6.9 0.9 %pad_maximum_fusion = bf16[8,65,512]{2,1,0:T(8,128)(2,1)} fusion(bf16[8,1,512]{2,1,0:T(2,128)(2,1)S(1)} %copy.78, bf16[8,32,512]{2,1,0:T(8,128)(2,1)S(1)} %bitcast.146, bf16[8,32,512]{2,1,0:T(8,128)(2,1)S(1)} %bitcast.141), kind=kLoop, calls=%fused_computation.21 | loop fusion | flops 1597440 | bytes 1064960 | tf_op jit(solution)/shard_map/concatenate | solution.py:171
  7.8 7.3 %all-to-all-start = ((bf16[8,65,512]{2,1,0:T(8,128)(2,1)}), bf16[8,65,512]{2,1,0:T(8,128)(2,1)S(1)}, u32[]{:S(2)}, u32[]{:S(2)}) async-start(bf16[8,65,512]{2,1,0:T(8,128)(2,1)} %pad_maximum_fusion), calls=%async_computation | async-start | bytes 1179648 | tf_op jit(solution)/shard_map/all_to_all | solution.py:179
  15.0 0.6 iota_compare_fusion.5
  15.7 0.6 dynamic_slice.11
  16.3 0.1 pad_add_fusion.3
  16.4 1.5 %fusion.45 = (f32[32]{0:T(128)}, f32[32]{0:T(128)}, f32[32]{0:T(128)}, f32[32]{0:T(128)}, f32[32]{0:T(128)}, /*index=5*/f32[32]{0:T(128)}, f32[32]{0:T(128)}, f32[32]{0:T(128)}, f32[32]{0:T(128)}) fusion(f32[3,3,256]{2,1,0:T(4,128)} %param.13, s32[]{:T(128)S(6)} %select_n.66, s32[]{:T(128)S(6)} %add.403, s32[]{:T(128)S(6)} %add.402), kind=kLoop, calls=%fused_computation.167 | loop fusion | bytes 2316 | tf_op jit(solution)/shard_map/mul | solution.py:200
  17.9 0.2 fusion.26
  18.1 0.2 convolution_add_fusion
  18.4 0.1 fusion.10
  18.4 0.6 slice_bitcast_fusion.21
  19.1 11.8 %all-to-all-done = bf16[8,65,512]{2,1,0:T(8,128)(2,1)S(1)} async-done(((bf16[8,65,512]{2,1,0:T(8,128)(2,1)}), bf16[8,65,512]{2,1,0:T(8,128)(2,1)S(1)}, u32[]{:S(2)}, u32[]{:S(2)}) %all-to-all-start) | async-done | bytes 532512 | tf_op jit(solution)/shard_map/all_to_all | solution.py:179
  30.9 0.1 convert_add_fusion
  31.1 0.2 subtract_reduce_fusion
  31.3 0.7 %iota_compare_fusion.1 = pred[8,512]{1,0:T(8,128)(4,1)} fusion(s32[8]{0:T(128)S(1)} %get-tuple-element.8), kind=kLoop, calls=%fused_computation.119 | loop fusion | flops 4096 | bytes 4128 | tf_op jit(solution)/shard_map/lt | solution.py:192
  32.0 0.1 copy.80
  32.0 0.1 copy.81
  32.1 0.1 add_add_fusion
  32.2 0.1 copy.79
  32.3 0.1 iota_add_fusion
  32.3 0.1 reshape.202
  32.5 0.1 copy.82
  32.6 0.6 gather_fusion.1
  33.1 0.6 gather_fusion
  33.7 0.1 compare_and_fusion
  33.9 0.1 convert_reduce_fusion
  34.0 4.3 %fusion.1 = bf16[8,64,768]{2,1,0:T(8,128)(2,1)S(1)} fusion(s32[8,512]{1,0:T(8,128)S(1)} %iota_add_fusion, pred[8,512]{1,0:T(8,128)(4,1)} %iota_compare_fusion.1, bf16[8,65,512]{2,1,0:T(8,128)(2,1)S(1)} %all-to-all-done), kind=kOutput, calls=%fused_computation.4 | convolution fusion | flops 408944640 | bytes 1331200 | tf_op jit(solution)/shard_map/icr,irj->icj/dot_general | solution.py:193
  38.4 0.1 slice_bitcast_fusion.7
  38.4 0.3 convolution_bitcast_fusion.1
  38.7 0.3 convolution_bitcast_fusion
  38.9 0.1 pad_add_fusion
  39.0 0.1 slice_convert_fusion.1
  39.2 0.4 slice_select_fusion
  39.6 0.2 fusion.29
  39.8 0.2 convolution_add_fusion.1
  40.3 0.1 slice_multiply_fusion.21
  40.3 0.0 copy-done.5
  40.4 0.1 slice_multiply_fusion.17
  40.4 0.2 copy-done.4
  40.6 0.1 slice_multiply_fusion.13
  40.7 0.0 copy-done.9
  40.7 0.2 subtract_select_fusion
  41.0 0.2 add_select_fusion
  41.2 0.1 pad_maximum_fusion.1
  41.3 0.5 copy-done.3
  41.8 0.9 %fusion.13 = f32[32,8,256]{2,1,0:T(8,128)S(1)} fusion(f32[512,256,1]{1,0,2:T(8,128)S(1)} %copy-done.3, f32[32,8,512]{2,0,1:T(8,128)S(1)} %pad_maximum_fusion.1), kind=kOutput, calls=%fused_computation.28 | convolution fusion | flops 402653184 | bytes 1310720 | tf_op jit(solution)/shard_map/cnf,ft->cnt/dot_general | solution.py:255
  42.7 0.1 copy.104
  42.8 0.3 fusion.23
  43.1 10.8 %all_to_all.20 = bf16[1,32,8,256]{3,1,0,2:T(8,128)(2,1)S(1)} all-to-all(bf16[1,32,8,256]{3,1,0,2:T(8,128)(2,1)S(1)} %copy.89), channel_id=1, replica_groups=mesh['ctx'=8,'ch'=4] {'ctx'}, dimensions={2} | all-to-all | bytes 262144 | tf_op jit(solution)/shard_map/all_to_all | solution.py:259
  53.9 7.2 %all_gather.3 = bf16[1024,256]{1,0:T(8,128)(2,1)S(1)} all-gather(bf16[256,256]{1,0:T(8,128)(2,1)S(1)} %bitcast.150), channel_id=1, replica_groups=mesh['ctx'=8,'ch'=4] {'ch'}, dimensions={0}, use_global_device_ids=true | all-gather | bytes 655360 | tf_op jit(solution)/shard_map/all_gather | solution.py:263
  61.1 1.3 %fusion.5 = bf16[2048,256]{0,1:T(8,128)(2,1)S(1)} fusion(bf16[1024,256]{1,0:T(8,128)(2,1)S(1)} %all_gather.3, bf16[2048,1024]{1,0:T(8,128)(2,1)S(1)} %copy-done.19), kind=kOutput, calls=%fused_computation.10 | convolution fusion | flops 1074266112 | bytes 5767168 | tf_op jit(solution)/shard_map/dot_general | solution.py:261
  62.4 1.3 %copy.90 = bf16[2048,256]{1,0:T(8,128)(2,1)} copy(bf16[2048,256]{0,1:T(8,128)(2,1)S(1)} %fusion.5) | data formatting | bytes 2097152 | tf_op jit(solution)/shard_map/convert_element_type | solution.py:266
  (71 shorter events, 0.5 us)
Async XLA Ops:
  0.0 16.3 %copy-start = (bf16[256,2048]{1,0:T(8,128)(2,1)S(1)}, bf16[256,2048]{1,0:T(8,128)(2,1)}, u32[]{:S(2)}) copy-start(bf16[256,2048]{1,0:T(8,128)(2,1)} %param.14) | copy-start | bytes 3145732
  1.7 5.2 %slice-start = ((bf16[3,256,512]{2,1,0:T(8,128)(2,1)}), bf16[1,256,512]{2,1,0:T(8,128)(2,1)S(1)}, s32[]{:S(2)}) async-start(bf16[3,256,512]{2,1,0:T(8,128)(2,1)} %param.11), calls=%async_computation.2 | async-start | bytes 524288 | tf_op jit(solution)/shard_map/slice | solution.py:173
  4.3 11.3 %copy-start.18 = (s32[4]{0:T(128)S(1)}, s32[4]{0:T(128)}, u32[]{:S(2)}) copy-start(s32[4]{0:T(128)} %constant.198) | copy-start | bytes 52
  4.3 11.3 %copy-start.17 = (s32[4]{0:T(128)S(1)}, s32[4]{0:T(128)}, u32[]{:S(2)}) copy-start(s32[4]{0:T(128)} %constant.199) | copy-start | bytes 52
  4.3 11.3 %copy-start.20 = (f32[256]{0:T(256)S(1)}, f32[256]{0:T(256)}, u32[]{:S(2)}) copy-start(f32[256]{0:T(256)} %param.15) | copy-start | bytes 3076
  5.9 12.0 %copy-start.2 = (bf16[256,512,1]{1,0,2:T(8,128)(2,1)S(1)}, bf16[256,512,1]{1,0,2:T(8,128)(2,1)}, u32[]{:S(2)}) copy-start(bf16[256,512,1]{1,0,2:T(8,128)(2,1)} %constant.200) | copy-start | bytes 786436
  5.9 12.2 %copy-start.1 = (bf16[256,512,1]{1,0,2:T(8,128)(2,1)S(1)}, bf16[256,512,1]{1,0,2:T(8,128)(2,1)}, u32[]{:S(2)}) copy-start(bf16[256,512,1]{1,0,2:T(8,128)(2,1)} %constant.201) | copy-start | bytes 786436
  7.8 23.1 %all-to-all-start = ((bf16[8,65,512]{2,1,0:T(8,128)(2,1)}), bf16[8,65,512]{2,1,0:T(8,128)(2,1)S(1)}, u32[]{:S(2)}, u32[]{:S(2)}) async-start(bf16[8,65,512]{2,1,0:T(8,128)(2,1)} %pad_maximum_fusion), calls=%async_computation | async-start | bytes 1179648 | tf_op jit(solution)/shard_map/all_to_all | solution.py:179
  38.3 0.9 %copy-start.10 = (f32[32]{0:T(128)S(1)}, f32[32]{0:T(128)}, u32[]{:S(2)}) copy-start(f32[32]{0:T(128)} %get-tuple-element.77) | copy-start | bytes 388
  38.3 0.9 %copy-start.11 = (f32[32]{0:T(128)S(1)}, f32[32]{0:T(128)}, u32[]{:S(2)}) copy-start(f32[32]{0:T(128)} %get-tuple-element.78) | copy-start | bytes 388
  38.3 0.9 %copy-start.12 = (f32[32]{0:T(128)S(1)}, f32[32]{0:T(128)}, u32[]{:S(2)}) copy-start(f32[32]{0:T(128)} %get-tuple-element.79) | copy-start | bytes 388
  38.3 0.9 %copy-start.13 = (f32[32]{0:T(128)S(1)}, f32[32]{0:T(128)}, u32[]{:S(2)}) copy-start(f32[32]{0:T(128)} %get-tuple-element.80) | copy-start | bytes 388
  38.3 0.9 %copy-start.14 = (f32[32]{0:T(128)S(1)}, f32[32]{0:T(128)}, u32[]{:S(2)}) copy-start(f32[32]{0:T(128)} %get-tuple-element.81) | copy-start | bytes 388
  38.4 0.9 %copy-start.15 = (f32[32]{0:T(128)S(1)}, f32[32]{0:T(128)}, u32[]{:S(2)}) copy-start(f32[32]{0:T(128)} %get-tuple-element.84) | copy-start | bytes 388
  39.6 0.8 %copy-start.5 = (f32[32,256]{1,0:T(8,128)S(1)}, f32[32,256]{1,0:T(8,128)}, u32[]{:S(2)}) copy-start(f32[32,256]{1,0:T(8,128)} %get-tuple-element.74) | copy-start | bytes 98308
  39.8 0.8 %copy-start.4 = (f32[32,256]{1,0:T(8,128)S(1)}, f32[32,256]{1,0:T(8,128)}, u32[]{:S(2)}) copy-start(f32[32,256]{1,0:T(8,128)} %get-tuple-element.75) | copy-start | bytes 98308
  40.1 0.7 %copy-start.9 = (pred[256]{0:T(512)(128)(4,1)S(1)}, pred[256]{0:T(512)(128)(4,1)}, u32[]{:S(2)}) copy-start(pred[256]{0:T(512)(128)(4,1)} %iota_compare_fusion.5) | copy-start | bytes 772
  40.7 1.0 %copy-start.3 = (f32[512,256,1]{1,0,2:T(8,128)S(1)}, f32[512,256,1]{1,0,2:T(8,128)}, u32[]{:S(2)}) copy-start(f32[512,256,1]{1,0,2:T(8,128)} %constant.202) | copy-start | bytes 1572868
  40.9 1.8 %copy-start.6 = (f32[32]{0:T(128)S(1)}, f32[32]{0:T(128)}, u32[]{:S(2)}) copy-start(f32[32]{0:T(128)} %get-tuple-element.76) | copy-start | bytes 388
  40.9 1.8 %copy-start.7 = (f32[32]{0:T(128)S(1)}, f32[32]{0:T(128)}, u32[]{:S(2)}) copy-start(f32[32]{0:T(128)} %get-tuple-element.82) | copy-start | bytes 388
  41.0 1.8 %copy-start.8 = (f32[32]{0:T(128)S(1)}, f32[32]{0:T(128)}, u32[]{:S(2)}) copy-start(f32[32]{0:T(128)} %get-tuple-element.83) | copy-start | bytes 388
  41.0 1.8 %copy-start.16 = (f32[32]{0:T(128)S(1)}, f32[32]{0:T(128)}, u32[]{:S(2)}) copy-start(f32[32]{0:T(128)} %dynamic_slice.11) | copy-start | bytes 388
  41.2 19.9 %copy-start.19 = (bf16[2048,1024]{1,0:T(8,128)(2,1)S(1)}, bf16[2048,1024]{1,0:T(8,128)(2,1)}, u32[]{:S(2)}) copy-start(bf16[2048,1024]{1,0:T(8,128)(2,1)} %param.16) | copy-start | bytes 12582916

commit v8 on v7

--- a/solution.py
+++ b/solution.py
@@ -1,3 +1,4 @@
+import functools
 import math
 
 import jax
@@ -5,12 +6,15 @@
 import ml_dtypes
 import numpy as np
 from jax import lax
+from jax.experimental import pallas as pl
+from jax.experimental.pallas import tpu as pltpu
 from jax.sharding import PartitionSpec as P
 
 T_DEV = 256
 HALF = T_DEV // 2
 PERIOD = 2 * T_DEV
 GROUP = 8
+EDGE = 128
 
 
 def split_bf16(table):
@@ -135,6 +139,42 @@
     return mixed.astype(jnp.bfloat16)
 
 
+def sender_kernel(count_ref, arrivals_ref, taps_ref, out_ref, *, n_ctx, own):
+    count = count_ref[0]
+    capacity = arrivals_ref.shape[2]
+    lane = lax.broadcasted_iota(jnp.int32, arrivals_ref.shape[1:], 1)
+    near = []
+    firsts = []
+    lasts = []
+    for part in range(2):
+        x = arrivals_ref[1 + part].astype(jnp.float32)
+        back1 = jnp.where(lane >= 1, pltpu.roll(x, 1, 1), 0.0)
+        back2 = jnp.where(lane >= 2, pltpu.roll(x, 2, 1), 0.0)
+        s = taps_ref[3 * part] * x
+        s = s + taps_ref[3 * part + 1] * back1
+        s = s + taps_ref[3 * part + 2] * back2
+        near.append(s)
+        firsts += [x[:, 0:1], x[:, 1:2]]
+        lasts += [
+            jnp.sum(jnp.where(lane == count - 2 + k, x, 0.0), axis=1, keepdims=True)
+            for k in range(2)
+        ]
+    mixed = (near[0] * near[1]).astype(jnp.bfloat16)
+    edge_lane = lax.broadcasted_iota(jnp.int32, (arrivals_ref.shape[1], EDGE), 1)
+    edge = jnp.zeros((arrivals_ref.shape[1], EDGE), jnp.float32)
+    for k, value in enumerate(firsts[:2] + firsts[2:] + lasts[:2] + lasts[2:]):
+        edge = jnp.where(edge_lane == k, value, edge)
+    edge = jnp.where(edge_lane == 8, (count // 16).astype(jnp.float32), edge)
+    edge = jnp.where(edge_lane == 9, (count % 16).astype(jnp.float32), edge)
+    edge = edge.astype(jnp.bfloat16)
+    for j in range(n_ctx):
+        rows = slice(j * own, (j + 1) * own)
+        out_ref[j, :own, :capacity] = arrivals_ref[0, rows, :]
+        out_ref[j, :own, capacity:] = jnp.zeros((own, EDGE), jnp.bfloat16)
+        out_ref[j, own:, :capacity] = mixed[rows]
+        out_ref[j, own:, capacity:] = edge[rows]
+
+
 def by_transpose(arrivals, counts, short_taps, filter_taps, skip_gain, out_weight):
     n_ctx = lax.axis_size("ctx")
     device = lax.axis_index("ctx")
@@ -145,43 +185,21 @@
     own = channels // n_ctx
     forward, inverse = dft_tables()
 
-    count = counts[0]
-    pair = arrivals[1:].astype(jnp.float32)
-    ahead = jnp.pad(pair, ((0, 0), (0, 0), (2, 0)))
-    near = short_taps[1:, 0, :, None] * ahead[:, :, 2:]
-    near = near + short_taps[1:, 1, :, None] * ahead[:, :, 1:-1]
-    near = near + short_taps[1:, 2, :, None] * ahead[:, :, :-2]
-    own_mixed = (near[0] * near[1]).astype(jnp.bfloat16)
-    row = jnp.arange(capacity, dtype=jnp.int32)
-    last = jnp.stack(
-        [jnp.sum(jnp.where(row == count - 2 + k, pair, 0.0), axis=2) for k in range(2)], axis=2
-    )
-    edge = jnp.concatenate(
-        [pair[0, :, :2], pair[1, :, :2], last[0], last[1]], axis=1
-    ).astype(jnp.bfloat16)
-    code = jnp.stack([count // 16, count % 16]).astype(jnp.bfloat16)
-    edge_row = jnp.concatenate(
-        [
-            edge.reshape(n_ctx, own * 8),
-            jnp.broadcast_to(code, (n_ctx, 2)),
-            jnp.zeros((n_ctx, capacity - own * 8 - 2), jnp.bfloat16),
+    tap_column = short_taps[1:].reshape(6, channels)[:, :, None]
+    payload = pl.pallas_call(
+        functools.partial(sender_kernel, n_ctx=n_ctx, own=own),
+        in_specs=[
+            pl.BlockSpec(memory_space=pltpu.SMEM),
+            pl.BlockSpec(memory_space=pltpu.VMEM),
+            pl.BlockSpec(memory_space=pltpu.VMEM),
         ],
-        axis=1,
-    )
-    payload = jnp.concatenate(
-        [
-            arrivals[0].reshape(n_ctx, own, capacity),
-            own_mixed.reshape(n_ctx, own, capacity),
-            edge_row[:, None, :],
-        ],
-        axis=1,
-    )
+        out_specs=pl.BlockSpec(memory_space=pltpu.VMEM),
+        out_shape=jax.ShapeDtypeStruct((n_ctx, 2 * own, capacity + EDGE), jnp.bfloat16),
+    )(counts, arrivals, tap_column)
     got = lax.all_to_all(payload, "ctx", 0, 0, tiled=False)
-    rows = got[:, : 2 * own]
-    edge_in = got[:, 2 * own]
-    every_count = (
-        edge_in[:, own * 8].astype(jnp.int32) * 16 + edge_in[:, own * 8 + 1].astype(jnp.int32)
-    )
+    rows = got[:, :, :capacity]
+    edge_in = got[:, own:, capacity:]
+    every_count = edge_in[:, 0, 8].astype(jnp.int32) * 16 + edge_in[:, 0, 9].astype(jnp.int32)
     offsets = jnp.cumsum(every_count) - every_count
 
     frame = 3 * T_DEV
@@ -202,7 +220,7 @@
     shorted_gate = shorted_gate + taps[0, 2, :, None] * gate[:, :-2]
     from_senders = full[own:, T_DEV : T_DEV + length]
 
-    values = edge_in[:, : own * 8].reshape(n_ctx, own, 8)
+    values = edge_in[:, :, :8]
     count_col = every_count[:, None]
     at_row = jnp.concatenate(
         [jnp.zeros_like(count_col), jnp.ones_like(count_col), count_col - 2, count_col - 1], axis=1
@@ -213,7 +231,9 @@
     marks = ((slot - 2 == spot[:, :, None]) & valid[:, :, None]).astype(jnp.bfloat16)
     near_in = []
     for part in range(2):
-        pick = values[:, :, jnp.array([2 * part, 2 * part + 1, 4 + 2 * part, 5 + 2 * part])]
+        pick = jnp.concatenate(
+            [values[:, :, 2 * part : 2 * part + 2], values[:, :, 4 + 2 * part : 6 + 2 * part]], axis=2
+        )
         around = jnp.einsum(
             "ics,isj->cj", pick, marks, preferred_element_type=jnp.float32
         )

time: 64.2 us -> 61.9 us (0.964)
  other arithmetic: 8.31 us -> 3.46 us
  waiting for transfers between devices: 11.8 us -> 15.5 us
  local copies, waits for them, and re-layouts: 8.99 us -> 5.59 us
  Pallas kernels: 0 us -> 3.24 us
    all_to_all x1, waiting for transfers between devices: 11.8 us -> 15.5 us  [by_transpose(): got = lax.all_to_all(payload, 'ctx', 0, 0, tiled=False)]
    pallas_call x0 -> x1, Pallas kernels: none -> 3.24 us  [by_transpose(): pl.pallas_call(functools.partial(sender_kernel, n_ctx=n_ctx, own=own), in...]
    another operation x0 -> x2, local copies, waits for them, and re-layouts: none -> 1.58 us  [the longest x1 1.5 us: by_transpose(): tap_column = short_taps[1:].reshape(6, channels)[:, :, None]]
    reduce_sum x1 -> x0, other arithmetic: 1.37 us -> none  [by_transpose(): jnp.sum(jnp.where(row == count - 2 + k, pair, 0.0), axis=2)]
    convert_element_type x2 -> x0, other arithmetic: 1.28 us -> none  [the longest x1 1.2 us: by_transpose(): pair = arrivals[1:].astype(jnp.float32)]
    gather x2 -> x0, local copies, waits for them, and re-layouts: 1.13 us -> none  [by_transpose(): values[:, :, jnp.array([2 * part, 2 * part + 1, 4 + 2 * part, 5 + 2 * par...]
    slice x7 -> x2, local copies, waits for them, and re-layouts: 1.74 us -> 0.82 us  [the longest x1 0.7 us: by_transpose(): tap_column = short_taps[1:].reshape(6, channels)[:, :, None]]
    concatenate x2 -> x0, other arithmetic: 0.91 us -> none  [the longest x1 0.88 us: by_transpose(): jnp.concatenate([arrivals[0].reshape(n_ctx, own, capacity), own_mixed.res...]
  transfers between devices with their start and end apart: 1 -> 1, of which waited for: 1 -> 1; matrix products, arithmetic and copies ran while one was open for 6% -> 3% of each run, Pallas kernels for 0% -> 0%
where the time goes in v8:
time: 61.9 us; the launch traced here: 61.6 us
  blocking collectives  18 us (29%)
  waiting for transfers between devices  15.5 us (25%)
  matrix products  7.42 us (12%)
  starting transfers between devices  7.26 us (12%)
  local copies, waits for them, and re-layouts  5.59 us (9%)
  other arithmetic  3.46 us (6%)
  Pallas kernels  3.24 us (5%)
  between operations  1.13 us (2%)
    all_to_all x1, waiting for transfers between devices, by_transpose(): got = lax.all_to_all(payload, 'ctx', 0, 0, tiled=False)  15.5 us
    all_to_all x1, blocking collectives, by_transpose(): lax.all_to_all(gated.reshape(own, n_ctx, T_DEV), 'ctx', 1, 0, tiled=False)  10.8 us
    all_to_all x1, starting transfers between devices, by_transpose(): got = lax.all_to_all(payload, 'ctx', 0, 0, tiled=False)  7.26 us
    all_gather x1, blocking collectives, by_transpose(): lax.all_gather(gated_block, 'ch', axis=0, tiled=True)  7.19 us
    dot_general x1, matrix products, by_transpose(): jnp.einsum('icr,irj->icj', rows, select, preferred_element_type=jnp.bfloa...  3.58 us
    pallas_call x1, Pallas kernels, by_transpose(): pl.pallas_call(functools.partial(sender_kernel, n_ctx=n_ctx, own=own), in...  3.24 us
    another operation x1, local copies, waits for them, and re-layouts, by_transpose(): tap_column = short_taps[1:].reshape(6, channels)[:, :, None]  1.5 us
    convert_element_type x1, local copies, waits for them, and re-layouts, by_transpose(): return mixed.astype(jnp.bfloat16)  1.31 us
  transfers between devices with their start and end apart: 1, of which 1 were waited for; matrix products, arithmetic and copies ran while one was open for 3% of the time, Pallas kernels for 0%

profile of v8, /device:TPU:0, one launch (start us, length us, event | category | flops | bytes accessed | tf_op | source)
XLA Modules:
  0.0 61.6 jit_solution(10341066357047767399)
XLA Ops:
  0.0 0.0 copy-start
  0.0 0.0 copy-start.2
  0.0 0.0 copy-start.1
  0.0 0.0 copy-start.5
  0.8 0.7 %slice.292 = f32[2,3,256]{2,1,0:T(4,128)S(1)} slice(f32[3,3,256]{2,1,0:T(4,128)} %param.11), slice={[1:3], [0:3], [0:256]} | slice | bytes 12288 | tf_op jit(solution)/shard_map/slice | solution.py:188
  1.5 1.5 %broadcast_in_dim_reshape.8.taps_ref = f32[6,256,1]{2,1,0:T(8,128)} reshape(f32[2,3,256]{2,1,0:T(4,128)S(1)} %slice.292) | data formatting | bytes 12288 | tf_op jit(solution)/shard_map/broadcast_in_dim;reshape | solution.py:188
  3.0 3.2 %shard_map.91 = bf16[8,64,640]{2,1,0:T(8,128)(2,1)} custom-call(s32[1]{0:T(128)S(6)} %copy.92.count_ref, bf16[3,256,512]{2,1,0:T(8,128)(2,1)} %arrivals_ref.1, f32[6,256,1]{2,1,0:T(8,128)} %broadcast_in_dim_reshape.8.taps_ref), custom_call_target="tpu_custom_call" | custom-call | tf_op jit(solution)/shard_map/pallas_call | solution.py:189
  6.2 7.3 %all-to-all-start = ((bf16[8,64,640]{2,1,0:T(8,128)(2,1)}), bf16[8,64,640]{2,1,0:T(8,128)(2,1)S(1)}, u32[]{:S(2)}, u32[]{:S(2)}) async-start(bf16[8,64,640]{2,1,0:T(8,128)(2,1)} %shard_map.91), calls=%async_computation | async-start | bytes 1310720 | tf_op jit(solution)/shard_map/all_to_all | solution.py:199
  13.5 0.0 copy-done
  13.6 0.9 %fusion.46 = (f32[32]{0:T(128)S(1)}, f32[32]{0:T(128)S(1)}, f32[32]{0:T(128)S(1)}, f32[32]{0:T(128)S(1)}, f32[32]{0:T(128)S(1)}, /*index=5*/f32[32]{0:T(128)S(1)}, f32[32]{0:T(128)S(1)}, f32[32]{0:T(128)S(1)}, f32[32]{0:T(128)S(1)}) fusion(f32[3,3,256]{2,1,0:T(4,128)} %param.11, s32[]{:T(128)S(6)} %select_n.43, s32[]{:T(128)S(6)} %add.405, s32[]{:T(128)S(6)} %add.404), kind=kLoop, calls=%fused_computation.146 | loop fusion | bytes 2316 | tf_op jit(solution)/shard_map/mul | solution.py:218
  14.5 0.1 pad_add_fusion.3
  14.6 0.0 copy-done.5
  14.6 0.1 dynamic_slice.11
  14.7 0.0 copy-done.2
  14.7 0.2 fusion.21
  14.9 0.0 copy-done.1
  14.9 0.2 convolution_add_fusion
  15.2 0.1 fusion.6
  15.3 15.5 %all-to-all-done = bf16[8,64,640]{2,1,0:T(8,128)(2,1)S(1)} async-done(((bf16[8,64,640]{2,1,0:T(8,128)(2,1)}), bf16[8,64,640]{2,1,0:T(8,128)(2,1)S(1)}, u32[]{:S(2)}, u32[]{:S(2)}) %all-to-all-start) | async-done | bytes 655392 | tf_op jit(solution)/shard_map/all_to_all | solution.py:199
  30.8 0.3 fusion.51
  31.1 0.1 iota_compare_fusion.1
  31.2 0.2 reduce-window.4
  31.4 0.1 copy.55
  31.5 0.1 copy.53
  31.6 0.5 add_reduce_fusion.1
  32.1 0.1 add_add_fusion
  32.2 0.1 copy.54
  32.3 0.1 iota_add_fusion
  32.3 0.2 compare_and_fusion
  32.5 0.2 convert_reduce_fusion
  32.7 3.6 %fusion.1 = bf16[8,64,768]{2,1,0:T(8,128)(2,1)S(1)} fusion(s32[8,512]{1,0:T(8,128)S(1)} %iota_add_fusion, pred[8,512]{1,0:T(8,128)(4,1)S(1)} %iota_compare_fusion.1, bf16[8,64,640]{2,1,0:T(8,128)(2,1)S(1)} %all-to-all-done), kind=kOutput, calls=%fused_computation.2 | convolution fusion | flops 408944640 | bytes 1331200 | tf_op jit(solution)/shard_map/icr,irj->icj/dot_general | solution.py:211
  36.3 0.1 slice_bitcast_fusion.7
  36.4 0.1 pad_add_fusion
  36.5 0.1 slice_convert_fusion.1
  36.6 0.1 fusion.53
  36.7 0.4 convolution_bitcast_fusion.1
  37.1 0.4 convolution_bitcast_fusion
  37.5 0.4 slice_select_fusion
  37.9 0.2 fusion.24
  38.1 0.2 convolution_add_fusion.1
  38.5 0.1 slice_multiply_fusion.20
  38.6 0.1 slice_multiply_fusion.16
  38.7 0.0 copy-start.3
  38.7 0.1 slice_multiply_fusion.12
  38.8 0.2 subtract_select_fusion
  39.0 0.0 copy-start.4
  39.0 0.2 add_select_fusion
  39.2 0.1 pad_maximum_fusion
  39.3 0.4 copy-done.3
  39.7 0.9 %fusion.8 = f32[32,8,256]{2,1,0:T(8,128)S(1)} fusion(f32[512,256,1]{1,0,2:T(8,128)S(1)} %copy-done.3, f32[32,8,512]{2,0,1:T(8,128)S(1)} %pad_maximum_fusion), kind=kOutput, calls=%fused_computation.15 | convolution fusion | flops 402653184 | bytes 1310720 | tf_op jit(solution)/shard_map/cnf,ft->cnt/dot_general | solution.py:275
  40.6 0.1 copy.72
  40.7 0.2 fusion.18
  41.0 10.8 %all_to_all.20 = bf16[1,32,8,256]{3,1,0,2:T(8,128)(2,1)S(1)} all-to-all(bf16[1,32,8,256]{3,1,0,2:T(8,128)(2,1)S(1)} %copy.63), channel_id=1, replica_groups=mesh['ctx'=8,'ch'=4] {'ctx'}, dimensions={2} | all-to-all | bytes 262144 | tf_op jit(solution)/shard_map/all_to_all | solution.py:279
  51.8 7.2 %all_gather.3 = bf16[1024,256]{1,0:T(8,128)(2,1)S(1)} all-gather(bf16[256,256]{1,0:T(8,128)(2,1)S(1)} %bitcast.117), channel_id=1, replica_groups=mesh['ctx'=8,'ch'=4] {'ch'}, dimensions={0}, use_global_device_ids=true | all-gather | bytes 655360 | tf_op jit(solution)/shard_map/all_gather | solution.py:283
  59.0 0.0 copy-done.4
  59.0 1.3 %fusion.5 = bf16[2048,256]{0,1:T(8,128)(2,1)S(1)} fusion(bf16[1024,256]{1,0:T(8,128)(2,1)S(1)} %all_gather.3, bf16[2048,1024]{1,0:T(8,128)(2,1)S(1)} %copy-done.4), kind=kOutput, calls=%fused_computation.8 | convolution fusion | flops 1074266112 | bytes 5767168 | tf_op jit(solution)/shard_map/dot_general | solution.py:281
  60.3 1.3 %copy.64 = bf16[2048,256]{1,0:T(8,128)(2,1)} copy(bf16[2048,256]{0,1:T(8,128)(2,1)S(1)} %fusion.5) | data formatting | bytes 2097152 | tf_op jit(solution)/shard_map/convert_element_type | solution.py:286
  (17 shorter events, 0.3 us)
Async XLA Ops:
  0.0 13.5 %copy-start = (bf16[256,2048]{1,0:T(8,128)(2,1)S(1)}, bf16[256,2048]{1,0:T(8,128)(2,1)}, u32[]{:S(2)}) copy-start(bf16[256,2048]{1,0:T(8,128)(2,1)} %param.12) | copy-start | bytes 3145732
  0.0 14.7 %copy-start.2 = (bf16[256,512,1]{1,0,2:T(8,128)(2,1)S(1)}, bf16[256,512,1]{1,0,2:T(8,128)(2,1)}, u32[]{:S(2)}) copy-start(bf16[256,512,1]{1,0,2:T(8,128)(2,1)} %constant.153) | copy-start | bytes 786436
  0.0 14.9 %copy-start.1 = (bf16[256,512,1]{1,0,2:T(8,128)(2,1)S(1)}, bf16[256,512,1]{1,0,2:T(8,128)(2,1)}, u32[]{:S(2)}) copy-start(bf16[256,512,1]{1,0,2:T(8,128)(2,1)} %constant.154) | copy-start | bytes 786436
  0.0 14.6 %copy-start.5 = (f32[256]{0:T(256)S(1)}, f32[256]{0:T(256)}, u32[]{:S(2)}) copy-start(f32[256]{0:T(256)} %param.13) | copy-start | bytes 3076
  6.2 24.6 %all-to-all-start = ((bf16[8,64,640]{2,1,0:T(8,128)(2,1)}), bf16[8,64,640]{2,1,0:T(8,128)(2,1)S(1)}, u32[]{:S(2)}, u32[]{:S(2)}) async-start(bf16[8,64,640]{2,1,0:T(8,128)(2,1)} %shard_map.91), calls=%async_computation | async-start | bytes 1310720 | tf_op jit(solution)/shard_map/all_to_all | solution.py:199
  38.7 1.0 %copy-start.3 = (f32[512,256,1]{1,0,2:T(8,128)S(1)}, f32[512,256,1]{1,0,2:T(8,128)}, u32[]{:S(2)}) copy-start(f32[512,256,1]{1,0,2:T(8,128)} %constant.155) | copy-start | bytes 1572868
  39.0 20.0 %copy-start.4 = (bf16[2048,1024]{1,0:T(8,128)(2,1)S(1)}, bf16[2048,1024]{1,0:T(8,128)(2,1)}, u32[]{:S(2)}) copy-start(bf16[2048,1024]{1,0:T(8,128)(2,1)} %param.14) | copy-start | bytes 12582916

commit v9 on v8

--- a/solution.py
+++ b/solution.py
@@ -143,29 +143,25 @@
     count = count_ref[0]
     capacity = arrivals_ref.shape[2]
     lane = lax.broadcasted_iota(jnp.int32, arrivals_ref.shape[1:], 1)
+    row = lax.broadcasted_iota(jnp.int32, (capacity, EDGE), 0)
+    column = lax.broadcasted_iota(jnp.int32, (capacity, EDGE), 1)
     near = []
-    firsts = []
-    lasts = []
+    edge = jnp.where(column[:1] == 8, (count // 16).astype(jnp.float32), 0.0)
+    edge = jnp.where(column[:1] == 9, (count % 16).astype(jnp.float32), edge)
     for part in range(2):
-        x = arrivals_ref[1 + part].astype(jnp.float32)
+        raw = arrivals_ref[1 + part]
+        x = raw.astype(jnp.float32)
         back1 = jnp.where(lane >= 1, pltpu.roll(x, 1, 1), 0.0)
         back2 = jnp.where(lane >= 2, pltpu.roll(x, 2, 1), 0.0)
-        s = taps_ref[3 * part] * x
-        s = s + taps_ref[3 * part + 1] * back1
-        s = s + taps_ref[3 * part + 2] * back2
+        s = taps_ref[:, 3 * part : 3 * part + 1] * x
+        s = s + taps_ref[:, 3 * part + 1 : 3 * part + 2] * back1
+        s = s + taps_ref[:, 3 * part + 2 : 3 * part + 3] * back2
         near.append(s)
-        firsts += [x[:, 0:1], x[:, 1:2]]
-        lasts += [
-            jnp.sum(jnp.where(lane == count - 2 + k, x, 0.0), axis=1, keepdims=True)
-            for k in range(2)
-        ]
+        wanted = jnp.where(column >= 4, count - 2 + column - 4 - 2 * part, column - 2 * part)
+        inside = (column % 4 >= 2 * part) & (column % 4 < 2 * part + 2) & (column < 8)
+        pick = ((row == wanted) & inside).astype(jnp.bfloat16)
+        edge = edge + jnp.dot(raw, pick, preferred_element_type=jnp.float32)
     mixed = (near[0] * near[1]).astype(jnp.bfloat16)
-    edge_lane = lax.broadcasted_iota(jnp.int32, (arrivals_ref.shape[1], EDGE), 1)
-    edge = jnp.zeros((arrivals_ref.shape[1], EDGE), jnp.float32)
-    for k, value in enumerate(firsts[:2] + firsts[2:] + lasts[:2] + lasts[2:]):
-        edge = jnp.where(edge_lane == k, value, edge)
-    edge = jnp.where(edge_lane == 8, (count // 16).astype(jnp.float32), edge)
-    edge = jnp.where(edge_lane == 9, (count % 16).astype(jnp.float32), edge)
     edge = edge.astype(jnp.bfloat16)
     for j in range(n_ctx):
         rows = slice(j * own, (j + 1) * own)
@@ -185,7 +181,7 @@
     own = channels // n_ctx
     forward, inverse = dft_tables()
 
-    tap_column = short_taps[1:].reshape(6, channels)[:, :, None]
+    tap_column = short_taps[1:].reshape(6, channels).T
     payload = pl.pallas_call(
         functools.partial(sender_kernel, n_ctx=n_ctx, own=own),
         in_specs=[

time: 61.9 us -> 60.8 us (0.982)
  waiting for transfers between devices: 15.5 us -> 13.9 us
  matrix products: 7.42 us -> 8.38 us
    all_to_all x1, waiting for transfers between devices: 15.5 us -> 13.9 us  [by_transpose(): got = lax.all_to_all(payload, 'ctx', 0, 0, tiled=False)]
    another operation x2 -> x1, local copies, waits for them, and re-layouts: 1.58 us -> 0.08 us  [the longest x1 1.5 us: by_transpose(): tap_column = short_taps[1:].reshape(6, channels)[:, :, None]]
    dot_general x2, matrix products: 0.44 us -> 1.4 us  [transform(): jnp.einsum(spec, blocks, hi, preferred_element_type=jnp.float32)]
    reshape x0 -> x2, local copies, waits for them, and re-layouts: none -> 0.8 us  [by_transpose(): tap_column = short_taps[1:].reshape(6, channels).T]
    dynamic_slice x1, local copies, waits for them, and re-layouts: 0.07 us -> 0.76 us  [by_transpose(): gains = lax.dynamic_slice_in_dim(skip_gain, first, own, 0)]
  transfers between devices with their start and end apart: 1 -> 1, of which waited for: 1 -> 1; matrix products, arithmetic and copies ran while one was open for 3% -> 5% of each run, Pallas kernels for 0% -> 0%
where the time goes in v9:
time: 60.8 us; the launch traced here: 60.5 us
  blocking collectives  18 us (30%)
  waiting for transfers between devices  13.9 us (23%)
  matrix products  8.38 us (14%)
  starting transfers between devices  7.25 us (12%)
  local copies, waits for them, and re-layouts  5.58 us (9%)
  other arithmetic  3.46 us (6%)
  Pallas kernels  2.83 us (5%)
  between operations  1.11 us (2%)
    all_to_all x1, waiting for transfers between devices, by_transpose(): got = lax.all_to_all(payload, 'ctx', 0, 0, tiled=False)  13.9 us
    all_to_all x1, blocking collectives, by_transpose(): lax.all_to_all(gated.reshape(own, n_ctx, T_DEV), 'ctx', 1, 0, tiled=False)  10.8 us
    all_to_all x1, starting transfers between devices, by_transpose(): got = lax.all_to_all(payload, 'ctx', 0, 0, tiled=False)  7.25 us
    all_gather x1, blocking collectives, by_transpose(): lax.all_gather(gated_block, 'ch', axis=0, tiled=True)  7.19 us
    dot_general x1, matrix products, by_transpose(): jnp.einsum('icr,irj->icj', rows, select, preferred_element_type=jnp.bfloa...  3.58 us
    pallas_call x1, Pallas kernels, by_transpose(): pl.pallas_call(functools.partial(sender_kernel, n_ctx=n_ctx, own=own), in...  2.83 us
    dot_general x2, matrix products, transform(): jnp.einsum(spec, blocks, hi, preferred_element_type=jnp.float32)  1.4 us
    convert_element_type x1, local copies, waits for them, and re-layouts, by_transpose(): return mixed.astype(jnp.bfloat16)  1.31 us
  transfers between devices with their start and end apart: 1, of which 1 were waited for; matrix products, arithmetic and copies ran while one was open for 5% of the time, Pallas kernels for 0%

profile of v9, /device:TPU:0, one launch (start us, length us, event | category | flops | bytes accessed | tf_op | source)
XLA Modules:
  0.0 60.5 jit_solution(12334153300425785447)
XLA Ops:
  0.0 0.0 copy-start
  0.0 0.0 copy-start.1
  0.8 0.7 %slice.292 = f32[2,3,256]{2,1,0:T(4,128)S(1)} slice(f32[3,3,256]{2,1,0:T(4,128)} %param.11), slice={[1:3], [0:3], [0:256]} | slice | bytes 12288 | tf_op jit(solution)/shard_map/slice | solution.py:184
  1.5 0.8 %copy.53 = f32[6,256]{0,1:T(8,128)} copy(f32[6,256]{1,0:T(8,128)S(1)} %reshape.242) | data formatting | bytes 12288 | tf_op jit(solution)/shard_map/reshape | solution.py:184
  2.3 2.8 %shard_map.91 = bf16[8,64,640]{2,1,0:T(8,128)(2,1)} custom-call(s32[1]{0:T(128)S(6)} %copy.93.count_ref, bf16[3,256,512]{2,1,0:T(8,128)(2,1)} %arrivals_ref.1, f32[256,6]{1,0:T(8,128)} %bitcast.118), custom_call_target="tpu_custom_call" | custom-call | tf_op jit(solution)/shard_map/pallas_call | solution.py:185
  5.1 7.3 %all-to-all-start = ((bf16[8,64,640]{2,1,0:T(8,128)(2,1)}), bf16[8,64,640]{2,1,0:T(8,128)(2,1)S(1)}, u32[]{:S(2)}, u32[]{:S(2)}) async-start(bf16[8,64,640]{2,1,0:T(8,128)(2,1)} %shard_map.91), calls=%async_computation | async-start | bytes 1310720 | tf_op jit(solution)/shard_map/all_to_all | solution.py:195
  12.4 0.0 copy-done
  12.4 0.9 %fusion.46 = (f32[32]{0:T(128)S(1)}, f32[32]{0:T(128)S(1)}, f32[32]{0:T(128)S(1)}, f32[32]{0:T(128)S(1)}, f32[32]{0:T(128)S(1)}, /*index=5*/f32[32]{0:T(128)S(1)}, f32[32]{0:T(128)S(1)}, f32[32]{0:T(128)S(1)}, f32[32]{0:T(128)S(1)}) fusion(f32[3,3,256]{2,1,0:T(4,128)} %param.11, s32[]{:T(128)S(6)} %select_n.43, s32[]{:T(128)S(6)} %add.405, s32[]{:T(128)S(6)} %add.404), kind=kLoop, calls=%fused_computation.146 | loop fusion | bytes 2316 | tf_op jit(solution)/shard_map/mul | solution.py:214
  13.3 0.1 pad_add_fusion.3
  13.4 0.8 %dynamic_slice.11 = f32[32]{0:T(128)S(1)} dynamic-slice(f32[256]{0:T(256)} %param.13, s32[]{:T(128)S(6)} %select_n.43), dynamic_slice_sizes={32} | dynamic-slice | bytes 260 | tf_op jit(solution)/shard_map/dynamic_slice | solution.py:272
  14.2 1.2 %fusion.21 = f32[32,9,512]{2,0,1:T(8,128)S(1)} fusion(bf16[256,512,1]{1,0,2:T(8,128)(2,1)} %constant.153, bf16[4,9,8,256]{3,2,1,0:T(8,128)(2,1)S(1)} %bitcast.113), kind=kOutput, calls=%fused_computation.55 | convolution fusion | flops 75497472 | bytes 999424 | tf_op jit(solution)/shard_map/cnt,tf->cnf/dot_general | solution.py:45
  15.4 0.0 copy-done.1
  15.4 0.2 convolution_add_fusion
  15.6 0.1 fusion.6
  15.7 13.9 %all-to-all-done = bf16[8,64,640]{2,1,0:T(8,128)(2,1)S(1)} async-done(((bf16[8,64,640]{2,1,0:T(8,128)(2,1)}), bf16[8,64,640]{2,1,0:T(8,128)(2,1)S(1)}, u32[]{:S(2)}, u32[]{:S(2)}) %all-to-all-start) | async-done | bytes 655392 | tf_op jit(solution)/shard_map/all_to_all | solution.py:195
  29.6 0.3 fusion.51
  30.0 0.1 iota_compare_fusion.1
  30.0 0.2 reduce-window.4
  30.3 0.1 copy.56
  30.4 0.1 copy.54
  30.4 0.5 add_reduce_fusion.1
  31.0 0.1 add_add_fusion
  31.0 0.1 copy.55
  31.1 0.1 iota_add_fusion
  31.2 0.2 compare_and_fusion
  31.4 0.2 convert_reduce_fusion
  31.6 3.6 %fusion.1 = bf16[8,64,768]{2,1,0:T(8,128)(2,1)S(1)} fusion(s32[8,512]{1,0:T(8,128)S(1)} %iota_add_fusion, pred[8,512]{1,0:T(8,128)(4,1)S(1)} %iota_compare_fusion.1, bf16[8,64,640]{2,1,0:T(8,128)(2,1)S(1)} %all-to-all-done), kind=kOutput, calls=%fused_computation.2 | convolution fusion | flops 408944640 | bytes 1331200 | tf_op jit(solution)/shard_map/icr,irj->icj/dot_general | solution.py:207
  35.2 0.0 copy-start.2
  35.2 0.1 slice_bitcast_fusion.7
  35.3 0.1 pad_add_fusion
  35.4 0.1 slice_convert_fusion.1
  35.5 0.1 fusion.53
  35.6 0.4 convolution_bitcast_fusion.1
  36.0 0.4 convolution_bitcast_fusion
  36.4 0.4 slice_select_fusion
  36.8 0.0 copy-done.2
  36.8 0.2 fusion.24
  37.0 0.2 convolution_add_fusion.1
  37.4 0.1 slice_multiply_fusion.20
  37.5 0.1 slice_multiply_fusion.16
  37.6 0.0 copy-start.3
  37.6 0.1 slice_multiply_fusion.12
  37.7 0.2 subtract_select_fusion
  37.9 0.0 copy-start.4
  37.9 0.2 add_select_fusion
  38.1 0.1 pad_maximum_fusion
  38.2 0.4 copy-done.3
  38.6 0.9 %fusion.8 = f32[32,8,256]{2,1,0:T(8,128)S(1)} fusion(f32[512,256,1]{1,0,2:T(8,128)S(1)} %copy-done.3, f32[32,8,512]{2,0,1:T(8,128)S(1)} %pad_maximum_fusion), kind=kOutput, calls=%fused_computation.15 | convolution fusion | flops 402653184 | bytes 1310720 | tf_op jit(solution)/shard_map/cnf,ft->cnt/dot_general | solution.py:271
  39.5 0.1 copy.73
  39.6 0.2 fusion.18
  39.9 10.8 %all_to_all.20 = bf16[1,32,8,256]{3,1,0,2:T(8,128)(2,1)S(1)} all-to-all(bf16[1,32,8,256]{3,1,0,2:T(8,128)(2,1)S(1)} %copy.64), channel_id=1, replica_groups=mesh['ctx'=8,'ch'=4] {'ctx'}, dimensions={2} | all-to-all | bytes 262144 | tf_op jit(solution)/shard_map/all_to_all | solution.py:275
  50.7 7.2 %all_gather.3 = bf16[1024,256]{1,0:T(8,128)(2,1)S(1)} all-gather(bf16[256,256]{1,0:T(8,128)(2,1)S(1)} %bitcast.119), channel_id=1, replica_groups=mesh['ctx'=8,'ch'=4] {'ch'}, dimensions={0}, use_global_device_ids=true | all-gather | bytes 655360 | tf_op jit(solution)/shard_map/all_gather | solution.py:279
  57.9 0.0 copy-done.4
  57.9 1.3 %fusion.5 = bf16[2048,256]{0,1:T(8,128)(2,1)S(1)} fusion(bf16[1024,256]{1,0:T(8,128)(2,1)S(1)} %all_gather.3, bf16[2048,1024]{1,0:T(8,128)(2,1)S(1)} %copy-done.4), kind=kOutput, calls=%fused_computation.8 | convolution fusion | flops 1074266112 | bytes 5767168 | tf_op jit(solution)/shard_map/dot_general | solution.py:277
  59.2 1.3 %copy.65 = bf16[2048,256]{1,0:T(8,128)(2,1)} copy(bf16[2048,256]{0,1:T(8,128)(2,1)S(1)} %fusion.5) | data formatting | bytes 2097152 | tf_op jit(solution)/shard_map/convert_element_type | solution.py:282
  (18 shorter events, 0.3 us)
Async XLA Ops:
  0.0 12.4 %copy-start = (bf16[256,2048]{1,0:T(8,128)(2,1)S(1)}, bf16[256,2048]{1,0:T(8,128)(2,1)}, u32[]{:S(2)}) copy-start(bf16[256,2048]{1,0:T(8,128)(2,1)} %param.12) | copy-start | bytes 3145732
  0.0 15.4 %copy-start.1 = (bf16[256,512,1]{1,0,2:T(8,128)(2,1)S(1)}, bf16[256,512,1]{1,0,2:T(8,128)(2,1)}, u32[]{:S(2)}) copy-start(bf16[256,512,1]{1,0,2:T(8,128)(2,1)} %constant.154) | copy-start | bytes 786436
  5.1 24.6 %all-to-all-start = ((bf16[8,64,640]{2,1,0:T(8,128)(2,1)}), bf16[8,64,640]{2,1,0:T(8,128)(2,1)S(1)}, u32[]{:S(2)}, u32[]{:S(2)}) async-start(bf16[8,64,640]{2,1,0:T(8,128)(2,1)} %shard_map.91), calls=%async_computation | async-start | bytes 1310720 | tf_op jit(solution)/shard_map/all_to_all | solution.py:195
  35.2 1.6 %copy-start.2 = (bf16[256,512,1]{1,0,2:T(8,128)(2,1)S(1)}, bf16[256,512,1]{1,0,2:T(8,128)(2,1)}, u32[]{:S(2)}) copy-start(bf16[256,512,1]{1,0,2:T(8,128)(2,1)} %constant.153) | copy-start | bytes 786436
  37.6 1.0 %copy-start.3 = (f32[512,256,1]{1,0,2:T(8,128)S(1)}, f32[512,256,1]{1,0,2:T(8,128)}, u32[]{:S(2)}) copy-start(f32[512,256,1]{1,0,2:T(8,128)} %constant.155) | copy-start | bytes 1572868
  37.9 20.0 %copy-start.4 = (bf16[2048,1024]{1,0:T(8,128)(2,1)S(1)}, bf16[2048,1024]{1,0:T(8,128)(2,1)}, u32[]{:S(2)}) copy-start(bf16[2048,1024]{1,0:T(8,128)(2,1)} %param.14) | copy-start | bytes 12582916

commit v10 on v9

--- a/solution.py
+++ b/solution.py
@@ -145,6 +145,13 @@
     lane = lax.broadcasted_iota(jnp.int32, arrivals_ref.shape[1:], 1)
     row = lax.broadcasted_iota(jnp.int32, (capacity, EDGE), 0)
     column = lax.broadcasted_iota(jnp.int32, (capacity, EDGE), 1)
+    square = lax.broadcasted_iota(jnp.int32, (lane.shape[0], lane.shape[0]), 0)
+    diagonal = square == lax.broadcasted_iota(jnp.int32, square.shape, 1)
+
+    def tap(part, k):
+        spread = jnp.where(diagonal, taps_ref[part, k : k + 1, :], 0.0)
+        return jnp.sum(spread, axis=1, keepdims=True)
+
     near = []
     edge = jnp.where(column[:1] == 8, (count // 16).astype(jnp.float32), 0.0)
     edge = jnp.where(column[:1] == 9, (count % 16).astype(jnp.float32), edge)
@@ -153,9 +160,9 @@
         x = raw.astype(jnp.float32)
         back1 = jnp.where(lane >= 1, pltpu.roll(x, 1, 1), 0.0)
         back2 = jnp.where(lane >= 2, pltpu.roll(x, 2, 1), 0.0)
-        s = taps_ref[:, 3 * part : 3 * part + 1] * x
-        s = s + taps_ref[:, 3 * part + 1 : 3 * part + 2] * back1
-        s = s + taps_ref[:, 3 * part + 2 : 3 * part + 3] * back2
+        s = tap(1 + part, 0) * x
+        s = s + tap(1 + part, 1) * back1
+        s = s + tap(1 + part, 2) * back2
         near.append(s)
         wanted = jnp.where(column >= 4, count - 2 + column - 4 - 2 * part, column - 2 * part)
         inside = (column % 4 >= 2 * part) & (column % 4 < 2 * part + 2) & (column < 8)
@@ -181,7 +188,6 @@
     own = channels // n_ctx
     forward, inverse = dft_tables()
 
-    tap_column = short_taps[1:].reshape(6, channels).T
     payload = pl.pallas_call(
         functools.partial(sender_kernel, n_ctx=n_ctx, own=own),
         in_specs=[
@@ -191,7 +197,7 @@
         ],
         out_specs=pl.BlockSpec(memory_space=pltpu.VMEM),
         out_shape=jax.ShapeDtypeStruct((n_ctx, 2 * own, capacity + EDGE), jnp.bfloat16),
-    )(counts, arrivals, tap_column)
+    )(counts, arrivals, short_taps)
     got = lax.all_to_all(payload, "ctx", 0, 0, tiled=False)
     rows = got[:, :, :capacity]
     edge_in = got[:, own:, capacity:]

time: 60.8 us -> 59.4 us (0.977)
  local copies, waits for them, and re-layouts: 5.58 us -> 4.07 us
    reshape x2 -> x0, local copies, waits for them, and re-layouts: 0.8 us -> none  [by_transpose(): tap_column = short_taps[1:].reshape(6, channels).T]
    slice x1 -> x0, local copies, waits for them, and re-layouts: 0.7 us -> none  [by_transpose(): tap_column = short_taps[1:].reshape(6, channels).T]
  transfers between devices with their start and end apart: 1 -> 1, of which waited for: 1 -> 1; matrix products, arithmetic and copies ran while one was open for 5% -> 6% of each run, Pallas kernels for 0% -> 0%
where the time goes in v10:
time: 59.4 us; the launch traced here: 59.1 us
  blocking collectives  18 us (30%)
  waiting for transfers between devices  13.9 us (23%)
  matrix products  8.4 us (14%)
  starting transfers between devices  7.25 us (12%)
  local copies, waits for them, and re-layouts  4.07 us (7%)
  other arithmetic  3.46 us (6%)
  Pallas kernels  2.95 us (5%)
  between operations  1.1 us (2%)
    all_to_all x1, waiting for transfers between devices, by_transpose(): got = lax.all_to_all(payload, 'ctx', 0, 0, tiled=False)  13.9 us
    all_to_all x1, blocking collectives, by_transpose(): lax.all_to_all(gated.reshape(own, n_ctx, T_DEV), 'ctx', 1, 0, tiled=False)  10.8 us
    all_to_all x1, starting transfers between devices, by_transpose(): got = lax.all_to_all(payload, 'ctx', 0, 0, tiled=False)  7.25 us
    all_gather x1, blocking collectives, by_transpose(): lax.all_gather(gated_block, 'ch', axis=0, tiled=True)  7.18 us
    dot_general x1, matrix products, by_transpose(): jnp.einsum('icr,irj->icj', rows, select, preferred_element_type=jnp.bfloa...  3.58 us
    pallas_call x1, Pallas kernels, by_transpose(): pl.pallas_call(functools.partial(sender_kernel, n_ctx=n_ctx, own=own), in...  2.95 us
    dot_general x2, matrix products, transform(): jnp.einsum(spec, blocks, hi, preferred_element_type=jnp.float32)  1.41 us
    convert_element_type x1, local copies, waits for them, and re-layouts, by_transpose(): return mixed.astype(jnp.bfloat16)  1.31 us
  transfers between devices with their start and end apart: 1, of which 1 were waited for; matrix products, arithmetic and copies ran while one was open for 6% of the time, Pallas kernels for 0%

profile of v10, /device:TPU:0, one launch (start us, length us, event | category | flops | bytes accessed | tf_op | source)
XLA Modules:
  0.0 59.1 jit_solution(7677699919350116965)
XLA Ops:
  0.0 0.0 copy-start
  0.0 0.0 copy-start.1
  0.8 2.9 %shard_map.91 = bf16[8,64,640]{2,1,0:T(8,128)(2,1)} custom-call(s32[1]{0:T(128)S(6)} %copy.88.count_ref, bf16[3,256,512]{2,1,0:T(8,128)(2,1)} %arrivals_ref.1, f32[3,3,256]{2,1,0:T(4,128)} %taps_ref.1), custom_call_target="tpu_custom_call" | custom-call | tf_op jit(solution)/shard_map/pallas_call | solution.py:191
  3.7 7.3 %all-to-all-start = ((bf16[8,64,640]{2,1,0:T(8,128)(2,1)}), bf16[8,64,640]{2,1,0:T(8,128)(2,1)S(1)}, u32[]{:S(2)}, u32[]{:S(2)}) async-start(bf16[8,64,640]{2,1,0:T(8,128)(2,1)} %shard_map.91), calls=%async_computation | async-start | bytes 1310720 | tf_op jit(solution)/shard_map/all_to_all | solution.py:201
  11.0 0.0 copy-done
  11.0 0.9 %fusion.46 = (f32[32]{0:T(128)S(1)}, f32[32]{0:T(128)S(1)}, f32[32]{0:T(128)S(1)}, f32[32]{0:T(128)S(1)}, f32[32]{0:T(128)S(1)}, /*index=5*/f32[32]{0:T(128)S(1)}, f32[32]{0:T(128)S(1)}, f32[32]{0:T(128)S(1)}, f32[32]{0:T(128)S(1)}) fusion(f32[3,3,256]{2,1,0:T(4,128)} %taps_ref.1, s32[]{:T(128)S(6)} %select_n.43, s32[]{:T(128)S(6)} %add.405, s32[]{:T(128)S(6)} %add.404), kind=kLoop, calls=%fused_computation.146 | loop fusion | bytes 2316 | tf_op jit(solution)/shard_map/mul | solution.py:220
  11.9 0.1 pad_add_fusion.3
  12.0 0.8 %dynamic_slice.11 = f32[32]{0:T(128)S(1)} dynamic-slice(f32[256]{0:T(256)} %param.13, s32[]{:T(128)S(6)} %select_n.43), dynamic_slice_sizes={32} | dynamic-slice | bytes 260 | tf_op jit(solution)/shard_map/dynamic_slice | solution.py:278
  12.8 1.2 %fusion.21 = f32[32,9,512]{2,0,1:T(8,128)S(1)} fusion(bf16[256,512,1]{1,0,2:T(8,128)(2,1)} %constant.153, bf16[4,9,8,256]{3,2,1,0:T(8,128)(2,1)S(1)} %bitcast.112), kind=kOutput, calls=%fused_computation.55 | convolution fusion | flops 75497472 | bytes 999424 | tf_op jit(solution)/shard_map/cnt,tf->cnf/dot_general | solution.py:45
  14.0 0.0 copy-done.1
  14.0 0.2 convolution_add_fusion
  14.3 0.1 fusion.6
  14.3 13.9 %all-to-all-done = bf16[8,64,640]{2,1,0:T(8,128)(2,1)S(1)} async-done(((bf16[8,64,640]{2,1,0:T(8,128)(2,1)}), bf16[8,64,640]{2,1,0:T(8,128)(2,1)S(1)}, u32[]{:S(2)}, u32[]{:S(2)}) %all-to-all-start) | async-done | bytes 655392 | tf_op jit(solution)/shard_map/all_to_all | solution.py:201
  28.3 0.3 fusion.51
  28.6 0.1 iota_compare_fusion.1
  28.7 0.2 reduce-window.4
  28.9 0.1 copy.51
  29.0 0.1 copy.49
  29.1 0.5 add_reduce_fusion.1
  29.6 0.1 add_add_fusion
  29.6 0.1 copy.50
  29.7 0.1 iota_add_fusion
  29.8 0.2 compare_and_fusion
  30.0 0.2 convert_reduce_fusion
  30.2 3.6 %fusion.1 = bf16[8,64,768]{2,1,0:T(8,128)(2,1)S(1)} fusion(s32[8,512]{1,0:T(8,128)S(1)} %iota_add_fusion, pred[8,512]{1,0:T(8,128)(4,1)S(1)} %iota_compare_fusion.1, bf16[8,64,640]{2,1,0:T(8,128)(2,1)S(1)} %all-to-all-done), kind=kOutput, calls=%fused_computation.2 | convolution fusion | flops 408944640 | bytes 1331200 | tf_op jit(solution)/shard_map/icr,irj->icj/dot_general | solution.py:213
  33.8 0.0 copy-start.2
  33.8 0.1 slice_bitcast_fusion.7
  33.9 0.1 pad_add_fusion
  34.0 0.1 slice_convert_fusion.1
  34.1 0.1 fusion.53
  34.2 0.4 convolution_bitcast_fusion.1
  34.6 0.4 convolution_bitcast_fusion
  35.0 0.4 slice_select_fusion
  35.4 0.0 copy-done.2
  35.4 0.2 fusion.24
  35.6 0.2 convolution_add_fusion.1
  36.0 0.1 slice_multiply_fusion.20
  36.1 0.1 slice_multiply_fusion.16
  36.2 0.0 copy-start.3
  36.2 0.1 slice_multiply_fusion.12
  36.3 0.2 subtract_select_fusion
  36.5 0.0 copy-start.4
  36.5 0.2 add_select_fusion
  36.7 0.1 pad_maximum_fusion
  36.8 0.4 copy-done.3
  37.2 0.9 %fusion.8 = f32[32,8,256]{2,1,0:T(8,128)S(1)} fusion(f32[512,256,1]{1,0,2:T(8,128)S(1)} %copy-done.3, f32[32,8,512]{2,0,1:T(8,128)S(1)} %pad_maximum_fusion), kind=kOutput, calls=%fused_computation.15 | convolution fusion | flops 402653184 | bytes 1310720 | tf_op jit(solution)/shard_map/cnf,ft->cnt/dot_general | solution.py:277
  38.1 0.1 copy.68
  38.2 0.2 fusion.18
  38.5 10.8 %all_to_all.20 = bf16[1,32,8,256]{3,1,0,2:T(8,128)(2,1)S(1)} all-to-all(bf16[1,32,8,256]{3,1,0,2:T(8,128)(2,1)S(1)} %copy.59), channel_id=1, replica_groups=mesh['ctx'=8,'ch'=4] {'ctx'}, dimensions={2} | all-to-all | bytes 262144 | tf_op jit(solution)/shard_map/all_to_all | solution.py:281
  49.3 7.2 %all_gather.3 = bf16[1024,256]{1,0:T(8,128)(2,1)S(1)} all-gather(bf16[256,256]{1,0:T(8,128)(2,1)S(1)} %bitcast.117), channel_id=1, replica_groups=mesh['ctx'=8,'ch'=4] {'ch'}, dimensions={0}, use_global_device_ids=true | all-gather | bytes 655360 | tf_op jit(solution)/shard_map/all_gather | solution.py:285
  56.5 0.0 copy-done.4
  56.5 1.3 %fusion.5 = bf16[2048,256]{0,1:T(8,128)(2,1)S(1)} fusion(bf16[1024,256]{1,0:T(8,128)(2,1)S(1)} %all_gather.3, bf16[2048,1024]{1,0:T(8,128)(2,1)S(1)} %copy-done.4), kind=kOutput, calls=%fused_computation.8 | convolution fusion | flops 1074266112 | bytes 5767168 | tf_op jit(solution)/shard_map/dot_general | solution.py:283
  57.8 1.3 %copy.60 = bf16[2048,256]{1,0:T(8,128)(2,1)} copy(bf16[2048,256]{0,1:T(8,128)(2,1)S(1)} %fusion.5) | data formatting | bytes 2097152 | tf_op jit(solution)/shard_map/convert_element_type | solution.py:288
  (17 shorter events, 0.3 us)
Async XLA Ops:
  0.0 11.0 %copy-start = (bf16[256,2048]{1,0:T(8,128)(2,1)S(1)}, bf16[256,2048]{1,0:T(8,128)(2,1)}, u32[]{:S(2)}) copy-start(bf16[256,2048]{1,0:T(8,128)(2,1)} %param.12) | copy-start | bytes 3145732
  0.0 14.0 %copy-start.1 = (bf16[256,512,1]{1,0,2:T(8,128)(2,1)S(1)}, bf16[256,512,1]{1,0,2:T(8,128)(2,1)}, u32[]{:S(2)}) copy-start(bf16[256,512,1]{1,0,2:T(8,128)(2,1)} %constant.154) | copy-start | bytes 786436
  3.7 24.5 %all-to-all-start = ((bf16[8,64,640]{2,1,0:T(8,128)(2,1)}), bf16[8,64,640]{2,1,0:T(8,128)(2,1)S(1)}, u32[]{:S(2)}, u32[]{:S(2)}) async-start(bf16[8,64,640]{2,1,0:T(8,128)(2,1)} %shard_map.91), calls=%async_computation | async-start | bytes 1310720 | tf_op jit(solution)/shard_map/all_to_all | solution.py:201
  33.8 1.6 %copy-start.2 = (bf16[256,512,1]{1,0,2:T(8,128)(2,1)S(1)}, bf16[256,512,1]{1,0,2:T(8,128)(2,1)}, u32[]{:S(2)}) copy-start(bf16[256,512,1]{1,0,2:T(8,128)(2,1)} %constant.153) | copy-start | bytes 786436
  36.2 1.0 %copy-start.3 = (f32[512,256,1]{1,0,2:T(8,128)S(1)}, f32[512,256,1]{1,0,2:T(8,128)}, u32[]{:S(2)}) copy-start(f32[512,256,1]{1,0,2:T(8,128)} %constant.155) | copy-start | bytes 1572868
  36.5 20.0 %copy-start.4 = (bf16[2048,1024]{1,0:T(8,128)(2,1)S(1)}, bf16[2048,1024]{1,0:T(8,128)(2,1)}, u32[]{:S(2)}) copy-start(bf16[2048,1024]{1,0:T(8,128)(2,1)} %param.14) | copy-start | bytes 12582916

commit v11 on v10

--- a/solution.py
+++ b/solution.py
@@ -170,12 +170,21 @@
         edge = edge + jnp.dot(raw, pick, preferred_element_type=jnp.float32)
     mixed = (near[0] * near[1]).astype(jnp.bfloat16)
     edge = edge.astype(jnp.bfloat16)
+    flat_lane = lax.broadcasted_iota(jnp.int32, (EDGE, capacity), 1)
+    spread = (
+        (flat_lane < 8 * own) & (flat_lane % 8 == lax.broadcasted_iota(jnp.int32, (EDGE, capacity), 0))
+    ).astype(jnp.bfloat16)
+    channel = lax.broadcasted_iota(jnp.int32, (own, capacity), 0)
+    lane_out = lax.broadcasted_iota(jnp.int32, (own, capacity), 1)
+    code = jnp.where(lane_out[:1] == 8 * own, (count // 16).astype(jnp.float32), 0.0)
+    code = jnp.where(lane_out[:1] == 8 * own + 1, (count % 16).astype(jnp.float32), code)
     for j in range(n_ctx):
         rows = slice(j * own, (j + 1) * own)
-        out_ref[j, :own, :capacity] = arrivals_ref[0, rows, :]
-        out_ref[j, :own, capacity:] = jnp.zeros((own, EDGE), jnp.bfloat16)
-        out_ref[j, own:, :capacity] = mixed[rows]
-        out_ref[j, own:, capacity:] = edge[rows]
+        out_ref[j, :own, :] = arrivals_ref[0, rows, :]
+        out_ref[j, own : 2 * own, :] = mixed[rows]
+        tiled = jnp.dot(edge[rows], spread, preferred_element_type=jnp.float32)
+        flat = jnp.sum(jnp.where(lane_out // 8 == channel, tiled, 0.0), axis=0, keepdims=True)
+        out_ref[j, 2 * own : 2 * own + 1, :] = (flat + code).astype(jnp.bfloat16)
 
 
 def by_transpose(arrivals, counts, short_taps, filter_taps, skip_gain, out_weight):
@@ -196,12 +205,14 @@
             pl.BlockSpec(memory_space=pltpu.VMEM),
         ],
         out_specs=pl.BlockSpec(memory_space=pltpu.VMEM),
-        out_shape=jax.ShapeDtypeStruct((n_ctx, 2 * own, capacity + EDGE), jnp.bfloat16),
+        out_shape=jax.ShapeDtypeStruct((n_ctx, 2 * own + 1, capacity), jnp.bfloat16),
     )(counts, arrivals, short_taps)
     got = lax.all_to_all(payload, "ctx", 0, 0, tiled=False)
-    rows = got[:, :, :capacity]
-    edge_in = got[:, own:, capacity:]
-    every_count = edge_in[:, 0, 8].astype(jnp.int32) * 16 + edge_in[:, 0, 9].astype(jnp.int32)
+    rows = got[:, : 2 * own]
+    edge_in = got[:, 2 * own]
+    every_count = (
+        edge_in[:, own * 8].astype(jnp.int32) * 16 + edge_in[:, own * 8 + 1].astype(jnp.int32)
+    )
     offsets = jnp.cumsum(every_count) - every_count
 
     frame = 3 * T_DEV
@@ -222,7 +233,7 @@
     shorted_gate = shorted_gate + taps[0, 2, :, None] * gate[:, :-2]
     from_senders = full[own:, T_DEV : T_DEV + length]
 
-    values = edge_in[:, :, :8]
+    values = edge_in[:, : own * 8].reshape(n_ctx, own, 8)
     count_col = every_count[:, None]
     at_row = jnp.concatenate(
         [jnp.zeros_like(count_col), jnp.ones_like(count_col), count_col - 2, count_col - 1], axis=1

time: 59.4 us -> 57.6 us (0.970)
  waiting for transfers between devices: 13.9 us -> 12.5 us
  other arithmetic: 3.46 us -> 2.62 us
  local copies, waits for them, and re-layouts: 4.07 us -> 4.69 us
    all_to_all x1, waiting for transfers between devices: 13.9 us -> 12.5 us  [by_transpose(): got = lax.all_to_all(payload, 'ctx', 0, 0, tiled=False)]
where the time goes in v11:
time: 57.6 us; the launch traced here: 57.3 us
  blocking collectives  18 us (31%)
  waiting for transfers between devices  12.5 us (22%)
  matrix products  8.13 us (14%)
  starting transfers between devices  7.25 us (13%)
  local copies, waits for them, and re-layouts  4.69 us (8%)
  Pallas kernels  2.97 us (5%)
  other arithmetic  2.62 us (5%)
  between operations  1.1 us (2%)
    all_to_all x1, waiting for transfers between devices, by_transpose(): got = lax.all_to_all(payload, 'ctx', 0, 0, tiled=False)  12.5 us
    all_to_all x1, blocking collectives, by_transpose(): lax.all_to_all(gated.reshape(own, n_ctx, T_DEV), 'ctx', 1, 0, tiled=False)  10.8 us
    all_to_all x1, starting transfers between devices, by_transpose(): got = lax.all_to_all(payload, 'ctx', 0, 0, tiled=False)  7.25 us
    all_gather x1, blocking collectives, by_transpose(): lax.all_gather(gated_block, 'ch', axis=0, tiled=True)  7.2 us
    dot_general x1, matrix products, by_transpose(): jnp.einsum('icr,irj->icj', rows, select, preferred_element_type=jnp.bfloa...  3.58 us
    pallas_call x1, Pallas kernels, by_transpose(): pl.pallas_call(functools.partial(sender_kernel, n_ctx=n_ctx, own=own), in...  2.97 us
    dot_general x2, matrix products, transform(): jnp.einsum(spec, blocks, hi, preferred_element_type=jnp.float32)  1.41 us
    convert_element_type x1, local copies, waits for them, and re-layouts, by_transpose(): return mixed.astype(jnp.bfloat16)  1.31 us
  transfers between devices with their start and end apart: 1, of which 1 were waited for; matrix products, arithmetic and copies ran while one was open for 6% of the time, Pallas kernels for 0%

profile of v11, /device:TPU:0, one launch (start us, length us, event | category | flops | bytes accessed | tf_op | source)
XLA Modules:
  0.0 57.3 jit_solution(9767508835622034980)
XLA Ops:
  0.0 0.0 copy-start
  0.0 0.0 copy-start.1
  0.8 3.0 %shard_map.91 = bf16[8,65,512]{2,1,0:T(8,128)(2,1)} custom-call(s32[1]{0:T(128)S(6)} %copy.90.count_ref, bf16[3,256,512]{2,1,0:T(8,128)(2,1)} %arrivals_ref.1, f32[3,3,256]{2,1,0:T(4,128)} %taps_ref.1), custom_call_target="tpu_custom_call" | custom-call | tf_op jit(solution)/shard_map/pallas_call | solution.py:200
  3.7 7.3 %all-to-all-start = ((bf16[8,65,512]{2,1,0:T(8,128)(2,1)}), bf16[8,65,512]{2,1,0:T(8,128)(2,1)S(1)}, u32[]{:S(2)}, u32[]{:S(2)}) async-start(bf16[8,65,512]{2,1,0:T(8,128)(2,1)} %shard_map.91), calls=%async_computation | async-start | bytes 1179648 | tf_op jit(solution)/shard_map/all_to_all | solution.py:210
  11.0 0.8 %dynamic_slice.11 = f32[32]{0:T(128)S(1)} dynamic-slice(f32[256]{0:T(256)} %param.13, s32[]{:T(128)S(6)} %select_n.43), dynamic_slice_sizes={32} | dynamic-slice | bytes 260 | tf_op jit(solution)/shard_map/dynamic_slice | solution.py:289
  11.8 0.0 copy-done
  11.8 0.1 pad_add_fusion.3
  11.9 0.9 %fusion.44 = (f32[32]{0:T(128)S(1)}, f32[32]{0:T(128)S(1)}, f32[32]{0:T(128)S(1)}, f32[32]{0:T(128)S(1)}, f32[32]{0:T(128)S(1)}, /*index=5*/f32[32]{0:T(128)S(1)}, f32[32]{0:T(128)S(1)}, f32[32]{0:T(128)S(1)}, f32[32]{0:T(128)S(1)}) fusion(f32[3,3,256]{2,1,0:T(4,128)} %taps_ref.1, s32[]{:T(128)S(6)} %select_n.43, s32[]{:T(128)S(6)} %add.370, s32[]{:T(128)S(6)} %add.369), kind=kLoop, calls=%fused_computation.144 | loop fusion | bytes 2316 | tf_op jit(solution)/shard_map/mul | solution.py:231
  12.8 1.2 %fusion.21 = f32[32,9,512]{2,0,1:T(8,128)S(1)} fusion(bf16[256,512,1]{1,0,2:T(8,128)(2,1)} %constant.153, bf16[4,9,8,256]{3,2,1,0:T(8,128)(2,1)S(1)} %bitcast.107), kind=kOutput, calls=%fused_computation.54 | convolution fusion | flops 75497472 | bytes 999424 | tf_op jit(solution)/shard_map/cnt,tf->cnf/dot_general | solution.py:45
  14.0 0.0 copy-done.1
  14.0 0.2 convolution_add_fusion
  14.3 0.1 fusion.6
  14.3 12.5 %all-to-all-done = bf16[8,65,512]{2,1,0:T(8,128)(2,1)S(1)} async-done(((bf16[8,65,512]{2,1,0:T(8,128)(2,1)}), bf16[8,65,512]{2,1,0:T(8,128)(2,1)S(1)}, u32[]{:S(2)}, u32[]{:S(2)}) %all-to-all-start) | async-done | bytes 532512 | tf_op jit(solution)/shard_map/all_to_all | solution.py:210
  26.9 0.1 convert_add_fusion
  27.0 0.2 subtract_reduce_fusion
  27.2 0.1 iota_compare_fusion.1
  27.3 0.1 copy.45
  27.4 0.1 copy.46
  27.5 0.1 add_add_fusion
  27.5 0.1 copy.44
  27.6 0.1 iota_add_fusion
  27.7 0.1 reshape.191
  27.9 0.1 compare_and_fusion
  28.0 0.1 convert_reduce_fusion
  28.1 3.6 %fusion.1 = bf16[8,64,768]{2,1,0:T(8,128)(2,1)S(1)} fusion(s32[8,512]{1,0:T(8,128)S(1)} %iota_add_fusion, pred[8,512]{1,0:T(8,128)(4,1)S(1)} %iota_compare_fusion.1, bf16[8,65,512]{2,1,0:T(8,128)(2,1)S(1)} %all-to-all-done), kind=kOutput, calls=%fused_computation.2 | convolution fusion | flops 408944640 | bytes 1331200 | tf_op jit(solution)/shard_map/icr,irj->icj/dot_general | solution.py:224
  31.7 0.0 copy-start.2
  31.7 0.1 slice_bitcast_fusion.7
  31.8 0.1 fusion.50
  31.9 0.1 copy.62
  32.0 0.1 copy.64
  32.2 0.1 copy.63
  32.3 0.1 copy.65
  32.4 0.1 pad_add_fusion
  32.6 0.1 slice_convert_fusion
  32.7 0.3 convolution_bitcast_fusion
  32.9 0.3 convolution_bitcast_fusion.1
  33.2 0.4 slice_select_fusion
  33.6 0.0 copy-done.2
  33.6 0.2 fusion.24
  33.8 0.2 convolution_add_fusion.1
  34.2 0.1 slice_multiply_fusion.20
  34.3 0.1 slice_multiply_fusion.16
  34.4 0.0 copy-start.3
  34.4 0.1 slice_multiply_fusion.12
  34.5 0.2 subtract_select_fusion
  34.7 0.0 copy-start.4
  34.7 0.2 add_select_fusion
  34.9 0.1 pad_maximum_fusion
  35.0 0.4 copy-done.3
  35.4 0.9 %fusion.8 = f32[32,8,256]{2,1,0:T(8,128)S(1)} fusion(f32[512,256,1]{1,0,2:T(8,128)S(1)} %copy-done.3, f32[32,8,512]{2,0,1:T(8,128)S(1)} %pad_maximum_fusion), kind=kOutput, calls=%fused_computation.15 | convolution fusion | flops 402653184 | bytes 1310720 | tf_op jit(solution)/shard_map/cnf,ft->cnt/dot_general | solution.py:288
  36.3 0.1 copy.68
  36.4 0.2 fusion.18
  36.7 10.8 %all_to_all.20 = bf16[1,32,8,256]{3,1,0,2:T(8,128)(2,1)S(1)} all-to-all(bf16[1,32,8,256]{3,1,0,2:T(8,128)(2,1)S(1)} %copy.56), channel_id=1, replica_groups=mesh['ctx'=8,'ch'=4] {'ctx'}, dimensions={2} | all-to-all | bytes 262144 | tf_op jit(solution)/shard_map/all_to_all | solution.py:292
  47.5 7.2 %all_gather.3 = bf16[1024,256]{1,0:T(8,128)(2,1)S(1)} all-gather(bf16[256,256]{1,0:T(8,128)(2,1)S(1)} %bitcast.112), channel_id=1, replica_groups=mesh['ctx'=8,'ch'=4] {'ch'}, dimensions={0}, use_global_device_ids=true | all-gather | bytes 655360 | tf_op jit(solution)/shard_map/all_gather | solution.py:296
  54.7 0.0 copy-done.4
  54.7 1.3 %fusion.5 = bf16[2048,256]{0,1:T(8,128)(2,1)S(1)} fusion(bf16[1024,256]{1,0:T(8,128)(2,1)S(1)} %all_gather.3, bf16[2048,1024]{1,0:T(8,128)(2,1)S(1)} %copy-done.4), kind=kOutput, calls=%fused_computation.8 | convolution fusion | flops 1074266112 | bytes 5767168 | tf_op jit(solution)/shard_map/dot_general | solution.py:294
  56.0 1.3 %copy.57 = bf16[2048,256]{1,0:T(8,128)(2,1)} copy(bf16[2048,256]{0,1:T(8,128)(2,1)S(1)} %fusion.5) | data formatting | bytes 2097152 | tf_op jit(solution)/shard_map/convert_element_type | solution.py:299
  (20 shorter events, 0.3 us)
Async XLA Ops:
  0.0 11.8 %copy-start = (bf16[256,2048]{1,0:T(8,128)(2,1)S(1)}, bf16[256,2048]{1,0:T(8,128)(2,1)}, u32[]{:S(2)}) copy-start(bf16[256,2048]{1,0:T(8,128)(2,1)} %param.12) | copy-start | bytes 3145732
  0.0 14.0 %copy-start.1 = (bf16[256,512,1]{1,0,2:T(8,128)(2,1)S(1)}, bf16[256,512,1]{1,0,2:T(8,128)(2,1)}, u32[]{:S(2)}) copy-start(bf16[256,512,1]{1,0,2:T(8,128)(2,1)} %constant.154) | copy-start | bytes 786436
  3.7 23.1 %all-to-all-start = ((bf16[8,65,512]{2,1,0:T(8,128)(2,1)}), bf16[8,65,512]{2,1,0:T(8,128)(2,1)S(1)}, u32[]{:S(2)}, u32[]{:S(2)}) async-start(bf16[8,65,512]{2,1,0:T(8,128)(2,1)} %shard_map.91), calls=%async_computation | async-start | bytes 1179648 | tf_op jit(solution)/shard_map/all_to_all | solution.py:210
  31.7 1.8 %copy-start.2 = (bf16[256,512,1]{1,0,2:T(8,128)(2,1)S(1)}, bf16[256,512,1]{1,0,2:T(8,128)(2,1)}, u32[]{:S(2)}) copy-start(bf16[256,512,1]{1,0,2:T(8,128)(2,1)} %constant.153) | copy-start | bytes 786436
  34.4 1.0 %copy-start.3 = (f32[512,256,1]{1,0,2:T(8,128)S(1)}, f32[512,256,1]{1,0,2:T(8,128)}, u32[]{:S(2)}) copy-start(f32[512,256,1]{1,0,2:T(8,128)} %constant.155) | copy-start | bytes 1572868
  34.7 20.0 %copy-start.4 = (bf16[2048,1024]{1,0:T(8,128)(2,1)S(1)}, bf16[2048,1024]{1,0:T(8,128)(2,1)}, u32[]{:S(2)}) copy-start(bf16[2048,1024]{1,0:T(8,128)(2,1)} %param.14) | copy-start | bytes 12582916

commit v12 on v11

--- a/solution.py
+++ b/solution.py
@@ -215,15 +215,16 @@
     )
     offsets = jnp.cumsum(every_count) - every_count
 
-    frame = 3 * T_DEV
+    frame = 2 * T_DEV
     row = jnp.arange(capacity, dtype=jnp.int32)[None, :, None]
     col = jnp.arange(frame, dtype=jnp.int32)[None, None, :]
     sampler = jnp.arange(n_ctx, dtype=jnp.int32)[:, None, None]
-    shift = offsets[:, None, None] - (sampler - 1) * T_DEV
+    shift = offsets[:, None, None] - (sampler - 1) * T_DEV - HALF
     select = ((row + shift == col) & (row < every_count[:, None, None])).astype(jnp.bfloat16)
     placed = jnp.einsum("icr,irj->icj", rows, select, preferred_element_type=jnp.bfloat16)
     full = sum(
-        jnp.pad(placed[i], ((0, 0), (i * T_DEV, (n_ctx - 1 - i) * T_DEV))) for i in range(n_ctx)
+        jnp.pad(placed[i], ((0, 0), (i * T_DEV + HALF, (n_ctx - i) * T_DEV - HALF)))
+        for i in range(n_ctx)
     )
     first = device * own
     taps = lax.dynamic_slice_in_dim(short_taps, first, own, 2)

time: 57.6 us -> 56.5 us (0.981)
  matrix products: 8.13 us -> 7.03 us
    dot_general x1, matrix products: 3.58 us -> 2.49 us  [by_transpose(): jnp.einsum('icr,irj->icj', rows, select, preferred_element_type=jnp.bfloa...]
where the time goes in v12:
time: 56.5 us; the launch traced here: 56.1 us
  blocking collectives  18 us (32%)
  waiting for transfers between devices  12.5 us (22%)
  starting transfers between devices  7.25 us (13%)
  matrix products  7.03 us (12%)
  local copies, waits for them, and re-layouts  4.66 us (8%)
  Pallas kernels  2.97 us (5%)
  other arithmetic  2.6 us (5%)
  between operations  1.11 us (2%)
    all_to_all x1, waiting for transfers between devices, by_transpose(): got = lax.all_to_all(payload, 'ctx', 0, 0, tiled=False)  12.5 us
    all_to_all x1, blocking collectives, by_transpose(): lax.all_to_all(gated.reshape(own, n_ctx, T_DEV), 'ctx', 1, 0, tiled=False)  10.8 us
    all_to_all x1, starting transfers between devices, by_transpose(): got = lax.all_to_all(payload, 'ctx', 0, 0, tiled=False)  7.25 us
    all_gather x1, blocking collectives, by_transpose(): lax.all_gather(gated_block, 'ch', axis=0, tiled=True)  7.18 us
    pallas_call x1, Pallas kernels, by_transpose(): pl.pallas_call(functools.partial(sender_kernel, n_ctx=n_ctx, own=own), in...  2.97 us
    dot_general x1, matrix products, by_transpose(): jnp.einsum('icr,irj->icj', rows, select, preferred_element_type=jnp.bfloa...  2.49 us
    dot_general x2, matrix products, transform(): jnp.einsum(spec, blocks, hi, preferred_element_type=jnp.float32)  1.41 us
    convert_element_type x1, local copies, waits for them, and re-layouts, by_transpose(): return mixed.astype(jnp.bfloat16)  1.31 us
  transfers between devices with their start and end apart: 1, of which 1 were waited for; matrix products, arithmetic and copies ran while one was open for 6% of the time, Pallas kernels for 0%

profile of v12, /device:TPU:0, one launch (start us, length us, event | category | flops | bytes accessed | tf_op | source)
XLA Modules:
  0.0 56.1 jit_solution(18296162982164610533)
XLA Ops:
  0.0 0.0 copy-start
  0.0 0.0 copy-start.1
  0.8 3.0 %shard_map.91 = bf16[8,65,512]{2,1,0:T(8,128)(2,1)} custom-call(s32[1]{0:T(128)S(6)} %copy.90.count_ref, bf16[3,256,512]{2,1,0:T(8,128)(2,1)} %arrivals_ref.1, f32[3,3,256]{2,1,0:T(4,128)} %taps_ref.1), custom_call_target="tpu_custom_call" | custom-call | tf_op jit(solution)/shard_map/pallas_call | solution.py:200
  3.7 7.3 %all-to-all-start = ((bf16[8,65,512]{2,1,0:T(8,128)(2,1)}), bf16[8,65,512]{2,1,0:T(8,128)(2,1)S(1)}, u32[]{:S(2)}, u32[]{:S(2)}) async-start(bf16[8,65,512]{2,1,0:T(8,128)(2,1)} %shard_map.91), calls=%async_computation | async-start | bytes 1179648 | tf_op jit(solution)/shard_map/all_to_all | solution.py:210
  11.0 0.8 %dynamic_slice.11 = f32[32]{0:T(128)S(1)} dynamic-slice(f32[256]{0:T(256)} %param.13, s32[]{:T(128)S(6)} %select_n.43), dynamic_slice_sizes={32} | dynamic-slice | bytes 260 | tf_op jit(solution)/shard_map/dynamic_slice | solution.py:290
  11.8 0.0 copy-done
  11.8 0.1 pad_add_fusion.3
  11.9 0.9 %fusion.44 = (f32[32]{0:T(128)S(1)}, f32[32]{0:T(128)S(1)}, f32[32]{0:T(128)S(1)}, f32[32]{0:T(128)S(1)}, f32[32]{0:T(128)S(1)}, /*index=5*/f32[32]{0:T(128)S(1)}, f32[32]{0:T(128)S(1)}, f32[32]{0:T(128)S(1)}, f32[32]{0:T(128)S(1)}) fusion(f32[3,3,256]{2,1,0:T(4,128)} %taps_ref.1, s32[]{:T(128)S(6)} %select_n.43, s32[]{:T(128)S(6)} %add.376, s32[]{:T(128)S(6)} %add.375), kind=kLoop, calls=%fused_computation.144 | loop fusion | bytes 2316 | tf_op jit(solution)/shard_map/mul | solution.py:232
  12.8 1.2 %fusion.21 = f32[32,9,512]{2,0,1:T(8,128)S(1)} fusion(bf16[256,512,1]{1,0,2:T(8,128)(2,1)} %constant.156, bf16[4,9,8,256]{3,2,1,0:T(8,128)(2,1)S(1)} %bitcast.107), kind=kOutput, calls=%fused_computation.54 | convolution fusion | flops 75497472 | bytes 999424 | tf_op jit(solution)/shard_map/cnt,tf->cnf/dot_general | solution.py:45
  14.0 0.0 copy-done.1
  14.0 0.2 convolution_add_fusion
  14.3 0.1 fusion.6
  14.3 12.5 %all-to-all-done = bf16[8,65,512]{2,1,0:T(8,128)(2,1)S(1)} async-done(((bf16[8,65,512]{2,1,0:T(8,128)(2,1)}), bf16[8,65,512]{2,1,0:T(8,128)(2,1)S(1)}, u32[]{:S(2)}, u32[]{:S(2)}) %all-to-all-start) | async-done | bytes 532512 | tf_op jit(solution)/shard_map/all_to_all | solution.py:210
  26.9 0.1 convert_add_fusion
  27.0 0.2 subtract_reduce_fusion
  27.2 0.1 iota_compare_fusion.1
  27.3 0.1 copy.45
  27.4 0.1 copy.46
  27.5 0.1 add_add_fusion
  27.5 0.1 copy.44
  27.6 0.1 iota_add_fusion
  27.7 2.5 %fusion.1 = bf16[8,64,512]{2,1,0:T(8,128)(2,1)S(1)} fusion(s32[8,512]{1,0:T(8,128)S(1)} %iota_add_fusion, pred[8,512]{1,0:T(8,128)(4,1)S(1)} %iota_compare_fusion.1, bf16[8,65,512]{2,1,0:T(8,128)(2,1)S(1)} %all-to-all-done), kind=kOutput, calls=%fused_computation.2 | convolution fusion | flops 272629760 | bytes 1069056 | tf_op jit(solution)/shard_map/icr,irj->icj/dot_general | solution.py:224
  30.2 0.0 copy-start.2
  30.3 0.1 reshape.193
  30.4 0.1 compare_and_fusion
  30.5 0.1 convert_reduce_fusion
  30.7 0.1 fusion.50
  30.8 0.1 copy.62
  30.9 0.1 copy.64
  31.0 0.1 copy.63
  31.2 0.1 copy.65
  31.3 0.1 pad_add_fusion
  31.4 0.1 slice_convert_fusion
  31.5 0.3 convolution_bitcast_fusion
  31.8 0.3 convolution_bitcast_fusion.1
  32.0 0.4 slice_select_fusion
  32.4 0.0 copy-done.2
  32.4 0.2 fusion.24
  32.7 0.2 convolution_add_fusion.1
  33.1 0.1 slice_multiply_fusion.20
  33.1 0.1 slice_multiply_fusion.16
  33.2 0.0 copy-start.3
  33.2 0.1 slice_multiply_fusion.12
  33.3 0.2 subtract_select_fusion
  33.5 0.0 copy-start.4
  33.6 0.2 add_select_fusion
  33.8 0.1 pad_maximum_fusion
  33.8 0.4 copy-done.3
  34.3 0.9 %fusion.8 = f32[32,8,256]{2,1,0:T(8,128)S(1)} fusion(f32[512,256,1]{1,0,2:T(8,128)S(1)} %copy-done.3, f32[32,8,512]{2,0,1:T(8,128)S(1)} %pad_maximum_fusion), kind=kOutput, calls=%fused_computation.15 | convolution fusion | flops 402653184 | bytes 1310720 | tf_op jit(solution)/shard_map/cnf,ft->cnt/dot_general | solution.py:289
  35.1 0.1 copy.68
  35.2 0.2 fusion.18
  35.5 10.8 %all_to_all.20 = bf16[1,32,8,256]{3,1,0,2:T(8,128)(2,1)S(1)} all-to-all(bf16[1,32,8,256]{3,1,0,2:T(8,128)(2,1)S(1)} %copy.56), channel_id=1, replica_groups=mesh['ctx'=8,'ch'=4] {'ctx'}, dimensions={2} | all-to-all | bytes 262144 | tf_op jit(solution)/shard_map/all_to_all | solution.py:293
  46.3 7.2 %all_gather.3 = bf16[1024,256]{1,0:T(8,128)(2,1)S(1)} all-gather(bf16[256,256]{1,0:T(8,128)(2,1)S(1)} %bitcast.112), channel_id=1, replica_groups=mesh['ctx'=8,'ch'=4] {'ch'}, dimensions={0}, use_global_device_ids=true | all-gather | bytes 655360 | tf_op jit(solution)/shard_map/all_gather | solution.py:297
  53.5 0.0 copy-done.4
  53.5 1.3 %fusion.5 = bf16[2048,256]{0,1:T(8,128)(2,1)S(1)} fusion(bf16[1024,256]{1,0:T(8,128)(2,1)S(1)} %all_gather.3, bf16[2048,1024]{1,0:T(8,128)(2,1)S(1)} %copy-done.4), kind=kOutput, calls=%fused_computation.8 | convolution fusion | flops 1074266112 | bytes 5767168 | tf_op jit(solution)/shard_map/dot_general | solution.py:295
  54.8 1.3 %copy.57 = bf16[2048,256]{1,0:T(8,128)(2,1)} copy(bf16[2048,256]{0,1:T(8,128)(2,1)S(1)} %fusion.5) | data formatting | bytes 2097152 | tf_op jit(solution)/shard_map/convert_element_type | solution.py:300
  (21 shorter events, 0.4 us)
Async XLA Ops:
  0.0 11.8 %copy-start = (bf16[256,2048]{1,0:T(8,128)(2,1)S(1)}, bf16[256,2048]{1,0:T(8,128)(2,1)}, u32[]{:S(2)}) copy-start(bf16[256,2048]{1,0:T(8,128)(2,1)} %param.12) | copy-start | bytes 3145732
  0.0 14.0 %copy-start.1 = (bf16[256,512,1]{1,0,2:T(8,128)(2,1)S(1)}, bf16[256,512,1]{1,0,2:T(8,128)(2,1)}, u32[]{:S(2)}) copy-start(bf16[256,512,1]{1,0,2:T(8,128)(2,1)} %constant.157) | copy-start | bytes 786436
  3.7 23.1 %all-to-all-start = ((bf16[8,65,512]{2,1,0:T(8,128)(2,1)}), bf16[8,65,512]{2,1,0:T(8,128)(2,1)S(1)}, u32[]{:S(2)}, u32[]{:S(2)}) async-start(bf16[8,65,512]{2,1,0:T(8,128)(2,1)} %shard_map.91), calls=%async_computation | async-start | bytes 1179648 | tf_op jit(solution)/shard_map/all_to_all | solution.py:210
  30.2 2.2 %copy-start.2 = (bf16[256,512,1]{1,0,2:T(8,128)(2,1)S(1)}, bf16[256,512,1]{1,0,2:T(8,128)(2,1)}, u32[]{:S(2)}) copy-start(bf16[256,512,1]{1,0,2:T(8,128)(2,1)} %constant.156) | copy-start | bytes 786436
  33.2 1.0 %copy-start.3 = (f32[512,256,1]{1,0,2:T(8,128)S(1)}, f32[512,256,1]{1,0,2:T(8,128)}, u32[]{:S(2)}) copy-start(f32[512,256,1]{1,0,2:T(8,128)} %constant.158) | copy-start | bytes 1572868
  33.5 20.0 %copy-start.4 = (bf16[2048,1024]{1,0:T(8,128)(2,1)S(1)}, bf16[2048,1024]{1,0:T(8,128)(2,1)}, u32[]{:S(2)}) copy-start(bf16[2048,1024]{1,0:T(8,128)(2,1)} %param.14) | copy-start | bytes 12582916

commit v13 on v12

--- a/solution.py
+++ b/solution.py
@@ -148,9 +148,11 @@
     square = lax.broadcasted_iota(jnp.int32, (lane.shape[0], lane.shape[0]), 0)
     diagonal = square == lax.broadcasted_iota(jnp.int32, square.shape, 1)
 
+    ones = jnp.ones((lane.shape[0], EDGE), jnp.float32)
+
     def tap(part, k):
         spread = jnp.where(diagonal, taps_ref[part, k : k + 1, :], 0.0)
-        return jnp.sum(spread, axis=1, keepdims=True)
+        return jnp.dot(spread, ones, precision=lax.Precision.HIGHEST)[:, :1]
 
     near = []
     edge = jnp.where(column[:1] == 8, (count // 16).astype(jnp.float32), 0.0)

time: 56.5 us -> 57.3 us (1.014)
  Pallas kernels: 2.97 us -> 3.81 us
    pallas_call x1, Pallas kernels: 2.97 us -> 3.81 us  [by_transpose(): pl.pallas_call(functools.partial(sender_kernel, n_ctx=n_ctx, own=own), in...]
where the time goes in v13:
time: 57.3 us; the launch traced here: 57 us
  blocking collectives  18 us (31%)
  waiting for transfers between devices  12.6 us (22%)
  starting transfers between devices  7.25 us (13%)
  matrix products  7.02 us (12%)
  local copies, waits for them, and re-layouts  4.66 us (8%)
  Pallas kernels  3.81 us (7%)
  other arithmetic  2.6 us (5%)
  between operations  1.11 us (2%)
    all_to_all x1, waiting for transfers between devices, by_transpose(): got = lax.all_to_all(payload, 'ctx', 0, 0, tiled=False)  12.6 us
    all_to_all x1, blocking collectives, by_transpose(): lax.all_to_all(gated.reshape(own, n_ctx, T_DEV), 'ctx', 1, 0, tiled=False)  10.8 us
    all_to_all x1, starting transfers between devices, by_transpose(): got = lax.all_to_all(payload, 'ctx', 0, 0, tiled=False)  7.25 us
    all_gather x1, blocking collectives, by_transpose(): lax.all_gather(gated_block, 'ch', axis=0, tiled=True)  7.18 us
    pallas_call x1, Pallas kernels, by_transpose(): pl.pallas_call(functools.partial(sender_kernel, n_ctx=n_ctx, own=own), in...  3.81 us
    dot_general x1, matrix products, by_transpose(): jnp.einsum('icr,irj->icj', rows, select, preferred_element_type=jnp.bfloa...  2.49 us
    dot_general x2, matrix products, transform(): jnp.einsum(spec, blocks, hi, preferred_element_type=jnp.float32)  1.39 us
    convert_element_type x1, local copies, waits for them, and re-layouts, by_transpose(): return mixed.astype(jnp.bfloat16)  1.31 us
  transfers between devices with their start and end apart: 1, of which 1 were waited for; matrix products, arithmetic and copies ran while one was open for 6% of the time, Pallas kernels for 0%

profile of v13, /device:TPU:0, one launch (start us, length us, event | category | flops | bytes accessed | tf_op | source)
XLA Modules:
  0.0 57.0 jit_solution(16968636450243809598)
XLA Ops:
  0.0 0.0 copy-start
  0.0 0.0 copy-start.1
  0.8 3.8 %shard_map.91 = bf16[8,65,512]{2,1,0:T(8,128)(2,1)} custom-call(s32[1]{0:T(128)S(6)} %copy.90.count_ref, bf16[3,256,512]{2,1,0:T(8,128)(2,1)} %arrivals_ref.1, f32[3,3,256]{2,1,0:T(4,128)} %taps_ref.1), custom_call_target="tpu_custom_call" | custom-call | tf_op jit(solution)/shard_map/pallas_call | solution.py:202
  4.6 7.3 %all-to-all-start = ((bf16[8,65,512]{2,1,0:T(8,128)(2,1)}), bf16[8,65,512]{2,1,0:T(8,128)(2,1)S(1)}, u32[]{:S(2)}, u32[]{:S(2)}) async-start(bf16[8,65,512]{2,1,0:T(8,128)(2,1)} %shard_map.91), calls=%async_computation | async-start | bytes 1179648 | tf_op jit(solution)/shard_map/all_to_all | solution.py:212
  11.9 0.8 %dynamic_slice.11 = f32[32]{0:T(128)S(1)} dynamic-slice(f32[256]{0:T(256)} %param.13, s32[]{:T(128)S(6)} %select_n.43), dynamic_slice_sizes={32} | dynamic-slice | bytes 260 | tf_op jit(solution)/shard_map/dynamic_slice | solution.py:292
  12.6 0.0 copy-done
  12.6 0.1 pad_add_fusion.3
  12.7 0.9 %fusion.44 = (f32[32]{0:T(128)S(1)}, f32[32]{0:T(128)S(1)}, f32[32]{0:T(128)S(1)}, f32[32]{0:T(128)S(1)}, f32[32]{0:T(128)S(1)}, /*index=5*/f32[32]{0:T(128)S(1)}, f32[32]{0:T(128)S(1)}, f32[32]{0:T(128)S(1)}, f32[32]{0:T(128)S(1)}) fusion(f32[3,3,256]{2,1,0:T(4,128)} %taps_ref.1, s32[]{:T(128)S(6)} %select_n.43, s32[]{:T(128)S(6)} %add.376, s32[]{:T(128)S(6)} %add.375), kind=kLoop, calls=%fused_computation.144 | loop fusion | bytes 2316 | tf_op jit(solution)/shard_map/mul | solution.py:234
  13.6 1.2 %fusion.21 = f32[32,9,512]{2,0,1:T(8,128)S(1)} fusion(bf16[256,512,1]{1,0,2:T(8,128)(2,1)} %constant.156, bf16[4,9,8,256]{3,2,1,0:T(8,128)(2,1)S(1)} %bitcast.107), kind=kOutput, calls=%fused_computation.54 | convolution fusion | flops 75497472 | bytes 999424 | tf_op jit(solution)/shard_map/cnt,tf->cnf/dot_general | solution.py:45
  14.8 0.0 copy-done.1
  14.8 0.2 convolution_add_fusion
  15.1 0.1 fusion.6
  15.2 12.6 %all-to-all-done = bf16[8,65,512]{2,1,0:T(8,128)(2,1)S(1)} async-done(((bf16[8,65,512]{2,1,0:T(8,128)(2,1)}), bf16[8,65,512]{2,1,0:T(8,128)(2,1)S(1)}, u32[]{:S(2)}, u32[]{:S(2)}) %all-to-all-start) | async-done | bytes 532512 | tf_op jit(solution)/shard_map/all_to_all | solution.py:212
  27.7 0.1 convert_add_fusion
  27.8 0.2 subtract_reduce_fusion
  28.1 0.1 iota_compare_fusion.1
  28.1 0.1 copy.45
  28.2 0.1 copy.46
  28.3 0.1 add_add_fusion
  28.4 0.1 copy.44
  28.5 0.1 iota_add_fusion
  28.5 2.5 %fusion.1 = bf16[8,64,512]{2,1,0:T(8,128)(2,1)S(1)} fusion(s32[8,512]{1,0:T(8,128)S(1)} %iota_add_fusion, pred[8,512]{1,0:T(8,128)(4,1)S(1)} %iota_compare_fusion.1, bf16[8,65,512]{2,1,0:T(8,128)(2,1)S(1)} %all-to-all-done), kind=kOutput, calls=%fused_computation.2 | convolution fusion | flops 272629760 | bytes 1069056 | tf_op jit(solution)/shard_map/icr,irj->icj/dot_general | solution.py:226
  31.0 0.0 copy-start.2
  31.1 0.1 reshape.193
  31.3 0.1 compare_and_fusion
  31.4 0.1 convert_reduce_fusion
  31.5 0.1 fusion.50
  31.6 0.1 copy.62
  31.7 0.1 copy.64
  31.9 0.1 copy.63
  32.0 0.1 copy.65
  32.2 0.1 pad_add_fusion
  32.2 0.1 slice_convert_fusion
  32.4 0.3 convolution_bitcast_fusion
  32.6 0.3 convolution_bitcast_fusion.1
  32.9 0.4 slice_select_fusion
  33.3 0.0 copy-done.2
  33.3 0.2 fusion.24
  33.5 0.2 convolution_add_fusion.1
  33.9 0.1 slice_multiply_fusion.20
  34.0 0.1 slice_multiply_fusion.16
  34.1 0.0 copy-start.3
  34.1 0.1 slice_multiply_fusion.12
  34.2 0.2 subtract_select_fusion
  34.4 0.0 copy-start.4
  34.4 0.2 add_select_fusion
  34.6 0.1 pad_maximum_fusion
  34.7 0.4 copy-done.3
  35.1 0.9 %fusion.8 = f32[32,8,256]{2,1,0:T(8,128)S(1)} fusion(f32[512,256,1]{1,0,2:T(8,128)S(1)} %copy-done.3, f32[32,8,512]{2,0,1:T(8,128)S(1)} %pad_maximum_fusion), kind=kOutput, calls=%fused_computation.15 | convolution fusion | flops 402653184 | bytes 1310720 | tf_op jit(solution)/shard_map/cnf,ft->cnt/dot_general | solution.py:291
  36.0 0.1 copy.68
  36.1 0.2 fusion.18
  36.4 10.8 %all_to_all.20 = bf16[1,32,8,256]{3,1,0,2:T(8,128)(2,1)S(1)} all-to-all(bf16[1,32,8,256]{3,1,0,2:T(8,128)(2,1)S(1)} %copy.56), channel_id=1, replica_groups=mesh['ctx'=8,'ch'=4] {'ctx'}, dimensions={2} | all-to-all | bytes 262144 | tf_op jit(solution)/shard_map/all_to_all | solution.py:295
  47.2 7.2 %all_gather.3 = bf16[1024,256]{1,0:T(8,128)(2,1)S(1)} all-gather(bf16[256,256]{1,0:T(8,128)(2,1)S(1)} %bitcast.112), channel_id=1, replica_groups=mesh['ctx'=8,'ch'=4] {'ch'}, dimensions={0}, use_global_device_ids=true | all-gather | bytes 655360 | tf_op jit(solution)/shard_map/all_gather | solution.py:299
  54.3 0.0 copy-done.4
  54.3 1.3 %fusion.5 = bf16[2048,256]{0,1:T(8,128)(2,1)S(1)} fusion(bf16[1024,256]{1,0:T(8,128)(2,1)S(1)} %all_gather.3, bf16[2048,1024]{1,0:T(8,128)(2,1)S(1)} %copy-done.4), kind=kOutput, calls=%fused_computation.8 | convolution fusion | flops 1074266112 | bytes 5767168 | tf_op jit(solution)/shard_map/dot_general | solution.py:297
  55.7 1.3 %copy.57 = bf16[2048,256]{1,0:T(8,128)(2,1)} copy(bf16[2048,256]{0,1:T(8,128)(2,1)S(1)} %fusion.5) | data formatting | bytes 2097152 | tf_op jit(solution)/shard_map/convert_element_type | solution.py:302
  (21 shorter events, 0.4 us)
Async XLA Ops:
  0.0 12.6 %copy-start = (bf16[256,2048]{1,0:T(8,128)(2,1)S(1)}, bf16[256,2048]{1,0:T(8,128)(2,1)}, u32[]{:S(2)}) copy-start(bf16[256,2048]{1,0:T(8,128)(2,1)} %param.12) | copy-start | bytes 3145732
  0.0 14.8 %copy-start.1 = (bf16[256,512,1]{1,0,2:T(8,128)(2,1)S(1)}, bf16[256,512,1]{1,0,2:T(8,128)(2,1)}, u32[]{:S(2)}) copy-start(bf16[256,512,1]{1,0,2:T(8,128)(2,1)} %constant.157) | copy-start | bytes 786436
  4.6 23.1 %all-to-all-start = ((bf16[8,65,512]{2,1,0:T(8,128)(2,1)}), bf16[8,65,512]{2,1,0:T(8,128)(2,1)S(1)}, u32[]{:S(2)}, u32[]{:S(2)}) async-start(bf16[8,65,512]{2,1,0:T(8,128)(2,1)} %shard_map.91), calls=%async_computation | async-start | bytes 1179648 | tf_op jit(solution)/shard_map/all_to_all | solution.py:212
  31.0 2.2 %copy-start.2 = (bf16[256,512,1]{1,0,2:T(8,128)(2,1)S(1)}, bf16[256,512,1]{1,0,2:T(8,128)(2,1)}, u32[]{:S(2)}) copy-start(bf16[256,512,1]{1,0,2:T(8,128)(2,1)} %constant.156) | copy-start | bytes 786436
  34.1 1.0 %copy-start.3 = (f32[512,256,1]{1,0,2:T(8,128)S(1)}, f32[512,256,1]{1,0,2:T(8,128)}, u32[]{:S(2)}) copy-start(f32[512,256,1]{1,0,2:T(8,128)} %constant.158) | copy-start | bytes 1572868
  34.4 20.0 %copy-start.4 = (bf16[2048,1024]{1,0:T(8,128)(2,1)S(1)}, bf16[2048,1024]{1,0:T(8,128)(2,1)}, u32[]{:S(2)}) copy-start(bf16[2048,1024]{1,0:T(8,128)(2,1)} %param.14) | copy-start | bytes 12582916

commit v14 on v12

--- a/solution.py
+++ b/solution.py
@@ -142,48 +142,47 @@
 def sender_kernel(count_ref, arrivals_ref, taps_ref, out_ref, *, n_ctx, own):
     count = count_ref[0]
     capacity = arrivals_ref.shape[2]
-    lane = lax.broadcasted_iota(jnp.int32, arrivals_ref.shape[1:], 1)
+    channels = arrivals_ref.shape[1]
+    lane = lax.broadcasted_iota(jnp.int32, (own, capacity), 1)
+    channel = lax.broadcasted_iota(jnp.int32, (own, capacity), 0)
     row = lax.broadcasted_iota(jnp.int32, (capacity, EDGE), 0)
     column = lax.broadcasted_iota(jnp.int32, (capacity, EDGE), 1)
-    square = lax.broadcasted_iota(jnp.int32, (lane.shape[0], lane.shape[0]), 0)
-    diagonal = square == lax.broadcasted_iota(jnp.int32, square.shape, 1)
-
-    def tap(part, k):
-        spread = jnp.where(diagonal, taps_ref[part, k : k + 1, :], 0.0)
-        return jnp.sum(spread, axis=1, keepdims=True)
-
-    near = []
-    edge = jnp.where(column[:1] == 8, (count // 16).astype(jnp.float32), 0.0)
-    edge = jnp.where(column[:1] == 9, (count % 16).astype(jnp.float32), edge)
+    picks = []
     for part in range(2):
-        raw = arrivals_ref[1 + part]
-        x = raw.astype(jnp.float32)
-        back1 = jnp.where(lane >= 1, pltpu.roll(x, 1, 1), 0.0)
-        back2 = jnp.where(lane >= 2, pltpu.roll(x, 2, 1), 0.0)
-        s = tap(1 + part, 0) * x
-        s = s + tap(1 + part, 1) * back1
-        s = s + tap(1 + part, 2) * back2
-        near.append(s)
         wanted = jnp.where(column >= 4, count - 2 + column - 4 - 2 * part, column - 2 * part)
         inside = (column % 4 >= 2 * part) & (column % 4 < 2 * part + 2) & (column < 8)
-        pick = ((row == wanted) & inside).astype(jnp.bfloat16)
-        edge = edge + jnp.dot(raw, pick, preferred_element_type=jnp.float32)
-    mixed = (near[0] * near[1]).astype(jnp.bfloat16)
-    edge = edge.astype(jnp.bfloat16)
+        picks.append(((row == wanted) & inside).astype(jnp.bfloat16))
     flat_lane = lax.broadcasted_iota(jnp.int32, (EDGE, capacity), 1)
     spread = (
         (flat_lane < 8 * own) & (flat_lane % 8 == lax.broadcasted_iota(jnp.int32, (EDGE, capacity), 0))
     ).astype(jnp.bfloat16)
-    channel = lax.broadcasted_iota(jnp.int32, (own, capacity), 0)
-    lane_out = lax.broadcasted_iota(jnp.int32, (own, capacity), 1)
-    code = jnp.where(lane_out[:1] == 8 * own, (count // 16).astype(jnp.float32), 0.0)
-    code = jnp.where(lane_out[:1] == 8 * own + 1, (count % 16).astype(jnp.float32), code)
+    code = jnp.where(lane[:1] == 8 * own, (count // 16).astype(jnp.float32), 0.0)
+    code = jnp.where(lane[:1] == 8 * own + 1, (count % 16).astype(jnp.float32), code)
+    tap_lane = lax.broadcasted_iota(jnp.int32, (own, channels), 1)
+    tap_row = lax.broadcasted_iota(jnp.int32, (own, channels), 0)
     for j in range(n_ctx):
         rows = slice(j * own, (j + 1) * own)
+        mine = tap_lane == tap_row + j * own
+
+        def tap(part, k):
+            return jnp.sum(jnp.where(mine, taps_ref[part, k : k + 1, :], 0.0), axis=1, keepdims=True)
+
+        near = []
+        edge = jnp.zeros((own, EDGE), jnp.float32)
+        for part in range(2):
+            raw = arrivals_ref[1 + part, rows, :]
+            x = raw.astype(jnp.float32)
+            back1 = jnp.where(lane >= 1, pltpu.roll(x, 1, 1), 0.0)
+            back2 = jnp.where(lane >= 2, pltpu.roll(x, 2, 1), 0.0)
+            s = tap(1 + part, 0) * x
+            s = s + tap(1 + part, 1) * back1
+            s = s + tap(1 + part, 2) * back2
+            near.append(s)
+            edge = edge + jnp.dot(raw, picks[part], preferred_element_type=jnp.float32)
         out_ref[j, :own, :] = arrivals_ref[0, rows, :]
-        out_ref[j, own : 2 * own, :] = mixed[rows]
-        tiled = jnp.dot(edge[rows], spread, preferred_element_type=jnp.float32)
-        flat = jnp.sum(jnp.where(lane_out // 8 == channel, tiled, 0.0), axis=0, keepdims=True)
+        out_ref[j, own : 2 * own, :] = (near[0] * near[1]).astype(jnp.bfloat16)
+        tiled = jnp.dot(edge.astype(jnp.bfloat16), spread, preferred_element_type=jnp.float32)
+        flat = jnp.sum(jnp.where(lane // 8 == channel, tiled, 0.0), axis=0, keepdims=True)
         out_ref[j, 2 * own : 2 * own + 1, :] = (flat + code).astype(jnp.bfloat16)
 
 

time: 56.5 us -> 56.9 us (level)
  no operation moved by 1% of the time
where the time goes in v14:
time: 56.9 us; the launch traced here: 56.6 us
  blocking collectives  18 us (32%)
  waiting for transfers between devices  12.6 us (22%)
  starting transfers between devices  7.25 us (13%)
  matrix products  7.02 us (12%)
  local copies, waits for them, and re-layouts  4.66 us (8%)
  Pallas kernels  3.43 us (6%)
  other arithmetic  2.6 us (5%)
  between operations  1.11 us (2%)
    all_to_all x1, waiting for transfers between devices, by_transpose(): got = lax.all_to_all(payload, 'ctx', 0, 0, tiled=False)  12.6 us
    all_to_all x1, blocking collectives, by_transpose(): lax.all_to_all(gated.reshape(own, n_ctx, T_DEV), 'ctx', 1, 0, tiled=False)  10.8 us
    all_to_all x1, starting transfers between devices, by_transpose(): got = lax.all_to_all(payload, 'ctx', 0, 0, tiled=False)  7.25 us
    all_gather x1, blocking collectives, by_transpose(): lax.all_gather(gated_block, 'ch', axis=0, tiled=True)  7.18 us
    pallas_call x1, Pallas kernels, by_transpose(): pl.pallas_call(functools.partial(sender_kernel, n_ctx=n_ctx, own=own), in...  3.43 us
    dot_general x1, matrix products, by_transpose(): jnp.einsum('icr,irj->icj', rows, select, preferred_element_type=jnp.bfloa...  2.5 us
    dot_general x2, matrix products, transform(): jnp.einsum(spec, blocks, hi, preferred_element_type=jnp.float32)  1.4 us
    convert_element_type x1, local copies, waits for them, and re-layouts, by_transpose(): return mixed.astype(jnp.bfloat16)  1.31 us
  transfers between devices with their start and end apart: 1, of which 1 were waited for; matrix products, arithmetic and copies ran while one was open for 6% of the time, Pallas kernels for 0%

profile of v14, /device:TPU:0, one launch (start us, length us, event | category | flops | bytes accessed | tf_op | source)
XLA Modules:
  0.0 56.6 jit_solution(12297400359980179230)
XLA Ops:
  0.0 0.0 copy-start
  0.0 0.0 copy-start.1
  0.8 3.4 %shard_map.91 = bf16[8,65,512]{2,1,0:T(8,128)(2,1)} custom-call(s32[1]{0:T(128)S(6)} %copy.90.count_ref, bf16[3,256,512]{2,1,0:T(8,128)(2,1)} %arrivals_ref.1, f32[3,3,256]{2,1,0:T(4,128)} %taps_ref.1), custom_call_target="tpu_custom_call" | custom-call | tf_op jit(solution)/shard_map/pallas_call | solution.py:199
  4.2 7.3 %all-to-all-start = ((bf16[8,65,512]{2,1,0:T(8,128)(2,1)}), bf16[8,65,512]{2,1,0:T(8,128)(2,1)S(1)}, u32[]{:S(2)}, u32[]{:S(2)}) async-start(bf16[8,65,512]{2,1,0:T(8,128)(2,1)} %shard_map.91), calls=%async_computation | async-start | bytes 1179648 | tf_op jit(solution)/shard_map/all_to_all | solution.py:209
  11.5 0.8 %dynamic_slice.11 = f32[32]{0:T(128)S(1)} dynamic-slice(f32[256]{0:T(256)} %param.13, s32[]{:T(128)S(6)} %select_n.43), dynamic_slice_sizes={32} | dynamic-slice | bytes 260 | tf_op jit(solution)/shard_map/dynamic_slice | solution.py:289
  12.2 0.0 copy-done
  12.2 0.1 pad_add_fusion.3
  12.3 0.9 %fusion.44 = (f32[32]{0:T(128)S(1)}, f32[32]{0:T(128)S(1)}, f32[32]{0:T(128)S(1)}, f32[32]{0:T(128)S(1)}, f32[32]{0:T(128)S(1)}, /*index=5*/f32[32]{0:T(128)S(1)}, f32[32]{0:T(128)S(1)}, f32[32]{0:T(128)S(1)}, f32[32]{0:T(128)S(1)}) fusion(f32[3,3,256]{2,1,0:T(4,128)} %taps_ref.1, s32[]{:T(128)S(6)} %select_n.43, s32[]{:T(128)S(6)} %add.376, s32[]{:T(128)S(6)} %add.375), kind=kLoop, calls=%fused_computation.144 | loop fusion | bytes 2316 | tf_op jit(solution)/shard_map/mul | solution.py:231
  13.3 1.2 %fusion.21 = f32[32,9,512]{2,0,1:T(8,128)S(1)} fusion(bf16[256,512,1]{1,0,2:T(8,128)(2,1)} %constant.156, bf16[4,9,8,256]{3,2,1,0:T(8,128)(2,1)S(1)} %bitcast.107), kind=kOutput, calls=%fused_computation.54 | convolution fusion | flops 75497472 | bytes 999424 | tf_op jit(solution)/shard_map/cnt,tf->cnf/dot_general | solution.py:45
  14.4 0.0 copy-done.1
  14.5 0.2 convolution_add_fusion
  14.7 0.1 fusion.6
  14.8 12.6 %all-to-all-done = bf16[8,65,512]{2,1,0:T(8,128)(2,1)S(1)} async-done(((bf16[8,65,512]{2,1,0:T(8,128)(2,1)}), bf16[8,65,512]{2,1,0:T(8,128)(2,1)S(1)}, u32[]{:S(2)}, u32[]{:S(2)}) %all-to-all-start) | async-done | bytes 532512 | tf_op jit(solution)/shard_map/all_to_all | solution.py:209
  27.4 0.1 convert_add_fusion
  27.5 0.2 subtract_reduce_fusion
  27.7 0.1 iota_compare_fusion.1
  27.8 0.1 copy.45
  27.8 0.1 copy.46
  27.9 0.1 add_add_fusion
  28.0 0.1 copy.44
  28.1 0.1 iota_add_fusion
  28.2 2.5 %fusion.1 = bf16[8,64,512]{2,1,0:T(8,128)(2,1)S(1)} fusion(s32[8,512]{1,0:T(8,128)S(1)} %iota_add_fusion, pred[8,512]{1,0:T(8,128)(4,1)S(1)} %iota_compare_fusion.1, bf16[8,65,512]{2,1,0:T(8,128)(2,1)S(1)} %all-to-all-done), kind=kOutput, calls=%fused_computation.2 | convolution fusion | flops 272629760 | bytes 1069056 | tf_op jit(solution)/shard_map/icr,irj->icj/dot_general | solution.py:223
  30.7 0.0 copy-start.2
  30.7 0.1 reshape.193
  30.9 0.1 compare_and_fusion
  31.0 0.1 convert_reduce_fusion
  31.1 0.1 fusion.50
  31.3 0.1 copy.62
  31.4 0.1 copy.64
  31.5 0.1 copy.63
  31.6 0.1 copy.65
  31.8 0.1 pad_add_fusion
  31.9 0.1 slice_convert_fusion
  32.0 0.3 convolution_bitcast_fusion
  32.2 0.3 convolution_bitcast_fusion.1
  32.5 0.4 slice_select_fusion
  32.9 0.0 copy-done.2
  32.9 0.2 fusion.24
  33.1 0.2 convolution_add_fusion.1
  33.5 0.1 slice_multiply_fusion.20
  33.6 0.1 slice_multiply_fusion.16
  33.7 0.0 copy-start.3
  33.7 0.1 slice_multiply_fusion.12
  33.8 0.2 subtract_select_fusion
  34.0 0.0 copy-start.4
  34.0 0.2 add_select_fusion
  34.2 0.1 pad_maximum_fusion
  34.3 0.4 copy-done.3
  34.7 0.9 %fusion.8 = f32[32,8,256]{2,1,0:T(8,128)S(1)} fusion(f32[512,256,1]{1,0,2:T(8,128)S(1)} %copy-done.3, f32[32,8,512]{2,0,1:T(8,128)S(1)} %pad_maximum_fusion), kind=kOutput, calls=%fused_computation.15 | convolution fusion | flops 402653184 | bytes 1310720 | tf_op jit(solution)/shard_map/cnf,ft->cnt/dot_general | solution.py:288
  35.6 0.1 copy.68
  35.7 0.2 fusion.18
  36.0 10.8 %all_to_all.20 = bf16[1,32,8,256]{3,1,0,2:T(8,128)(2,1)S(1)} all-to-all(bf16[1,32,8,256]{3,1,0,2:T(8,128)(2,1)S(1)} %copy.56), channel_id=1, replica_groups=mesh['ctx'=8,'ch'=4] {'ctx'}, dimensions={2} | all-to-all | bytes 262144 | tf_op jit(solution)/shard_map/all_to_all | solution.py:292
  46.8 7.2 %all_gather.3 = bf16[1024,256]{1,0:T(8,128)(2,1)S(1)} all-gather(bf16[256,256]{1,0:T(8,128)(2,1)S(1)} %bitcast.112), channel_id=1, replica_groups=mesh['ctx'=8,'ch'=4] {'ch'}, dimensions={0}, use_global_device_ids=true | all-gather | bytes 655360 | tf_op jit(solution)/shard_map/all_gather | solution.py:296
  54.0 0.0 copy-done.4
  54.0 1.3 %fusion.5 = bf16[2048,256]{0,1:T(8,128)(2,1)S(1)} fusion(bf16[1024,256]{1,0:T(8,128)(2,1)S(1)} %all_gather.3, bf16[2048,1024]{1,0:T(8,128)(2,1)S(1)} %copy-done.4), kind=kOutput, calls=%fused_computation.8 | convolution fusion | flops 1074266112 | bytes 5767168 | tf_op jit(solution)/shard_map/dot_general | solution.py:294
  55.3 1.3 %copy.57 = bf16[2048,256]{1,0:T(8,128)(2,1)} copy(bf16[2048,256]{0,1:T(8,128)(2,1)S(1)} %fusion.5) | data formatting | bytes 2097152 | tf_op jit(solution)/shard_map/convert_element_type | solution.py:299
  (21 shorter events, 0.4 us)
Async XLA Ops:
  0.0 12.2 %copy-start = (bf16[256,2048]{1,0:T(8,128)(2,1)S(1)}, bf16[256,2048]{1,0:T(8,128)(2,1)}, u32[]{:S(2)}) copy-start(bf16[256,2048]{1,0:T(8,128)(2,1)} %param.12) | copy-start | bytes 3145732
  0.0 14.4 %copy-start.1 = (bf16[256,512,1]{1,0,2:T(8,128)(2,1)S(1)}, bf16[256,512,1]{1,0,2:T(8,128)(2,1)}, u32[]{:S(2)}) copy-start(bf16[256,512,1]{1,0,2:T(8,128)(2,1)} %constant.157) | copy-start | bytes 786436
  4.2 23.1 %all-to-all-start = ((bf16[8,65,512]{2,1,0:T(8,128)(2,1)}), bf16[8,65,512]{2,1,0:T(8,128)(2,1)S(1)}, u32[]{:S(2)}, u32[]{:S(2)}) async-start(bf16[8,65,512]{2,1,0:T(8,128)(2,1)} %shard_map.91), calls=%async_computation | async-start | bytes 1179648 | tf_op jit(solution)/shard_map/all_to_all | solution.py:209
  30.7 2.2 %copy-start.2 = (bf16[256,512,1]{1,0,2:T(8,128)(2,1)S(1)}, bf16[256,512,1]{1,0,2:T(8,128)(2,1)}, u32[]{:S(2)}) copy-start(bf16[256,512,1]{1,0,2:T(8,128)(2,1)} %constant.156) | copy-start | bytes 786436
  33.7 1.0 %copy-start.3 = (f32[512,256,1]{1,0,2:T(8,128)S(1)}, f32[512,256,1]{1,0,2:T(8,128)}, u32[]{:S(2)}) copy-start(f32[512,256,1]{1,0,2:T(8,128)} %constant.158) | copy-start | bytes 1572868
  34.0 20.0 %copy-start.4 = (bf16[2048,1024]{1,0:T(8,128)(2,1)S(1)}, bf16[2048,1024]{1,0:T(8,128)(2,1)}, u32[]{:S(2)}) copy-start(bf16[2048,1024]{1,0:T(8,128)(2,1)} %param.14) | copy-start | bytes 12582916

commit v15 on v12

--- a/solution.py
+++ b/solution.py
@@ -6,6 +6,7 @@
 import ml_dtypes
 import numpy as np
 from jax import lax
+from jax.experimental.layout import Layout, with_layout_constraint
 from jax.experimental import pallas as pl
 from jax.experimental.pallas import tpu as pltpu
 from jax.sharding import PartitionSpec as P
@@ -297,7 +298,7 @@
         lax.all_gather(gated_block, "ch", axis=0, tiled=True),
         preferred_element_type=jnp.float32,
     )
-    return mixed.astype(jnp.bfloat16)
+    return with_layout_constraint(mixed.astype(jnp.bfloat16), Layout((0, 1)))
 
 
 def on_device(arrivals, counts, short_taps, filter_taps, skip_gain, out_weight):

time: 56.5 us -> 56.1 us (level)
  local copies, waits for them, and re-layouts: 4.66 us -> 3.36 us
  matrix products: 7.03 us -> 7.98 us
    convert_element_type x1 -> x0, local copies, waits for them, and re-layouts: 1.31 us -> none  [by_transpose(): return mixed.astype(jnp.bfloat16)]
    dot_general x1, matrix products: 1.3 us -> 2.25 us  [by_transpose(): jnp.dot(out_weight, lax.all_gather(gated_block, 'ch', axis=0, tiled=True)...]
where the time goes in v15:
time: 56.1 us; the launch traced here: 55.8 us
  blocking collectives  18 us (32%)
  waiting for transfers between devices  12.5 us (22%)
  matrix products  7.98 us (14%)
  starting transfers between devices  7.25 us (13%)
  local copies, waits for them, and re-layouts  3.36 us (6%)
  Pallas kernels  2.97 us (5%)
  other arithmetic  2.6 us (5%)
  between operations  1.1 us (2%)
    all_to_all x1, waiting for transfers between devices, by_transpose(): got = lax.all_to_all(payload, 'ctx', 0, 0, tiled=False)  12.5 us
    all_to_all x1, blocking collectives, by_transpose(): lax.all_to_all(gated.reshape(own, n_ctx, T_DEV), 'ctx', 1, 0, tiled=False)  10.8 us
    all_to_all x1, starting transfers between devices, by_transpose(): got = lax.all_to_all(payload, 'ctx', 0, 0, tiled=False)  7.25 us
    all_gather x1, blocking collectives, by_transpose(): lax.all_gather(gated_block, 'ch', axis=0, tiled=True)  7.18 us
    pallas_call x1, Pallas kernels, by_transpose(): pl.pallas_call(functools.partial(sender_kernel, n_ctx=n_ctx, own=own), in...  2.97 us
    dot_general x1, matrix products, by_transpose(): jnp.einsum('icr,irj->icj', rows, select, preferred_element_type=jnp.bfloa...  2.49 us
    dot_general x1, matrix products, by_transpose(): jnp.dot(out_weight, lax.all_gather(gated_block, 'ch', axis=0, tiled=True)...  2.25 us
    dot_general x2, matrix products, transform(): jnp.einsum(spec, blocks, hi, preferred_element_type=jnp.float32)  1.41 us
  transfers between devices with their start and end apart: 1, of which 1 were waited for; matrix products, arithmetic and copies ran while one was open for 6% of the time, Pallas kernels for 0%

profile of v15, /device:TPU:0, one launch (start us, length us, event | category | flops | bytes accessed | tf_op | source)
XLA Modules:
  0.0 55.8 jit_solution(10823340392453144653)
XLA Ops:
  0.0 0.0 copy-start
  0.0 0.0 copy-start.1
  0.8 3.0 %shard_map.91 = bf16[8,65,512]{2,1,0:T(8,128)(2,1)} custom-call(s32[1]{0:T(128)S(6)} %copy.86.count_ref, bf16[3,256,512]{2,1,0:T(8,128)(2,1)} %arrivals_ref.1, f32[3,3,256]{2,1,0:T(4,128)} %taps_ref.1), custom_call_target="tpu_custom_call" | custom-call | tf_op jit(solution)/shard_map/pallas_call | solution.py:201
  3.7 7.3 %all-to-all-start = ((bf16[8,65,512]{2,1,0:T(8,128)(2,1)}), bf16[8,65,512]{2,1,0:T(8,128)(2,1)S(1)}, u32[]{:S(2)}, u32[]{:S(2)}) async-start(bf16[8,65,512]{2,1,0:T(8,128)(2,1)} %shard_map.91), calls=%async_computation | async-start | bytes 1179648 | tf_op jit(solution)/shard_map/all_to_all | solution.py:211
  11.0 0.8 %dynamic_slice.11 = f32[32]{0:T(128)S(1)} dynamic-slice(f32[256]{0:T(256)} %param.13, s32[]{:T(128)S(6)} %select_n.43), dynamic_slice_sizes={32} | dynamic-slice | bytes 260 | tf_op jit(solution)/shard_map/dynamic_slice | solution.py:291
  11.8 0.0 copy-done
  11.8 0.1 pad_add_fusion.3
  11.9 0.9 %fusion.44 = (f32[32]{0:T(128)S(1)}, f32[32]{0:T(128)S(1)}, f32[32]{0:T(128)S(1)}, f32[32]{0:T(128)S(1)}, f32[32]{0:T(128)S(1)}, /*index=5*/f32[32]{0:T(128)S(1)}, f32[32]{0:T(128)S(1)}, f32[32]{0:T(128)S(1)}, f32[32]{0:T(128)S(1)}) fusion(f32[3,3,256]{2,1,0:T(4,128)} %taps_ref.1, s32[]{:T(128)S(6)} %select_n.43, s32[]{:T(128)S(6)} %add.376, s32[]{:T(128)S(6)} %add.375), kind=kLoop, calls=%fused_computation.144 | loop fusion | bytes 2316 | tf_op jit(solution)/shard_map/mul | solution.py:233
  12.8 1.2 %fusion.21 = f32[32,9,512]{2,0,1:T(8,128)S(1)} fusion(bf16[256,512,1]{1,0,2:T(8,128)(2,1)} %constant.156, bf16[4,9,8,256]{3,2,1,0:T(8,128)(2,1)S(1)} %bitcast.107), kind=kOutput, calls=%fused_computation.54 | convolution fusion | flops 75497472 | bytes 999424 | tf_op jit(solution)/shard_map/cnt,tf->cnf/dot_general | solution.py:46
  14.0 0.0 copy-done.1
  14.0 0.2 convolution_add_fusion
  14.3 0.1 fusion.6
  14.3 12.5 %all-to-all-done = bf16[8,65,512]{2,1,0:T(8,128)(2,1)S(1)} async-done(((bf16[8,65,512]{2,1,0:T(8,128)(2,1)}), bf16[8,65,512]{2,1,0:T(8,128)(2,1)S(1)}, u32[]{:S(2)}, u32[]{:S(2)}) %all-to-all-start) | async-done | bytes 532512 | tf_op jit(solution)/shard_map/all_to_all | solution.py:211
  26.9 0.1 convert_add_fusion
  27.0 0.2 subtract_reduce_fusion
  27.2 0.1 iota_compare_fusion.1
  27.3 0.1 copy.42
  27.4 0.1 copy.43
  27.5 0.1 add_add_fusion
  27.5 0.1 copy.41
  27.6 0.1 iota_add_fusion
  27.7 2.5 %fusion.1 = bf16[8,64,512]{2,1,0:T(8,128)(2,1)S(1)} fusion(s32[8,512]{1,0:T(8,128)S(1)} %iota_add_fusion, pred[8,512]{1,0:T(8,128)(4,1)S(1)} %iota_compare_fusion.1, bf16[8,65,512]{2,1,0:T(8,128)(2,1)S(1)} %all-to-all-done), kind=kOutput, calls=%fused_computation.2 | convolution fusion | flops 272629760 | bytes 1069056 | tf_op jit(solution)/shard_map/icr,irj->icj/dot_general | solution.py:225
  30.2 0.0 copy-start.2
  30.3 0.1 reshape.193
  30.4 0.1 compare_and_fusion
  30.5 0.1 convert_reduce_fusion
  30.7 0.1 fusion.50
  30.8 0.1 copy.58
  30.9 0.1 copy.60
  31.0 0.1 copy.59
  31.2 0.1 copy.61
  31.3 0.1 pad_add_fusion
  31.4 0.1 slice_convert_fusion
  31.5 0.3 convolution_bitcast_fusion
  31.8 0.3 convolution_bitcast_fusion.1
  32.0 0.4 slice_select_fusion
  32.4 0.0 copy-done.2
  32.4 0.2 fusion.24
  32.7 0.2 convolution_add_fusion.1
  33.1 0.1 slice_multiply_fusion.20
  33.1 0.1 slice_multiply_fusion.16
  33.2 0.0 copy-start.3
  33.2 0.1 slice_multiply_fusion.12
  33.3 0.2 subtract_select_fusion
  33.5 0.0 copy-start.4
  33.6 0.2 add_select_fusion
  33.8 0.1 pad_maximum_fusion
  33.8 0.4 copy-done.3
  34.3 0.9 %fusion.8 = f32[32,8,256]{2,1,0:T(8,128)S(1)} fusion(f32[512,256,1]{1,0,2:T(8,128)S(1)} %copy-done.3, f32[32,8,512]{2,0,1:T(8,128)S(1)} %pad_maximum_fusion), kind=kOutput, calls=%fused_computation.15 | convolution fusion | flops 402653184 | bytes 1310720 | tf_op jit(solution)/shard_map/cnf,ft->cnt/dot_general | solution.py:290
  35.1 0.1 copy.64
  35.2 0.2 fusion.18
  35.5 10.8 %all_to_all.20 = bf16[1,32,8,256]{3,1,0,2:T(8,128)(2,1)S(1)} all-to-all(bf16[1,32,8,256]{3,1,0,2:T(8,128)(2,1)S(1)} %copy.53), channel_id=1, replica_groups=mesh['ctx'=8,'ch'=4] {'ctx'}, dimensions={2} | all-to-all | bytes 262144 | tf_op jit(solution)/shard_map/all_to_all | solution.py:294
  46.3 7.2 %all_gather.3 = bf16[1024,256]{1,0:T(8,128)(2,1)S(1)} all-gather(bf16[256,256]{1,0:T(8,128)(2,1)S(1)} %bitcast.112), channel_id=1, replica_groups=mesh['ctx'=8,'ch'=4] {'ch'}, dimensions={0}, use_global_device_ids=true | all-gather | bytes 655360 | tf_op jit(solution)/shard_map/all_gather | solution.py:298
  53.5 0.0 copy-done.4
  53.5 2.3 %fusion.5 = bf16[2048,256]{1,0:T(8,128)(2,1)} fusion(bf16[2048,1024]{1,0:T(8,128)(2,1)S(1)} %copy-done.4, bf16[1024,256]{1,0:T(8,128)(2,1)S(1)} %all_gather.3), kind=kOutput, calls=%fused_computation.8 | convolution fusion | flops 1074266112 | bytes 5767168 | tf_op jit(solution)/shard_map/dot_general | solution.py:296
  (21 shorter events, 0.4 us)
Async XLA Ops:
  0.0 11.8 %copy-start = (bf16[256,2048]{1,0:T(8,128)(2,1)S(1)}, bf16[256,2048]{1,0:T(8,128)(2,1)}, u32[]{:S(2)}) copy-start(bf16[256,2048]{1,0:T(8,128)(2,1)} %param.12) | copy-start | bytes 3145732
  0.0 14.0 %copy-start.1 = (bf16[256,512,1]{1,0,2:T(8,128)(2,1)S(1)}, bf16[256,512,1]{1,0,2:T(8,128)(2,1)}, u32[]{:S(2)}) copy-start(bf16[256,512,1]{1,0,2:T(8,128)(2,1)} %constant.157) | copy-start | bytes 786436
  3.7 23.1 %all-to-all-start = ((bf16[8,65,512]{2,1,0:T(8,128)(2,1)}), bf16[8,65,512]{2,1,0:T(8,128)(2,1)S(1)}, u32[]{:S(2)}, u32[]{:S(2)}) async-start(bf16[8,65,512]{2,1,0:T(8,128)(2,1)} %shard_map.91), calls=%async_computation | async-start | bytes 1179648 | tf_op jit(solution)/shard_map/all_to_all | solution.py:211
  30.2 2.2 %copy-start.2 = (bf16[256,512,1]{1,0,2:T(8,128)(2,1)S(1)}, bf16[256,512,1]{1,0,2:T(8,128)(2,1)}, u32[]{:S(2)}) copy-start(bf16[256,512,1]{1,0,2:T(8,128)(2,1)} %constant.156) | copy-start | bytes 786436
  33.2 1.0 %copy-start.3 = (f32[512,256,1]{1,0,2:T(8,128)S(1)}, f32[512,256,1]{1,0,2:T(8,128)}, u32[]{:S(2)}) copy-start(f32[512,256,1]{1,0,2:T(8,128)} %constant.158) | copy-start | bytes 1572868
  33.5 20.0 %copy-start.4 = (bf16[2048,1024]{1,0:T(8,128)(2,1)S(1)}, bf16[2048,1024]{1,0:T(8,128)(2,1)}, u32[]{:S(2)}) copy-start(bf16[2048,1024]{1,0:T(8,128)(2,1)} %param.14) | copy-start | bytes 12582916

commit v16 on v15

--- a/solution.py
+++ b/solution.py
@@ -243,20 +243,21 @@
     valid = jnp.concatenate([at_row[:, :2] < count_col, at_row[:, 2:] >= 2], axis=1)
     spot = offsets[:, None] + at_row
     slot = jnp.arange(length + 2, dtype=jnp.int32)[None, None, :]
-    marks = ((slot - 2 == spot[:, :, None]) & valid[:, :, None]).astype(jnp.bfloat16)
+    marks = (slot - 2 == spot[:, :, None]) & valid[:, :, None]
+    slots = np.arange(8)
+    spot8 = jnp.concatenate([spot[:, :2], spot[:, :2], spot[:, 2:], spot[:, 2:]], axis=1)
+    valid8 = jnp.concatenate([valid[:, :2], valid[:, :2], valid[:, 2:], valid[:, 2:]], axis=1)
+    by_slot = (slot - 2 == spot8[:, :, None]) & valid8[:, :, None]
+    belongs = jnp.asarray((slots // 2) % 2 == np.arange(2)[:, None])
+    spread = (by_slot[:, :, None, :] & belongs.T[None, :, :, None]).astype(jnp.bfloat16)
+    around = jnp.einsum("ics,ispj->pcj", values, spread, preferred_element_type=jnp.float32)
     near_in = []
     for part in range(2):
-        pick = jnp.concatenate(
-            [values[:, :, 2 * part : 2 * part + 2], values[:, :, 4 + 2 * part : 6 + 2 * part]], axis=2
-        )
-        around = jnp.einsum(
-            "ics,isj->cj", pick, marks, preferred_element_type=jnp.float32
-        )
-        s = taps[1 + part, 0, :, None] * around[:, 2:]
-        s = s + taps[1 + part, 1, :, None] * around[:, 1:-1]
-        s = s + taps[1 + part, 2, :, None] * around[:, :-2]
+        s = taps[1 + part, 0, :, None] * around[part, :, 2:]
+        s = s + taps[1 + part, 1, :, None] * around[part, :, 1:-1]
+        s = s + taps[1 + part, 2, :, None] * around[part, :, :-2]
         near_in.append(s)
-    at_start = jnp.sum(marks[:, :2, 2:].astype(jnp.float32), axis=(0, 1)) > 0
+    at_start = jnp.any(marks[:, :2, 2:], axis=(0, 1))
     mixed_input = jnp.where(
         at_start[None, :], (near_in[0] * near_in[1]).astype(jnp.bfloat16), from_senders
     )

time: 56.1 us -> 55.6 us (level)
  no operation moved by 1% of the time
where the time goes in v16:
time: 55.6 us; the launch traced here: 55.3 us
  blocking collectives  18 us (32%)
  waiting for transfers between devices  12.5 us (22%)
  matrix products  7.82 us (14%)
  starting transfers between devices  7.25 us (13%)
  Pallas kernels  2.97 us (5%)
  local copies, waits for them, and re-layouts  2.89 us (5%)
  other arithmetic  2.82 us (5%)
  between operations  1.07 us (2%)
    all_to_all x1, waiting for transfers between devices, by_transpose(): got = lax.all_to_all(payload, 'ctx', 0, 0, tiled=False)  12.5 us
    all_to_all x1, blocking collectives, by_transpose(): lax.all_to_all(gated.reshape(own, n_ctx, T_DEV), 'ctx', 1, 0, tiled=False)  10.8 us
    all_to_all x1, starting transfers between devices, by_transpose(): got = lax.all_to_all(payload, 'ctx', 0, 0, tiled=False)  7.25 us
    all_gather x1, blocking collectives, by_transpose(): lax.all_gather(gated_block, 'ch', axis=0, tiled=True)  7.18 us
    pallas_call x1, Pallas kernels, by_transpose(): pl.pallas_call(functools.partial(sender_kernel, n_ctx=n_ctx, own=own), in...  2.97 us
    dot_general x1, matrix products, by_transpose(): jnp.einsum('icr,irj->icj', rows, select, preferred_element_type=jnp.bfloa...  2.5 us
    dot_general x1, matrix products, by_transpose(): jnp.dot(out_weight, lax.all_gather(gated_block, 'ch', axis=0, tiled=True)...  2.25 us
    dot_general x2, matrix products, transform(): jnp.einsum(spec, blocks, hi, preferred_element_type=jnp.float32)  1.4 us
  transfers between devices with their start and end apart: 1, of which 1 were waited for; matrix products, arithmetic and copies ran while one was open for 6% of the time, Pallas kernels for 0%

profile of v16, /device:TPU:0, one launch (start us, length us, event | category | flops | bytes accessed | tf_op | source)
XLA Modules:
  0.0 55.3 jit_solution(2796937361751792145)
XLA Ops:
  0.0 0.0 copy-start
  0.0 0.0 copy-start.1
  0.8 3.0 %shard_map.100 = bf16[8,65,512]{2,1,0:T(8,128)(2,1)} custom-call(s32[1]{0:T(128)S(6)} %copy.79.count_ref, bf16[3,256,512]{2,1,0:T(8,128)(2,1)} %arrivals_ref.1, f32[3,3,256]{2,1,0:T(4,128)} %taps_ref.1), custom_call_target="tpu_custom_call" | custom-call | tf_op jit(solution)/shard_map/pallas_call | solution.py:201
  3.7 7.3 %all-to-all-start = ((bf16[8,65,512]{2,1,0:T(8,128)(2,1)}), bf16[8,65,512]{2,1,0:T(8,128)(2,1)S(1)}, u32[]{:S(2)}, u32[]{:S(2)}) async-start(bf16[8,65,512]{2,1,0:T(8,128)(2,1)} %shard_map.100), calls=%async_computation | async-start | bytes 1179648 | tf_op jit(solution)/shard_map/all_to_all | solution.py:211
  11.0 0.1 pad.175.clone
  11.1 0.1 slice.365
  11.2 0.8 %dynamic_slice.11 = f32[32]{0:T(128)S(1)} dynamic-slice(f32[256]{0:T(256)} %param.14, s32[]{:T(128)S(6)} %select_n.43), dynamic_slice_sizes={32} | dynamic-slice | bytes 260 | tf_op jit(solution)/shard_map/dynamic_slice | solution.py:292
  11.9 0.0 copy-done
  11.9 0.9 %fusion.50 = (f32[32]{0:T(128)S(1)}, f32[32]{0:T(128)S(1)}, f32[32]{0:T(128)S(1)}, f32[32]{0:T(128)S(1)}, f32[32]{0:T(128)S(1)}, /*index=5*/f32[32]{0:T(128)S(1)}, f32[32]{0:T(128)S(1)}, f32[32]{0:T(128)S(1)}, f32[32]{0:T(128)S(1)}) fusion(f32[3,3,256]{2,1,0:T(4,128)} %taps_ref.1, s32[]{:T(128)S(6)} %select_n.43, s32[]{:T(128)S(6)} %add.382, s32[]{:T(128)S(6)} %add.381), kind=kLoop, calls=%fused_computation.149 | loop fusion | bytes 2316 | tf_op jit(solution)/shard_map/mul | solution.py:233
  12.9 1.2 %fusion.30 = f32[32,9,512]{2,0,1:T(8,128)S(1)} fusion(bf16[256,512,1]{1,0,2:T(8,128)(2,1)} %constant.160, bf16[4,9,8,256]{3,2,1,0:T(8,128)(2,1)S(1)} %bitcast.169), kind=kOutput, calls=%fused_computation.62 | convolution fusion | flops 75497472 | bytes 999424 | tf_op jit(solution)/shard_map/cnt,tf->cnf/dot_general | solution.py:46
  14.1 0.0 copy-done.1
  14.1 0.2 convolution_add_fusion
  14.3 0.1 fusion.9
  14.4 12.5 %all-to-all-done = bf16[8,65,512]{2,1,0:T(8,128)(2,1)S(1)} async-done(((bf16[8,65,512]{2,1,0:T(8,128)(2,1)}), bf16[8,65,512]{2,1,0:T(8,128)(2,1)S(1)}, u32[]{:S(2)}, u32[]{:S(2)}) %all-to-all-start) | async-done | bytes 532512 | tf_op jit(solution)/shard_map/all_to_all | solution.py:211
  26.9 0.1 convert_add_fusion
  27.0 0.2 subtract_reduce_fusion
  27.2 0.1 add_compare_fusion
  27.3 0.1 pad_add_fusion.4
  27.4 0.1 pad_add_fusion.3
  27.5 0.1 iota_compare_fusion.1
  27.6 0.1 copy.77
  27.7 0.1 add_add_fusion
  27.7 0.1 fusion.52
  27.8 0.1 copy.76
  27.9 0.1 pad_add_fusion.2
  28.0 0.0 copy-start.5
  28.0 0.1 iota_add_fusion
  28.0 2.5 %fusion.1 = bf16[8,64,512]{2,1,0:T(8,128)(2,1)S(1)} fusion(s32[8,512]{1,0:T(8,128)S(1)} %iota_add_fusion, pred[8,512]{1,0:T(8,128)(4,1)S(1)} %iota_compare_fusion.1, bf16[8,65,512]{2,1,0:T(8,128)(2,1)S(1)} %all-to-all-done), kind=kOutput, calls=%fused_computation.2 | convolution fusion | flops 272629760 | bytes 1069056 | tf_op jit(solution)/shard_map/icr,irj->icj/dot_general | solution.py:225
  30.5 0.0 copy-start.2
  30.6 0.1 reshape.195
  30.7 0.1 pad_add_fusion
  30.8 0.1 slice_convert_fusion
  30.9 0.2 compare_and_fusion
  31.1 0.1 and_reduce_fusion
  31.2 0.0 copy-done.5
  31.2 0.4 convolution_bitcast_fusion
  31.5 0.4 slice_select_fusion
  31.9 0.0 copy-done.2
  31.9 0.2 fusion.33
  32.2 0.2 convolution_add_fusion.1
  32.6 0.1 slice_multiply_fusion.14
  32.6 0.1 slice_multiply_fusion.10
  32.7 0.0 copy-start.3
  32.7 0.1 slice_multiply_fusion.6
  32.8 0.2 subtract_select_fusion
  33.0 0.0 copy-start.4
  33.1 0.2 add_select_fusion
  33.3 0.1 pad_maximum_fusion
  33.3 0.4 copy-done.3
  33.8 0.9 %fusion.11 = f32[32,8,256]{2,1,0:T(8,128)S(1)} fusion(f32[512,256,1]{1,0,2:T(8,128)S(1)} %copy-done.3, f32[32,8,512]{2,0,1:T(8,128)S(1)} %pad_maximum_fusion), kind=kOutput, calls=%fused_computation.18 | convolution fusion | flops 402653184 | bytes 1310720 | tf_op jit(solution)/shard_map/cnf,ft->cnt/dot_general | solution.py:291
  34.6 0.1 copy.55
  34.7 0.2 fusion.27
  35.0 10.8 %all_to_all.20 = bf16[1,32,8,256]{3,1,0,2:T(8,128)(2,1)S(1)} all-to-all(bf16[1,32,8,256]{3,1,0,2:T(8,128)(2,1)S(1)} %copy.45), channel_id=1, replica_groups=mesh['ctx'=8,'ch'=4] {'ctx'}, dimensions={2} | all-to-all | bytes 262144 | tf_op jit(solution)/shard_map/all_to_all | solution.py:295
  45.8 7.2 %all_gather.3 = bf16[1024,256]{1,0:T(8,128)(2,1)S(1)} all-gather(bf16[256,256]{1,0:T(8,128)(2,1)S(1)} %bitcast.174), channel_id=1, replica_groups=mesh['ctx'=8,'ch'=4] {'ch'}, dimensions={0}, use_global_device_ids=true | all-gather | bytes 655360 | tf_op jit(solution)/shard_map/all_gather | solution.py:299
  53.0 0.0 copy-done.4
  53.0 2.2 %fusion.5 = bf16[2048,256]{1,0:T(8,128)(2,1)} fusion(bf16[2048,1024]{1,0:T(8,128)(2,1)S(1)} %copy-done.4, bf16[1024,256]{1,0:T(8,128)(2,1)S(1)} %all_gather.3), kind=kOutput, calls=%fused_computation.7 | convolution fusion | flops 1074266112 | bytes 5767168 | tf_op jit(solution)/shard_map/dot_general | solution.py:297
  (19 shorter events, 0.3 us)
Async XLA Ops:
  0.0 11.9 %copy-start = (bf16[256,2048]{1,0:T(8,128)(2,1)S(1)}, bf16[256,2048]{1,0:T(8,128)(2,1)}, u32[]{:S(2)}) copy-start(bf16[256,2048]{1,0:T(8,128)(2,1)} %param.13) | copy-start | bytes 3145732
  0.0 14.1 %copy-start.1 = (bf16[256,512,1]{1,0,2:T(8,128)(2,1)S(1)}, bf16[256,512,1]{1,0,2:T(8,128)(2,1)}, u32[]{:S(2)}) copy-start(bf16[256,512,1]{1,0,2:T(8,128)(2,1)} %constant.161) | copy-start | bytes 786436
  3.7 23.1 %all-to-all-start = ((bf16[8,65,512]{2,1,0:T(8,128)(2,1)}), bf16[8,65,512]{2,1,0:T(8,128)(2,1)S(1)}, u32[]{:S(2)}, u32[]{:S(2)}) async-start(bf16[8,65,512]{2,1,0:T(8,128)(2,1)} %shard_map.100), calls=%async_computation | async-start | bytes 1179648 | tf_op jit(solution)/shard_map/all_to_all | solution.py:211
  28.0 3.2 %copy-start.5 = (pred[8,2]{0,1:T(4,128)(4,1)S(1)}, pred[8,2]{0,1:T(4,128)(4,1)}, u32[]{:S(2)}) copy-start(pred[8,2]{0,1:T(4,128)(4,1)} %constant.159) | copy-start | bytes 52
  30.5 1.4 %copy-start.2 = (bf16[256,512,1]{1,0,2:T(8,128)(2,1)S(1)}, bf16[256,512,1]{1,0,2:T(8,128)(2,1)}, u32[]{:S(2)}) copy-start(bf16[256,512,1]{1,0,2:T(8,128)(2,1)} %constant.160) | copy-start | bytes 786436
  32.7 1.0 %copy-start.3 = (f32[512,256,1]{1,0,2:T(8,128)S(1)}, f32[512,256,1]{1,0,2:T(8,128)}, u32[]{:S(2)}) copy-start(f32[512,256,1]{1,0,2:T(8,128)} %constant.162) | copy-start | bytes 1572868
  33.0 20.0 %copy-start.4 = (bf16[2048,1024]{1,0:T(8,128)(2,1)S(1)}, bf16[2048,1024]{1,0:T(8,128)(2,1)}, u32[]{:S(2)}) copy-start(bf16[2048,1024]{1,0:T(8,128)(2,1)} %param.15) | copy-start | bytes 12582916

commit v17 on v16

--- a/solution.py
+++ b/solution.py
@@ -153,24 +153,29 @@
         spread = jnp.where(diagonal, taps_ref[part, k : k + 1, :], 0.0)
         return jnp.sum(spread, axis=1, keepdims=True)
 
-    near = []
     edge = jnp.where(column[:1] == 8, (count // 16).astype(jnp.float32), 0.0)
     edge = jnp.where(column[:1] == 9, (count % 16).astype(jnp.float32), edge)
+    columns = []
     for part in range(2):
-        raw = arrivals_ref[1 + part]
-        x = raw.astype(jnp.float32)
-        back1 = jnp.where(lane >= 1, pltpu.roll(x, 1, 1), 0.0)
-        back2 = jnp.where(lane >= 2, pltpu.roll(x, 2, 1), 0.0)
-        s = tap(1 + part, 0) * x
-        s = s + tap(1 + part, 1) * back1
-        s = s + tap(1 + part, 2) * back2
-        near.append(s)
         wanted = jnp.where(column >= 4, count - 2 + column - 4 - 2 * part, column - 2 * part)
         inside = (column % 4 >= 2 * part) & (column % 4 < 2 * part + 2) & (column < 8)
         pick = ((row == wanted) & inside).astype(jnp.bfloat16)
-        edge = edge + jnp.dot(raw, pick, preferred_element_type=jnp.float32)
-    mixed = (near[0] * near[1]).astype(jnp.bfloat16)
+        edge = edge + jnp.dot(arrivals_ref[1 + part], pick, preferred_element_type=jnp.float32)
+        columns.append([tap(1 + part, k) for k in range(3)])
     edge = edge.astype(jnp.bfloat16)
+    block_lane = lane[:own]
+    for j in range(n_ctx):
+        rows = slice(j * own, (j + 1) * own)
+        near = []
+        for part in range(2):
+            x = arrivals_ref[1 + part, rows, :].astype(jnp.float32)
+            back1 = jnp.where(block_lane >= 1, pltpu.roll(x, 1, 1), 0.0)
+            back2 = jnp.where(block_lane >= 2, pltpu.roll(x, 2, 1), 0.0)
+            s = columns[part][0][rows] * x
+            s = s + columns[part][1][rows] * back1
+            s = s + columns[part][2][rows] * back2
+            near.append(s)
+        out_ref[j, own : 2 * own, :] = (near[0] * near[1]).astype(jnp.bfloat16)
     flat_lane = lax.broadcasted_iota(jnp.int32, (EDGE, capacity), 1)
     spread = (
         (flat_lane < 8 * own) & (flat_lane % 8 == lax.broadcasted_iota(jnp.int32, (EDGE, capacity), 0))
@@ -182,7 +187,6 @@
     for j in range(n_ctx):
         rows = slice(j * own, (j + 1) * own)
         out_ref[j, :own, :] = arrivals_ref[0, rows, :]
-        out_ref[j, own : 2 * own, :] = mixed[rows]
         tiled = jnp.dot(edge[rows], spread, preferred_element_type=jnp.float32)
         flat = jnp.sum(jnp.where(lane_out // 8 == channel, tiled, 0.0), axis=0, keepdims=True)
         out_ref[j, 2 * own : 2 * own + 1, :] = (flat + code).astype(jnp.bfloat16)

time: 55.6 us -> 55.4 us (level)
  no operation moved by 1% of the time
where the time goes in v17:
time: 55.4 us; the launch traced here: 55 us
  blocking collectives  18 us (32%)
  waiting for transfers between devices  12.5 us (23%)
  matrix products  7.81 us (14%)
  starting transfers between devices  7.24 us (13%)
  local copies, waits for them, and re-layouts  2.89 us (5%)
  other arithmetic  2.82 us (5%)
  Pallas kernels  2.74 us (5%)
  between operations  1.07 us (2%)
    all_to_all x1, waiting for transfers between devices, by_transpose(): got = lax.all_to_all(payload, 'ctx', 0, 0, tiled=False)  12.5 us
    all_to_all x1, blocking collectives, by_transpose(): lax.all_to_all(gated.reshape(own, n_ctx, T_DEV), 'ctx', 1, 0, tiled=False)  10.8 us
    all_to_all x1, starting transfers between devices, by_transpose(): got = lax.all_to_all(payload, 'ctx', 0, 0, tiled=False)  7.24 us
    all_gather x1, blocking collectives, by_transpose(): lax.all_gather(gated_block, 'ch', axis=0, tiled=True)  7.18 us
    pallas_call x1, Pallas kernels, by_transpose(): pl.pallas_call(functools.partial(sender_kernel, n_ctx=n_ctx, own=own), in...  2.74 us
    dot_general x1, matrix products, by_transpose(): jnp.einsum('icr,irj->icj', rows, select, preferred_element_type=jnp.bfloa...  2.49 us
    dot_general x1, matrix products, by_transpose(): jnp.dot(out_weight, lax.all_gather(gated_block, 'ch', axis=0, tiled=True)...  2.25 us
    dot_general x2, matrix products, transform(): jnp.einsum(spec, blocks, hi, preferred_element_type=jnp.float32)  1.39 us
  transfers between devices with their start and end apart: 1, of which 1 were waited for; matrix products, arithmetic and copies ran while one was open for 6% of the time, Pallas kernels for 0%

profile of v17, /device:TPU:0, one launch (start us, length us, event | category | flops | bytes accessed | tf_op | source)
XLA Modules:
  0.0 55.0 jit_solution(5428871930211544886)
XLA Ops:
  0.0 0.0 copy-start
  0.0 0.0 copy-start.1
  0.8 2.7 %shard_map.100 = bf16[8,65,512]{2,1,0:T(8,128)(2,1)} custom-call(s32[1]{0:T(128)S(6)} %copy.79.count_ref, bf16[3,256,512]{2,1,0:T(8,128)(2,1)} %arrivals_ref.1, f32[3,3,256]{2,1,0:T(4,128)} %taps_ref.1), custom_call_target="tpu_custom_call" | custom-call | tf_op jit(solution)/shard_map/pallas_call | solution.py:205
  3.5 7.2 %all-to-all-start = ((bf16[8,65,512]{2,1,0:T(8,128)(2,1)}), bf16[8,65,512]{2,1,0:T(8,128)(2,1)S(1)}, u32[]{:S(2)}, u32[]{:S(2)}) async-start(bf16[8,65,512]{2,1,0:T(8,128)(2,1)} %shard_map.100), calls=%async_computation | async-start | bytes 1179648 | tf_op jit(solution)/shard_map/all_to_all | solution.py:215
  10.8 0.1 pad.175.clone
  10.8 0.1 slice.365
  10.9 0.8 %dynamic_slice.11 = f32[32]{0:T(128)S(1)} dynamic-slice(f32[256]{0:T(256)} %param.14, s32[]{:T(128)S(6)} %select_n.43), dynamic_slice_sizes={32} | dynamic-slice | bytes 260 | tf_op jit(solution)/shard_map/dynamic_slice | solution.py:296
  11.7 0.0 copy-done
  11.7 0.9 %fusion.50 = (f32[32]{0:T(128)S(1)}, f32[32]{0:T(128)S(1)}, f32[32]{0:T(128)S(1)}, f32[32]{0:T(128)S(1)}, f32[32]{0:T(128)S(1)}, /*index=5*/f32[32]{0:T(128)S(1)}, f32[32]{0:T(128)S(1)}, f32[32]{0:T(128)S(1)}, f32[32]{0:T(128)S(1)}) fusion(f32[3,3,256]{2,1,0:T(4,128)} %taps_ref.1, s32[]{:T(128)S(6)} %select_n.43, s32[]{:T(128)S(6)} %add.382, s32[]{:T(128)S(6)} %add.381), kind=kLoop, calls=%fused_computation.149 | loop fusion | bytes 2316 | tf_op jit(solution)/shard_map/mul | solution.py:237
  12.6 1.2 %fusion.30 = f32[32,9,512]{2,0,1:T(8,128)S(1)} fusion(bf16[256,512,1]{1,0,2:T(8,128)(2,1)} %constant.160, bf16[4,9,8,256]{3,2,1,0:T(8,128)(2,1)S(1)} %bitcast.169), kind=kOutput, calls=%fused_computation.62 | convolution fusion | flops 75497472 | bytes 999424 | tf_op jit(solution)/shard_map/cnt,tf->cnf/dot_general | solution.py:46
  13.8 0.0 copy-done.1
  13.8 0.2 convolution_add_fusion
  14.1 0.1 fusion.9
  14.2 12.5 %all-to-all-done = bf16[8,65,512]{2,1,0:T(8,128)(2,1)S(1)} async-done(((bf16[8,65,512]{2,1,0:T(8,128)(2,1)}), bf16[8,65,512]{2,1,0:T(8,128)(2,1)S(1)}, u32[]{:S(2)}, u32[]{:S(2)}) %all-to-all-start) | async-done | bytes 532512 | tf_op jit(solution)/shard_map/all_to_all | solution.py:215
  26.7 0.1 convert_add_fusion
  26.8 0.2 subtract_reduce_fusion
  27.0 0.1 add_compare_fusion
  27.1 0.1 pad_add_fusion.4
  27.2 0.1 pad_add_fusion.3
  27.2 0.1 iota_compare_fusion.1
  27.3 0.1 copy.77
  27.4 0.1 add_add_fusion
  27.5 0.1 fusion.52
  27.6 0.1 copy.76
  27.6 0.1 pad_add_fusion.2
  27.7 0.0 copy-start.5
  27.7 0.1 iota_add_fusion
  27.8 2.5 %fusion.1 = bf16[8,64,512]{2,1,0:T(8,128)(2,1)S(1)} fusion(s32[8,512]{1,0:T(8,128)S(1)} %iota_add_fusion, pred[8,512]{1,0:T(8,128)(4,1)S(1)} %iota_compare_fusion.1, bf16[8,65,512]{2,1,0:T(8,128)(2,1)S(1)} %all-to-all-done), kind=kOutput, calls=%fused_computation.2 | convolution fusion | flops 272629760 | bytes 1069056 | tf_op jit(solution)/shard_map/icr,irj->icj/dot_general | solution.py:229
  30.3 0.0 copy-start.2
  30.3 0.1 reshape.195
  30.5 0.1 pad_add_fusion
  30.5 0.1 slice_convert_fusion
  30.6 0.2 compare_and_fusion
  30.8 0.1 and_reduce_fusion
  30.9 0.0 copy-done.5
  30.9 0.4 convolution_bitcast_fusion
  31.3 0.4 slice_select_fusion
  31.7 0.0 copy-done.2
  31.7 0.2 fusion.33
  31.9 0.2 convolution_add_fusion.1
  32.3 0.1 slice_multiply_fusion.14
  32.4 0.1 slice_multiply_fusion.10
  32.5 0.0 copy-start.3
  32.5 0.1 slice_multiply_fusion.6
  32.6 0.2 subtract_select_fusion
  32.8 0.0 copy-start.4
  32.8 0.2 add_select_fusion
  33.0 0.1 pad_maximum_fusion
  33.1 0.4 copy-done.3
  33.5 0.9 %fusion.11 = f32[32,8,256]{2,1,0:T(8,128)S(1)} fusion(f32[512,256,1]{1,0,2:T(8,128)S(1)} %copy-done.3, f32[32,8,512]{2,0,1:T(8,128)S(1)} %pad_maximum_fusion), kind=kOutput, calls=%fused_computation.18 | convolution fusion | flops 402653184 | bytes 1310720 | tf_op jit(solution)/shard_map/cnf,ft->cnt/dot_general | solution.py:295
  34.4 0.1 copy.55
  34.5 0.2 fusion.27
  34.8 10.8 %all_to_all.20 = bf16[1,32,8,256]{3,1,0,2:T(8,128)(2,1)S(1)} all-to-all(bf16[1,32,8,256]{3,1,0,2:T(8,128)(2,1)S(1)} %copy.45), channel_id=1, replica_groups=mesh['ctx'=8,'ch'=4] {'ctx'}, dimensions={2} | all-to-all | bytes 262144 | tf_op jit(solution)/shard_map/all_to_all | solution.py:299
  45.6 7.2 %all_gather.3 = bf16[1024,256]{1,0:T(8,128)(2,1)S(1)} all-gather(bf16[256,256]{1,0:T(8,128)(2,1)S(1)} %bitcast.174), channel_id=1, replica_groups=mesh['ctx'=8,'ch'=4] {'ch'}, dimensions={0}, use_global_device_ids=true | all-gather | bytes 655360 | tf_op jit(solution)/shard_map/all_gather | solution.py:303
  52.8 0.0 copy-done.4
  52.8 2.2 %fusion.5 = bf16[2048,256]{1,0:T(8,128)(2,1)} fusion(bf16[2048,1024]{1,0:T(8,128)(2,1)S(1)} %copy-done.4, bf16[1024,256]{1,0:T(8,128)(2,1)S(1)} %all_gather.3), kind=kOutput, calls=%fused_computation.7 | convolution fusion | flops 1074266112 | bytes 5767168 | tf_op jit(solution)/shard_map/dot_general | solution.py:301
  (19 shorter events, 0.3 us)
Async XLA Ops:
  0.0 11.7 %copy-start = (bf16[256,2048]{1,0:T(8,128)(2,1)S(1)}, bf16[256,2048]{1,0:T(8,128)(2,1)}, u32[]{:S(2)}) copy-start(bf16[256,2048]{1,0:T(8,128)(2,1)} %param.13) | copy-start | bytes 3145732
  0.0 13.8 %copy-start.1 = (bf16[256,512,1]{1,0,2:T(8,128)(2,1)S(1)}, bf16[256,512,1]{1,0,2:T(8,128)(2,1)}, u32[]{:S(2)}) copy-start(bf16[256,512,1]{1,0,2:T(8,128)(2,1)} %constant.161) | copy-start | bytes 786436
  3.5 23.1 %all-to-all-start = ((bf16[8,65,512]{2,1,0:T(8,128)(2,1)}), bf16[8,65,512]{2,1,0:T(8,128)(2,1)S(1)}, u32[]{:S(2)}, u32[]{:S(2)}) async-start(bf16[8,65,512]{2,1,0:T(8,128)(2,1)} %shard_map.100), calls=%async_computation | async-start | bytes 1179648 | tf_op jit(solution)/shard_map/all_to_all | solution.py:215
  27.7 3.2 %copy-start.5 = (pred[8,2]{0,1:T(4,128)(4,1)S(1)}, pred[8,2]{0,1:T(4,128)(4,1)}, u32[]{:S(2)}) copy-start(pred[8,2]{0,1:T(4,128)(4,1)} %constant.159) | copy-start | bytes 52
  30.3 1.4 %copy-start.2 = (bf16[256,512,1]{1,0,2:T(8,128)(2,1)S(1)}, bf16[256,512,1]{1,0,2:T(8,128)(2,1)}, u32[]{:S(2)}) copy-start(bf16[256,512,1]{1,0,2:T(8,128)(2,1)} %constant.160) | copy-start | bytes 786436
  32.5 1.0 %copy-start.3 = (f32[512,256,1]{1,0,2:T(8,128)S(1)}, f32[512,256,1]{1,0,2:T(8,128)}, u32[]{:S(2)}) copy-start(f32[512,256,1]{1,0,2:T(8,128)} %constant.162) | copy-start | bytes 1572868
  32.8 20.0 %copy-start.4 = (bf16[2048,1024]{1,0:T(8,128)(2,1)S(1)}, bf16[2048,1024]{1,0:T(8,128)(2,1)}, u32[]{:S(2)}) copy-start(bf16[2048,1024]{1,0:T(8,128)(2,1)} %param.15) | copy-start | bytes 12582916

commit v18 on v17

--- a/solution.py
+++ b/solution.py
@@ -143,10 +143,10 @@
 def sender_kernel(count_ref, arrivals_ref, taps_ref, out_ref, *, n_ctx, own):
     count = count_ref[0]
     capacity = arrivals_ref.shape[2]
-    lane = lax.broadcasted_iota(jnp.int32, arrivals_ref.shape[1:], 1)
     row = lax.broadcasted_iota(jnp.int32, (capacity, EDGE), 0)
     column = lax.broadcasted_iota(jnp.int32, (capacity, EDGE), 1)
-    square = lax.broadcasted_iota(jnp.int32, (lane.shape[0], lane.shape[0]), 0)
+    channels = arrivals_ref.shape[1]
+    square = lax.broadcasted_iota(jnp.int32, (channels, channels), 0)
     diagonal = square == lax.broadcasted_iota(jnp.int32, square.shape, 1)
 
     def tap(part, k):
@@ -163,7 +163,7 @@
         edge = edge + jnp.dot(arrivals_ref[1 + part], pick, preferred_element_type=jnp.float32)
         columns.append([tap(1 + part, k) for k in range(3)])
     edge = edge.astype(jnp.bfloat16)
-    block_lane = lane[:own]
+    block_lane = lax.broadcasted_iota(jnp.int32, (own, capacity), 1)
     for j in range(n_ctx):
         rows = slice(j * own, (j + 1) * own)
         near = []
@@ -184,10 +184,11 @@
     lane_out = lax.broadcasted_iota(jnp.int32, (own, capacity), 1)
     code = jnp.where(lane_out[:1] == 8 * own, (count // 16).astype(jnp.float32), 0.0)
     code = jnp.where(lane_out[:1] == 8 * own + 1, (count % 16).astype(jnp.float32), code)
+    tiled_all = jnp.dot(edge, spread, preferred_element_type=jnp.float32)
     for j in range(n_ctx):
         rows = slice(j * own, (j + 1) * own)
         out_ref[j, :own, :] = arrivals_ref[0, rows, :]
-        tiled = jnp.dot(edge[rows], spread, preferred_element_type=jnp.float32)
+        tiled = tiled_all[rows]
         flat = jnp.sum(jnp.where(lane_out // 8 == channel, tiled, 0.0), axis=0, keepdims=True)
         out_ref[j, 2 * own : 2 * own + 1, :] = (flat + code).astype(jnp.bfloat16)
 

time: 55.4 us -> 55.4 us (level)
  no operation moved by 1% of the time
where the time goes in v18:
time: 55.4 us; the launch traced here: 55 us
  blocking collectives  18 us (32%)
  waiting for transfers between devices  12.5 us (23%)
  matrix products  7.83 us (14%)
  starting transfers between devices  7.25 us (13%)
  local copies, waits for them, and re-layouts  2.89 us (5%)
  other arithmetic  2.82 us (5%)
  Pallas kernels  2.74 us (5%)
  between operations  1.07 us (2%)
    all_to_all x1, waiting for transfers between devices, by_transpose(): got = lax.all_to_all(payload, 'ctx', 0, 0, tiled=False)  12.5 us
    all_to_all x1, blocking collectives, by_transpose(): lax.all_to_all(gated.reshape(own, n_ctx, T_DEV), 'ctx', 1, 0, tiled=False)  10.8 us
    all_to_all x1, starting transfers between devices, by_transpose(): got = lax.all_to_all(payload, 'ctx', 0, 0, tiled=False)  7.25 us
    all_gather x1, blocking collectives, by_transpose(): lax.all_gather(gated_block, 'ch', axis=0, tiled=True)  7.18 us
    pallas_call x1, Pallas kernels, by_transpose(): pl.pallas_call(functools.partial(sender_kernel, n_ctx=n_ctx, own=own), in...  2.74 us
    dot_general x1, matrix products, by_transpose(): jnp.einsum('icr,irj->icj', rows, select, preferred_element_type=jnp.bfloa...  2.5 us
    dot_general x1, matrix products, by_transpose(): jnp.dot(out_weight, lax.all_gather(gated_block, 'ch', axis=0, tiled=True)...  2.25 us
    dot_general x2, matrix products, transform(): jnp.einsum(spec, blocks, hi, preferred_element_type=jnp.float32)  1.4 us
  transfers between devices with their start and end apart: 1, of which 1 were waited for; matrix products, arithmetic and copies ran while one was open for 6% of the time, Pallas kernels for 0%

profile of v18, /device:TPU:0, one launch (start us, length us, event | category | flops | bytes accessed | tf_op | source)
XLA Modules:
  0.0 55.0 jit_solution(3537710348643274916)
XLA Ops:
  0.0 0.0 copy-start
  0.0 0.0 copy-start.1
  0.8 2.7 %shard_map.100 = bf16[8,65,512]{2,1,0:T(8,128)(2,1)} custom-call(s32[1]{0:T(128)S(6)} %copy.79.count_ref, bf16[3,256,512]{2,1,0:T(8,128)(2,1)} %arrivals_ref.1, f32[3,3,256]{2,1,0:T(4,128)} %taps_ref.1), custom_call_target="tpu_custom_call" | custom-call | tf_op jit(solution)/shard_map/pallas_call | solution.py:206
  3.5 7.3 %all-to-all-start = ((bf16[8,65,512]{2,1,0:T(8,128)(2,1)}), bf16[8,65,512]{2,1,0:T(8,128)(2,1)S(1)}, u32[]{:S(2)}, u32[]{:S(2)}) async-start(bf16[8,65,512]{2,1,0:T(8,128)(2,1)} %shard_map.100), calls=%async_computation | async-start | bytes 1179648 | tf_op jit(solution)/shard_map/all_to_all | solution.py:216
  10.8 0.1 pad.175.clone
  10.9 0.1 slice.365
  10.9 0.8 %dynamic_slice.11 = f32[32]{0:T(128)S(1)} dynamic-slice(f32[256]{0:T(256)} %param.14, s32[]{:T(128)S(6)} %select_n.43), dynamic_slice_sizes={32} | dynamic-slice | bytes 260 | tf_op jit(solution)/shard_map/dynamic_slice | solution.py:297
  11.7 0.0 copy-done
  11.7 0.9 %fusion.50 = (f32[32]{0:T(128)S(1)}, f32[32]{0:T(128)S(1)}, f32[32]{0:T(128)S(1)}, f32[32]{0:T(128)S(1)}, f32[32]{0:T(128)S(1)}, /*index=5*/f32[32]{0:T(128)S(1)}, f32[32]{0:T(128)S(1)}, f32[32]{0:T(128)S(1)}, f32[32]{0:T(128)S(1)}) fusion(f32[3,3,256]{2,1,0:T(4,128)} %taps_ref.1, s32[]{:T(128)S(6)} %select_n.43, s32[]{:T(128)S(6)} %add.382, s32[]{:T(128)S(6)} %add.381), kind=kLoop, calls=%fused_computation.149 | loop fusion | bytes 2316 | tf_op jit(solution)/shard_map/mul | solution.py:238
  12.6 1.2 %fusion.30 = f32[32,9,512]{2,0,1:T(8,128)S(1)} fusion(bf16[256,512,1]{1,0,2:T(8,128)(2,1)} %constant.160, bf16[4,9,8,256]{3,2,1,0:T(8,128)(2,1)S(1)} %bitcast.169), kind=kOutput, calls=%fused_computation.62 | convolution fusion | flops 75497472 | bytes 999424 | tf_op jit(solution)/shard_map/cnt,tf->cnf/dot_general | solution.py:46
  13.8 0.0 copy-done.1
  13.8 0.2 convolution_add_fusion
  14.1 0.1 fusion.9
  14.2 12.5 %all-to-all-done = bf16[8,65,512]{2,1,0:T(8,128)(2,1)S(1)} async-done(((bf16[8,65,512]{2,1,0:T(8,128)(2,1)}), bf16[8,65,512]{2,1,0:T(8,128)(2,1)S(1)}, u32[]{:S(2)}, u32[]{:S(2)}) %all-to-all-start) | async-done | bytes 532512 | tf_op jit(solution)/shard_map/all_to_all | solution.py:216
  26.7 0.1 convert_add_fusion
  26.8 0.2 subtract_reduce_fusion
  27.0 0.1 add_compare_fusion
  27.1 0.1 pad_add_fusion.4
  27.2 0.1 pad_add_fusion.3
  27.2 0.1 iota_compare_fusion.1
  27.3 0.1 copy.77
  27.4 0.1 add_add_fusion
  27.5 0.1 fusion.52
  27.6 0.1 copy.76
  27.6 0.1 pad_add_fusion.2
  27.7 0.0 copy-start.5
  27.7 0.1 iota_add_fusion
  27.8 2.5 %fusion.1 = bf16[8,64,512]{2,1,0:T(8,128)(2,1)S(1)} fusion(s32[8,512]{1,0:T(8,128)S(1)} %iota_add_fusion, pred[8,512]{1,0:T(8,128)(4,1)S(1)} %iota_compare_fusion.1, bf16[8,65,512]{2,1,0:T(8,128)(2,1)S(1)} %all-to-all-done), kind=kOutput, calls=%fused_computation.2 | convolution fusion | flops 272629760 | bytes 1069056 | tf_op jit(solution)/shard_map/icr,irj->icj/dot_general | solution.py:230
  30.3 0.0 copy-start.2
  30.4 0.1 reshape.195
  30.5 0.1 pad_add_fusion
  30.5 0.1 slice_convert_fusion
  30.7 0.2 compare_and_fusion
  30.8 0.1 and_reduce_fusion
  30.9 0.0 copy-done.5
  30.9 0.4 convolution_bitcast_fusion
  31.3 0.4 slice_select_fusion
  31.7 0.0 copy-done.2
  31.7 0.2 fusion.33
  31.9 0.2 convolution_add_fusion.1
  32.3 0.1 slice_multiply_fusion.14
  32.4 0.1 slice_multiply_fusion.10
  32.5 0.0 copy-start.3
  32.5 0.1 slice_multiply_fusion.6
  32.6 0.2 subtract_select_fusion
  32.8 0.0 copy-start.4
  32.8 0.2 add_select_fusion
  33.0 0.1 pad_maximum_fusion
  33.1 0.4 copy-done.3
  33.5 0.9 %fusion.11 = f32[32,8,256]{2,1,0:T(8,128)S(1)} fusion(f32[512,256,1]{1,0,2:T(8,128)S(1)} %copy-done.3, f32[32,8,512]{2,0,1:T(8,128)S(1)} %pad_maximum_fusion), kind=kOutput, calls=%fused_computation.18 | convolution fusion | flops 402653184 | bytes 1310720 | tf_op jit(solution)/shard_map/cnf,ft->cnt/dot_general | solution.py:296
  34.4 0.1 copy.55
  34.5 0.2 fusion.27
  34.8 10.8 %all_to_all.20 = bf16[1,32,8,256]{3,1,0,2:T(8,128)(2,1)S(1)} all-to-all(bf16[1,32,8,256]{3,1,0,2:T(8,128)(2,1)S(1)} %copy.45), channel_id=1, replica_groups=mesh['ctx'=8,'ch'=4] {'ctx'}, dimensions={2} | all-to-all | bytes 262144 | tf_op jit(solution)/shard_map/all_to_all | solution.py:300
  45.6 7.2 %all_gather.3 = bf16[1024,256]{1,0:T(8,128)(2,1)S(1)} all-gather(bf16[256,256]{1,0:T(8,128)(2,1)S(1)} %bitcast.174), channel_id=1, replica_groups=mesh['ctx'=8,'ch'=4] {'ch'}, dimensions={0}, use_global_device_ids=true | all-gather | bytes 655360 | tf_op jit(solution)/shard_map/all_gather | solution.py:304
  52.8 0.0 copy-done.4
  52.8 2.2 %fusion.5 = bf16[2048,256]{1,0:T(8,128)(2,1)} fusion(bf16[2048,1024]{1,0:T(8,128)(2,1)S(1)} %copy-done.4, bf16[1024,256]{1,0:T(8,128)(2,1)S(1)} %all_gather.3), kind=kOutput, calls=%fused_computation.7 | convolution fusion | flops 1074266112 | bytes 5767168 | tf_op jit(solution)/shard_map/dot_general | solution.py:302
  (19 shorter events, 0.3 us)
Async XLA Ops:
  0.0 11.7 %copy-start = (bf16[256,2048]{1,0:T(8,128)(2,1)S(1)}, bf16[256,2048]{1,0:T(8,128)(2,1)}, u32[]{:S(2)}) copy-start(bf16[256,2048]{1,0:T(8,128)(2,1)} %param.13) | copy-start | bytes 3145732
  0.0 13.8 %copy-start.1 = (bf16[256,512,1]{1,0,2:T(8,128)(2,1)S(1)}, bf16[256,512,1]{1,0,2:T(8,128)(2,1)}, u32[]{:S(2)}) copy-start(bf16[256,512,1]{1,0,2:T(8,128)(2,1)} %constant.161) | copy-start | bytes 786436
  3.5 23.1 %all-to-all-start = ((bf16[8,65,512]{2,1,0:T(8,128)(2,1)}), bf16[8,65,512]{2,1,0:T(8,128)(2,1)S(1)}, u32[]{:S(2)}, u32[]{:S(2)}) async-start(bf16[8,65,512]{2,1,0:T(8,128)(2,1)} %shard_map.100), calls=%async_computation | async-start | bytes 1179648 | tf_op jit(solution)/shard_map/all_to_all | solution.py:216
  27.7 3.2 %copy-start.5 = (pred[8,2]{0,1:T(4,128)(4,1)S(1)}, pred[8,2]{0,1:T(4,128)(4,1)}, u32[]{:S(2)}) copy-start(pred[8,2]{0,1:T(4,128)(4,1)} %constant.159) | copy-start | bytes 52
  30.3 1.4 %copy-start.2 = (bf16[256,512,1]{1,0,2:T(8,128)(2,1)S(1)}, bf16[256,512,1]{1,0,2:T(8,128)(2,1)}, u32[]{:S(2)}) copy-start(bf16[256,512,1]{1,0,2:T(8,128)(2,1)} %constant.160) | copy-start | bytes 786436
  32.5 1.0 %copy-start.3 = (f32[512,256,1]{1,0,2:T(8,128)S(1)}, f32[512,256,1]{1,0,2:T(8,128)}, u32[]{:S(2)}) copy-start(f32[512,256,1]{1,0,2:T(8,128)} %constant.162) | copy-start | bytes 1572868
  32.8 20.0 %copy-start.4 = (bf16[2048,1024]{1,0:T(8,128)(2,1)S(1)}, bf16[2048,1024]{1,0:T(8,128)(2,1)}, u32[]{:S(2)}) copy-start(bf16[2048,1024]{1,0:T(8,128)(2,1)} %param.15) | copy-start | bytes 12582916

commit v19 on v17

--- a/solution.py
+++ b/solution.py
@@ -146,22 +146,20 @@
     lane = lax.broadcasted_iota(jnp.int32, arrivals_ref.shape[1:], 1)
     row = lax.broadcasted_iota(jnp.int32, (capacity, EDGE), 0)
     column = lax.broadcasted_iota(jnp.int32, (capacity, EDGE), 1)
-    square = lax.broadcasted_iota(jnp.int32, (lane.shape[0], lane.shape[0]), 0)
+    square = lax.broadcasted_iota(jnp.int32, (own, own), 0)
     diagonal = square == lax.broadcasted_iota(jnp.int32, square.shape, 1)
 
-    def tap(part, k):
-        spread = jnp.where(diagonal, taps_ref[part, k : k + 1, :], 0.0)
+    def tap(part, k, j):
+        spread = jnp.where(diagonal, taps_ref[part, k : k + 1, j * own : (j + 1) * own], 0.0)
         return jnp.sum(spread, axis=1, keepdims=True)
 
     edge = jnp.where(column[:1] == 8, (count // 16).astype(jnp.float32), 0.0)
     edge = jnp.where(column[:1] == 9, (count % 16).astype(jnp.float32), edge)
-    columns = []
     for part in range(2):
         wanted = jnp.where(column >= 4, count - 2 + column - 4 - 2 * part, column - 2 * part)
         inside = (column % 4 >= 2 * part) & (column % 4 < 2 * part + 2) & (column < 8)
         pick = ((row == wanted) & inside).astype(jnp.bfloat16)
         edge = edge + jnp.dot(arrivals_ref[1 + part], pick, preferred_element_type=jnp.float32)
-        columns.append([tap(1 + part, k) for k in range(3)])
     edge = edge.astype(jnp.bfloat16)
     block_lane = lane[:own]
     for j in range(n_ctx):
@@ -171,9 +169,9 @@
             x = arrivals_ref[1 + part, rows, :].astype(jnp.float32)
             back1 = jnp.where(block_lane >= 1, pltpu.roll(x, 1, 1), 0.0)
             back2 = jnp.where(block_lane >= 2, pltpu.roll(x, 2, 1), 0.0)
-            s = columns[part][0][rows] * x
-            s = s + columns[part][1][rows] * back1
-            s = s + columns[part][2][rows] * back2
+            s = tap(1 + part, 0, j) * x
+            s = s + tap(1 + part, 1, j) * back1
+            s = s + tap(1 + part, 2, j) * back2
             near.append(s)
         out_ref[j, own : 2 * own, :] = (near[0] * near[1]).astype(jnp.bfloat16)
     flat_lane = lax.broadcasted_iota(jnp.int32, (EDGE, capacity), 1)

time: 55.4 us -> 57.7 us (1.042)
  Pallas kernels: 2.74 us -> 5.03 us
    pallas_call x1, Pallas kernels: 2.74 us -> 5.03 us  [by_transpose(): pl.pallas_call(functools.partial(sender_kernel, n_ctx=n_ctx, own=own), in...]
where the time goes in v19:
time: 57.7 us; the launch traced here: 57.3 us
  blocking collectives  18 us (31%)
  waiting for transfers between devices  12.5 us (22%)
  matrix products  7.81 us (14%)
  starting transfers between devices  7.25 us (13%)
  Pallas kernels  5.03 us (9%)
  local copies, waits for them, and re-layouts  2.89 us (5%)
  other arithmetic  2.82 us (5%)
  between operations  1.07 us (2%)
    all_to_all x1, waiting for transfers between devices, by_transpose(): got = lax.all_to_all(payload, 'ctx', 0, 0, tiled=False)  12.5 us
    all_to_all x1, blocking collectives, by_transpose(): lax.all_to_all(gated.reshape(own, n_ctx, T_DEV), 'ctx', 1, 0, tiled=False)  10.8 us
    all_to_all x1, starting transfers between devices, by_transpose(): got = lax.all_to_all(payload, 'ctx', 0, 0, tiled=False)  7.25 us
    all_gather x1, blocking collectives, by_transpose(): lax.all_gather(gated_block, 'ch', axis=0, tiled=True)  7.18 us
    pallas_call x1, Pallas kernels, by_transpose(): pl.pallas_call(functools.partial(sender_kernel, n_ctx=n_ctx, own=own), in...  5.03 us
    dot_general x1, matrix products, by_transpose(): jnp.einsum('icr,irj->icj', rows, select, preferred_element_type=jnp.bfloa...  2.49 us
    dot_general x1, matrix products, by_transpose(): jnp.dot(out_weight, lax.all_gather(gated_block, 'ch', axis=0, tiled=True)...  2.25 us
    dot_general x2, matrix products, transform(): jnp.einsum(spec, blocks, hi, preferred_element_type=jnp.float32)  1.39 us
  transfers between devices with their start and end apart: 1, of which 1 were waited for; matrix products, arithmetic and copies ran while one was open for 6% of the time, Pallas kernels for 0%

profile of v19, /device:TPU:0, one launch (start us, length us, event | category | flops | bytes accessed | tf_op | source)
XLA Modules:
  0.0 57.3 jit_solution(7611616370774403473)
XLA Ops:
  0.0 0.0 copy-start
  0.0 0.0 copy-start.1
  0.8 5.0 %shard_map.100 = bf16[8,65,512]{2,1,0:T(8,128)(2,1)} custom-call(s32[1]{0:T(128)S(6)} %copy.79.count_ref, bf16[3,256,512]{2,1,0:T(8,128)(2,1)} %arrivals_ref.1, f32[3,3,256]{2,1,0:T(4,128)} %taps_ref.1), custom_call_target="tpu_custom_call" | custom-call | tf_op jit(solution)/shard_map/pallas_call | solution.py:203
  5.8 7.3 %all-to-all-start = ((bf16[8,65,512]{2,1,0:T(8,128)(2,1)}), bf16[8,65,512]{2,1,0:T(8,128)(2,1)S(1)}, u32[]{:S(2)}, u32[]{:S(2)}) async-start(bf16[8,65,512]{2,1,0:T(8,128)(2,1)} %shard_map.100), calls=%async_computation | async-start | bytes 1179648 | tf_op jit(solution)/shard_map/all_to_all | solution.py:213
  13.1 0.1 pad.175.clone
  13.2 0.1 slice.365
  13.2 0.8 %dynamic_slice.11 = f32[32]{0:T(128)S(1)} dynamic-slice(f32[256]{0:T(256)} %param.14, s32[]{:T(128)S(6)} %select_n.43), dynamic_slice_sizes={32} | dynamic-slice | bytes 260 | tf_op jit(solution)/shard_map/dynamic_slice | solution.py:294
  14.0 0.0 copy-done
  14.0 0.9 %fusion.50 = (f32[32]{0:T(128)S(1)}, f32[32]{0:T(128)S(1)}, f32[32]{0:T(128)S(1)}, f32[32]{0:T(128)S(1)}, f32[32]{0:T(128)S(1)}, /*index=5*/f32[32]{0:T(128)S(1)}, f32[32]{0:T(128)S(1)}, f32[32]{0:T(128)S(1)}, f32[32]{0:T(128)S(1)}) fusion(f32[3,3,256]{2,1,0:T(4,128)} %taps_ref.1, s32[]{:T(128)S(6)} %select_n.43, s32[]{:T(128)S(6)} %add.382, s32[]{:T(128)S(6)} %add.381), kind=kLoop, calls=%fused_computation.149 | loop fusion | bytes 2316 | tf_op jit(solution)/shard_map/mul | solution.py:235
  14.9 1.2 %fusion.30 = f32[32,9,512]{2,0,1:T(8,128)S(1)} fusion(bf16[256,512,1]{1,0,2:T(8,128)(2,1)} %constant.160, bf16[4,9,8,256]{3,2,1,0:T(8,128)(2,1)S(1)} %bitcast.169), kind=kOutput, calls=%fused_computation.62 | convolution fusion | flops 75497472 | bytes 999424 | tf_op jit(solution)/shard_map/cnt,tf->cnf/dot_general | solution.py:46
  16.1 0.0 copy-done.1
  16.1 0.2 convolution_add_fusion
  16.4 0.1 fusion.9
  16.5 12.5 %all-to-all-done = bf16[8,65,512]{2,1,0:T(8,128)(2,1)S(1)} async-done(((bf16[8,65,512]{2,1,0:T(8,128)(2,1)}), bf16[8,65,512]{2,1,0:T(8,128)(2,1)S(1)}, u32[]{:S(2)}, u32[]{:S(2)}) %all-to-all-start) | async-done | bytes 532512 | tf_op jit(solution)/shard_map/all_to_all | solution.py:213
  29.0 0.1 convert_add_fusion
  29.1 0.2 subtract_reduce_fusion
  29.3 0.1 add_compare_fusion
  29.4 0.1 pad_add_fusion.4
  29.5 0.1 pad_add_fusion.3
  29.5 0.1 iota_compare_fusion.1
  29.6 0.1 copy.77
  29.7 0.1 add_add_fusion
  29.8 0.1 fusion.52
  29.9 0.1 copy.76
  29.9 0.1 pad_add_fusion.2
  30.0 0.0 copy-start.5
  30.0 0.1 iota_add_fusion
  30.1 2.5 %fusion.1 = bf16[8,64,512]{2,1,0:T(8,128)(2,1)S(1)} fusion(s32[8,512]{1,0:T(8,128)S(1)} %iota_add_fusion, pred[8,512]{1,0:T(8,128)(4,1)S(1)} %iota_compare_fusion.1, bf16[8,65,512]{2,1,0:T(8,128)(2,1)S(1)} %all-to-all-done), kind=kOutput, calls=%fused_computation.2 | convolution fusion | flops 272629760 | bytes 1069056 | tf_op jit(solution)/shard_map/icr,irj->icj/dot_general | solution.py:227
  32.6 0.0 copy-start.2
  32.6 0.1 reshape.195
  32.8 0.1 pad_add_fusion
  32.8 0.1 slice_convert_fusion
  33.0 0.2 compare_and_fusion
  33.1 0.1 and_reduce_fusion
  33.2 0.0 copy-done.5
  33.2 0.4 convolution_bitcast_fusion
  33.6 0.4 slice_select_fusion
  34.0 0.0 copy-done.2
  34.0 0.2 fusion.33
  34.2 0.2 convolution_add_fusion.1
  34.6 0.1 slice_multiply_fusion.14
  34.7 0.1 slice_multiply_fusion.10
  34.8 0.0 copy-start.3
  34.8 0.1 slice_multiply_fusion.6
  34.9 0.2 subtract_select_fusion
  35.1 0.0 copy-start.4
  35.1 0.2 add_select_fusion
  35.3 0.1 pad_maximum_fusion
  35.4 0.4 copy-done.3
  35.8 0.9 %fusion.11 = f32[32,8,256]{2,1,0:T(8,128)S(1)} fusion(f32[512,256,1]{1,0,2:T(8,128)S(1)} %copy-done.3, f32[32,8,512]{2,0,1:T(8,128)S(1)} %pad_maximum_fusion), kind=kOutput, calls=%fused_computation.18 | convolution fusion | flops 402653184 | bytes 1310720 | tf_op jit(solution)/shard_map/cnf,ft->cnt/dot_general | solution.py:293
  36.7 0.1 copy.55
  36.8 0.2 fusion.27
  37.1 10.8 %all_to_all.20 = bf16[1,32,8,256]{3,1,0,2:T(8,128)(2,1)S(1)} all-to-all(bf16[1,32,8,256]{3,1,0,2:T(8,128)(2,1)S(1)} %copy.45), channel_id=1, replica_groups=mesh['ctx'=8,'ch'=4] {'ctx'}, dimensions={2} | all-to-all | bytes 262144 | tf_op jit(solution)/shard_map/all_to_all | solution.py:297
  47.9 7.2 %all_gather.3 = bf16[1024,256]{1,0:T(8,128)(2,1)S(1)} all-gather(bf16[256,256]{1,0:T(8,128)(2,1)S(1)} %bitcast.174), channel_id=1, replica_groups=mesh['ctx'=8,'ch'=4] {'ch'}, dimensions={0}, use_global_device_ids=true | all-gather | bytes 655360 | tf_op jit(solution)/shard_map/all_gather | solution.py:301
  55.1 0.0 copy-done.4
  55.1 2.2 %fusion.5 = bf16[2048,256]{1,0:T(8,128)(2,1)} fusion(bf16[2048,1024]{1,0:T(8,128)(2,1)S(1)} %copy-done.4, bf16[1024,256]{1,0:T(8,128)(2,1)S(1)} %all_gather.3), kind=kOutput, calls=%fused_computation.7 | convolution fusion | flops 1074266112 | bytes 5767168 | tf_op jit(solution)/shard_map/dot_general | solution.py:299
  (19 shorter events, 0.3 us)
Async XLA Ops:
  0.0 14.0 %copy-start = (bf16[256,2048]{1,0:T(8,128)(2,1)S(1)}, bf16[256,2048]{1,0:T(8,128)(2,1)}, u32[]{:S(2)}) copy-start(bf16[256,2048]{1,0:T(8,128)(2,1)} %param.13) | copy-start | bytes 3145732
  0.0 16.1 %copy-start.1 = (bf16[256,512,1]{1,0,2:T(8,128)(2,1)S(1)}, bf16[256,512,1]{1,0,2:T(8,128)(2,1)}, u32[]{:S(2)}) copy-start(bf16[256,512,1]{1,0,2:T(8,128)(2,1)} %constant.161) | copy-start | bytes 786436
  5.8 23.1 %all-to-all-start = ((bf16[8,65,512]{2,1,0:T(8,128)(2,1)}), bf16[8,65,512]{2,1,0:T(8,128)(2,1)S(1)}, u32[]{:S(2)}, u32[]{:S(2)}) async-start(bf16[8,65,512]{2,1,0:T(8,128)(2,1)} %shard_map.100), calls=%async_computation | async-start | bytes 1179648 | tf_op jit(solution)/shard_map/all_to_all | solution.py:213
  30.0 3.2 %copy-start.5 = (pred[8,2]{0,1:T(4,128)(4,1)S(1)}, pred[8,2]{0,1:T(4,128)(4,1)}, u32[]{:S(2)}) copy-start(pred[8,2]{0,1:T(4,128)(4,1)} %constant.159) | copy-start | bytes 52
  32.6 1.4 %copy-start.2 = (bf16[256,512,1]{1,0,2:T(8,128)(2,1)S(1)}, bf16[256,512,1]{1,0,2:T(8,128)(2,1)}, u32[]{:S(2)}) copy-start(bf16[256,512,1]{1,0,2:T(8,128)(2,1)} %constant.160) | copy-start | bytes 786436
  34.8 1.0 %copy-start.3 = (f32[512,256,1]{1,0,2:T(8,128)S(1)}, f32[512,256,1]{1,0,2:T(8,128)}, u32[]{:S(2)}) copy-start(f32[512,256,1]{1,0,2:T(8,128)} %constant.162) | copy-start | bytes 1572868
  35.1 20.0 %copy-start.4 = (bf16[2048,1024]{1,0:T(8,128)(2,1)S(1)}, bf16[2048,1024]{1,0:T(8,128)(2,1)}, u32[]{:S(2)}) copy-start(bf16[2048,1024]{1,0:T(8,128)(2,1)} %param.15) | copy-start | bytes 12582916

commit v20 on v17

--- a/solution.py
+++ b/solution.py
@@ -37,8 +37,8 @@
     inv_re[0, :] = 1.0 / PERIOD
     inv_im = -2.0 * np.sin(angle) / PERIOD
     inv_im[0, :] = np.where(np.arange(T_DEV) % 2 == 0, 1.0, -1.0) / PERIOD
-    inverse = np.concatenate([inv_re, inv_im], axis=0).astype(np.float32)
-    return split_bf16(forward), jnp.asarray(inverse)
+    inverse = np.concatenate([inv_re, inv_im], axis=0)
+    return split_bf16(forward), jnp.asarray(inverse.astype(np.float32)), split_bf16(inverse)
 
 
 def transform(blocks, forward, spec="kct,tf->kcf"):
@@ -72,7 +72,7 @@
     channels = arrivals.shape[1]
     capacity = arrivals.shape[2]
     n_blocks = filter_taps.shape[1] // T_DEV
-    forward, inverse = dft_tables()
+    forward, inverse, _ = dft_tables()
 
     every_count = lax.all_gather(counts, "ctx", axis=0, tiled=True)
     earlier = jnp.arange(n_ctx, dtype=jnp.int32) < device
@@ -200,7 +200,7 @@
     length = filter_taps.shape[1]
     n_blocks = length // T_DEV
     own = channels // n_ctx
-    forward, inverse = dft_tables()
+    forward, _, inverse = dft_tables()
 
     payload = pl.pallas_call(
         functools.partial(sender_kernel, n_ctx=n_ctx, own=own),
@@ -292,7 +292,13 @@
     spectrum = jnp.concatenate(
         [jnp.where(at_zero, rr, rr - ii), jnp.where(at_zero, ii, ri + ir)], axis=2
     )
-    conv_core = jnp.einsum("cnf,ft->cnt", spectrum, inverse, precision=lax.Precision.HIGHEST)
+    spec_hi = spectrum.astype(jnp.bfloat16)
+    spec_lo = (spectrum - spec_hi.astype(jnp.float32)).astype(jnp.bfloat16)
+    inv_hi, inv_lo = inverse
+    conv_core = sum(
+        jnp.einsum("cnf,ft->cnt", a, b, preferred_element_type=jnp.float32)
+        for a, b in ((spec_hi, inv_hi), (spec_hi, inv_lo), (spec_lo, inv_hi))
+    )
     gains = lax.dynamic_slice_in_dim(skip_gain, first, own, 0)
     conv = conv_core.reshape(own, length) + gains[:, None] * mixed_input.astype(jnp.float32)
     gated = (shorted_gate * conv).astype(jnp.bfloat16)

time: 55.4 us -> 55.3 us (level)
  no operation moved by 1% of the time
where the time goes in v20:
time: 55.3 us; the launch traced here: 54.9 us
  blocking collectives  18 us (33%)
  waiting for transfers between devices  12.5 us (23%)
  matrix products  7.79 us (14%)
  starting transfers between devices  7.24 us (13%)
  other arithmetic  2.83 us (5%)
  local copies, waits for them, and re-layouts  2.78 us (5%)
  Pallas kernels  2.74 us (5%)
  between operations  1.11 us (2%)
    all_to_all x1, waiting for transfers between devices, by_transpose(): got = lax.all_to_all(payload, 'ctx', 0, 0, tiled=False)  12.5 us
    all_to_all x1, blocking collectives, by_transpose(): lax.all_to_all(gated.reshape(own, n_ctx, T_DEV), 'ctx', 1, 0, tiled=False)  10.8 us
    all_to_all x1, starting transfers between devices, by_transpose(): got = lax.all_to_all(payload, 'ctx', 0, 0, tiled=False)  7.24 us
    all_gather x1, blocking collectives, by_transpose(): lax.all_gather(gated_block, 'ch', axis=0, tiled=True)  7.18 us
    pallas_call x1, Pallas kernels, by_transpose(): pl.pallas_call(functools.partial(sender_kernel, n_ctx=n_ctx, own=own), in...  2.74 us
    dot_general x1, matrix products, by_transpose(): jnp.einsum('icr,irj->icj', rows, select, preferred_element_type=jnp.bfloa...  2.49 us
    dot_general x1, matrix products, by_transpose(): jnp.dot(out_weight, lax.all_gather(gated_block, 'ch', axis=0, tiled=True)...  2.25 us
    dot_general x2, matrix products, transform(): jnp.einsum(spec, blocks, hi, preferred_element_type=jnp.float32)  1.39 us
  transfers between devices with their start and end apart: 1, of which 1 were waited for; matrix products, arithmetic and copies ran while one was open for 6% of the time, Pallas kernels for 0%

profile of v20, /device:TPU:0, one launch (start us, length us, event | category | flops | bytes accessed | tf_op | source)
XLA Modules:
  0.0 54.9 jit_solution(14188341374943441376)
XLA Ops:
  0.0 0.0 copy-start
  0.0 0.0 copy-start.2
  0.8 2.7 %shard_map.109 = bf16[8,65,512]{2,1,0:T(8,128)(2,1)} custom-call(s32[1]{0:T(128)S(6)} %copy.86.count_ref, bf16[3,256,512]{2,1,0:T(8,128)(2,1)} %arrivals_ref.1, f32[3,3,256]{2,1,0:T(4,128)} %taps_ref.1), custom_call_target="tpu_custom_call" | custom-call | tf_op jit(solution)/shard_map/pallas_call | solution.py:205
  3.5 7.2 %all-to-all-start = ((bf16[8,65,512]{2,1,0:T(8,128)(2,1)}), bf16[8,65,512]{2,1,0:T(8,128)(2,1)S(1)}, u32[]{:S(2)}, u32[]{:S(2)}) async-start(bf16[8,65,512]{2,1,0:T(8,128)(2,1)} %shard_map.109), calls=%async_computation | async-start | bytes 1179648 | tf_op jit(solution)/shard_map/all_to_all | solution.py:215
  10.8 0.1 pad.175.clone
  10.8 0.1 slice.365
  10.9 0.8 %dynamic_slice.11 = f32[32]{0:T(128)S(1)} dynamic-slice(f32[256]{0:T(256)} %param.15, s32[]{:T(128)S(6)} %select_n.43), dynamic_slice_sizes={32} | dynamic-slice | bytes 260 | tf_op jit(solution)/shard_map/dynamic_slice | solution.py:302
  11.7 0.0 copy-done
  11.7 0.9 %fusion.53 = (f32[32]{0:T(128)S(1)}, f32[32]{0:T(128)S(1)}, f32[32]{0:T(128)S(1)}, f32[32]{0:T(128)S(1)}, f32[32]{0:T(128)S(1)}, /*index=5*/f32[32]{0:T(128)S(1)}, f32[32]{0:T(128)S(1)}, f32[32]{0:T(128)S(1)}, f32[32]{0:T(128)S(1)}) fusion(f32[3,3,256]{2,1,0:T(4,128)} %taps_ref.1, s32[]{:T(128)S(6)} %select_n.43, s32[]{:T(128)S(6)} %add.390, s32[]{:T(128)S(6)} %add.389), kind=kLoop, calls=%fused_computation.155 | loop fusion | bytes 2316 | tf_op jit(solution)/shard_map/mul | solution.py:237
  12.6 1.2 %fusion.33 = f32[32,9,512]{2,0,1:T(8,128)S(1)} fusion(bf16[256,512,1]{1,0,2:T(8,128)(2,1)} %constant.163, bf16[4,9,8,256]{3,2,1,0:T(8,128)(2,1)S(1)} %bitcast.172), kind=kOutput, calls=%fused_computation.68 | convolution fusion | flops 75497472 | bytes 999424 | tf_op jit(solution)/shard_map/cnt,tf->cnf/dot_general | solution.py:46
  13.8 0.0 copy-done.2
  13.8 0.2 convolution_add_fusion
  14.1 0.1 fusion.9
  14.2 12.5 %all-to-all-done = bf16[8,65,512]{2,1,0:T(8,128)(2,1)S(1)} async-done(((bf16[8,65,512]{2,1,0:T(8,128)(2,1)}), bf16[8,65,512]{2,1,0:T(8,128)(2,1)S(1)}, u32[]{:S(2)}, u32[]{:S(2)}) %all-to-all-start) | async-done | bytes 532512 | tf_op jit(solution)/shard_map/all_to_all | solution.py:215
  26.7 0.1 convert_add_fusion
  26.8 0.2 subtract_reduce_fusion
  27.0 0.1 add_compare_fusion
  27.1 0.1 pad_add_fusion.4
  27.2 0.1 pad_add_fusion.3
  27.2 0.1 iota_compare_fusion.1
  27.3 0.1 copy.84
  27.4 0.1 add_add_fusion
  27.5 0.1 fusion.55
  27.6 0.1 copy.83
  27.6 0.1 pad_add_fusion.2
  27.7 0.0 copy-start.6
  27.7 0.1 iota_add_fusion
  27.8 2.5 %fusion.1 = bf16[8,64,512]{2,1,0:T(8,128)(2,1)S(1)} fusion(s32[8,512]{1,0:T(8,128)S(1)} %iota_add_fusion, pred[8,512]{1,0:T(8,128)(4,1)S(1)} %iota_compare_fusion.1, bf16[8,65,512]{2,1,0:T(8,128)(2,1)S(1)} %all-to-all-done), kind=kOutput, calls=%fused_computation.2 | convolution fusion | flops 272629760 | bytes 1069056 | tf_op jit(solution)/shard_map/icr,irj->icj/dot_general | solution.py:229
  30.3 0.0 copy-start.3
  30.3 0.1 reshape.195
  30.5 0.1 pad_add_fusion
  30.5 0.1 slice_convert_fusion
  30.6 0.2 compare_and_fusion
  30.8 0.1 and_reduce_fusion
  30.9 0.0 copy-done.6
  30.9 0.4 convolution_bitcast_fusion
  31.3 0.4 slice_select_fusion
  31.7 0.0 copy-done.3
  31.7 0.2 fusion.36
  31.9 0.2 convolution_add_fusion.1
  32.3 0.1 slice_multiply_fusion.14
  32.4 0.1 slice_multiply_fusion.10
  32.5 0.0 copy-start.1
  32.5 0.1 slice_multiply_fusion.6
  32.6 0.0 copy-start.4
  32.6 0.2 subtract_select_fusion
  32.8 0.2 add_select_fusion
  33.0 0.0 copy-start.5
  33.1 0.3 copy-done.1
  33.4 0.3 fusion.30
  33.7 0.0 copy-done.4
  33.7 0.3 convolution_add_fusion.3
  34.0 0.3 convolution_add_fusion.2
  34.3 0.1 copy.58
  34.4 0.2 fusion.26
  34.7 10.8 %all_to_all.20 = bf16[1,32,8,256]{3,1,0,2:T(8,128)(2,1)S(1)} all-to-all(bf16[1,32,8,256]{3,1,0,2:T(8,128)(2,1)S(1)} %copy.48), channel_id=1, replica_groups=mesh['ctx'=8,'ch'=4] {'ctx'}, dimensions={2} | all-to-all | bytes 262144 | tf_op jit(solution)/shard_map/all_to_all | solution.py:305
  45.5 7.2 %all_gather.3 = bf16[1024,256]{1,0:T(8,128)(2,1)S(1)} all-gather(bf16[256,256]{1,0:T(8,128)(2,1)S(1)} %bitcast.177), channel_id=1, replica_groups=mesh['ctx'=8,'ch'=4] {'ch'}, dimensions={0}, use_global_device_ids=true | all-gather | bytes 655360 | tf_op jit(solution)/shard_map/all_gather | solution.py:309
  52.7 0.0 copy-done.5
  52.7 2.3 %fusion.5 = bf16[2048,256]{1,0:T(8,128)(2,1)} fusion(bf16[2048,1024]{1,0:T(8,128)(2,1)S(1)} %copy-done.5, bf16[1024,256]{1,0:T(8,128)(2,1)S(1)} %all_gather.3), kind=kOutput, calls=%fused_computation.7 | convolution fusion | flops 1074266112 | bytes 5767168 | tf_op jit(solution)/shard_map/dot_general | solution.py:307
  (21 shorter events, 0.4 us)
Async XLA Ops:
  0.0 11.7 %copy-start = (bf16[256,2048]{1,0:T(8,128)(2,1)S(1)}, bf16[256,2048]{1,0:T(8,128)(2,1)}, u32[]{:S(2)}) copy-start(bf16[256,2048]{1,0:T(8,128)(2,1)} %param.14) | copy-start | bytes 3145732
  0.0 13.8 %copy-start.2 = (bf16[256,512,1]{1,0,2:T(8,128)(2,1)S(1)}, bf16[256,512,1]{1,0,2:T(8,128)(2,1)}, u32[]{:S(2)}) copy-start(bf16[256,512,1]{1,0,2:T(8,128)(2,1)} %constant.164) | copy-start | bytes 786436
  3.5 23.1 %all-to-all-start = ((bf16[8,65,512]{2,1,0:T(8,128)(2,1)}), bf16[8,65,512]{2,1,0:T(8,128)(2,1)S(1)}, u32[]{:S(2)}, u32[]{:S(2)}) async-start(bf16[8,65,512]{2,1,0:T(8,128)(2,1)} %shard_map.109), calls=%async_computation | async-start | bytes 1179648 | tf_op jit(solution)/shard_map/all_to_all | solution.py:215
  27.7 3.2 %copy-start.6 = (pred[8,2]{0,1:T(4,128)(4,1)S(1)}, pred[8,2]{0,1:T(4,128)(4,1)}, u32[]{:S(2)}) copy-start(pred[8,2]{0,1:T(4,128)(4,1)} %constant.162) | copy-start | bytes 52
  30.3 1.4 %copy-start.3 = (bf16[256,512,1]{1,0,2:T(8,128)(2,1)S(1)}, bf16[256,512,1]{1,0,2:T(8,128)(2,1)}, u32[]{:S(2)}) copy-start(bf16[256,512,1]{1,0,2:T(8,128)(2,1)} %constant.163) | copy-start | bytes 786436
  32.5 1.0 %copy-start.1 = (bf16[512,256,1]{1,0,2:T(8,128)(2,1)S(1)}, bf16[512,256,1]{1,0,2:T(8,128)(2,1)}, u32[]{:S(2)}) copy-start(bf16[512,256,1]{1,0,2:T(8,128)(2,1)} %constant.165) | copy-start | bytes 786436
  32.6 1.1 %copy-start.4 = (bf16[512,256,1]{1,0,2:T(8,128)(2,1)S(1)}, bf16[512,256,1]{1,0,2:T(8,128)(2,1)}, u32[]{:S(2)}) copy-start(bf16[512,256,1]{1,0,2:T(8,128)(2,1)} %constant.166) | copy-start | bytes 786436
  33.0 19.7 %copy-start.5 = (bf16[2048,1024]{1,0:T(8,128)(2,1)S(1)}, bf16[2048,1024]{1,0:T(8,128)(2,1)}, u32[]{:S(2)}) copy-start(bf16[2048,1024]{1,0:T(8,128)(2,1)} %param.16) | copy-start | bytes 12582916
